TPU v7x, 1024 devices: a whole 8x8x8 slice. The times are simulated.
1024 devices in a mesh: wave: 64 (over x, y_lo, core), lev: 16 (over z, y_hi).
Axes of the slice: x: 8, y: 8 (y_hi: 2, y_lo: 4; y = y_hi * 4 + y_lo), z: 8, core: 2. Of those that a mesh axis runs over, the one named last changes fastest.
Arguments:
- spectrum: bfloat16 [16, 4, 320, 768], P('lev', None, 'wave'), may hold values from -0.25 to 0.25
- legendre: bfloat16 [320, 640, 768], P('wave'), may hold values from -0.3125 to 0.3125
- owners: int32 [640], replicated, may hold values from 0 to 639, as said below
Outputs:
- spectral_tend: float32 [16, 4, 320, 768], P('lev', None, 'wave')
Inputs may be any that keep to these rules, and one draw needn't show every extreme that they name: `owners`: every wavenumber appears in exactly one slot, and slots 2p and 2p+1 hold two wavenumbers that add up to 639.
All inputs are finite; a program needn't handle non-finite values.
Results may differ from a plain program's by a relative error of at most 0.0059.
Values may be sent and summed in bfloat16 or wider, within the bound.
No kernel may reach another device: no remote copies, remote signals or barrier semaphores. Data moves between devices by JAX's collectives and lax.ppermute only.
A program may use at most 32 MiB of HBM per device.

v0:
```python
import math

import jax
import jax.numpy as jnp
from jax import lax
from jax.sharding import PartitionSpec as P

M = 640
NLAT = 1280
LON = 2688
NLATH = 640
NPK = 768


def with_halo(block, sides, width):
    for axis, dim in sides:
        count = lax.axis_size(axis)
        forward = [(i, i + 1) for i in range(count - 1)]
        backward = [(target, source) for source, target in forward]
        low = lax.ppermute(
            lax.slice_in_dim(block, block.shape[dim] - width, None, axis=dim), axis, forward
        )
        high = lax.ppermute(lax.slice_in_dim(block, 0, width, axis=dim), axis, backward)
        block = jnp.concatenate([low, block, high], axis=dim)
    return block


def pair_masks(leading):
    packed = jnp.arange(NPK, dtype=jnp.int32)[None, :]
    split_at = (M - leading)[:, None]
    in_first = (packed < split_at).astype(jnp.float32)
    in_second = ((packed >= split_at) & (packed < M + 1)).astype(jnp.float32)
    sign_first = (1 - 2 * (packed % 2)).astype(jnp.float32)
    sign_second = (1 - 2 * ((packed - split_at) % 2)).astype(jnp.float32)
    return (in_first, in_second, sign_first, sign_second)


def make_table(owners, lon_count):
    columns = jnp.arange(lon_count, dtype=jnp.int32)
    phases = owners[:, None] * columns[None, :] % lon_count
    angles = phases.astype(jnp.float32) * (2.0 * math.pi / lon_count)
    return jnp.concatenate([jnp.cos(angles), -jnp.sin(angles)], axis=0).astype(jnp.bfloat16)


def synthesize(coeffs, wave_table):
    row_block = coeffs.reshape(-1, wave_table.shape[0])
    grid_vals = jnp.dot(row_block, wave_table, preferred_element_type=jnp.float32)
    return grid_vals.reshape(coeffs.shape[0], coeffs.shape[1], 2, wave_table.shape[1])


def advect(padded):
    centre = padded[:, 1:-1]
    slopes = 0.5 * (padded[:, 2:] - padded[:, :-2])
    leading = centre[:, :, 0] * slopes[:, :, 1]
    second = centre[:, :, 1] * slopes[:, :, 0] + 0.5 * centre[:, :, 0] * centre[:, :, 1]
    return jnp.stack([leading, second], axis=2).astype(jnp.bfloat16)


def analyze(tendency, wave_table, lat_start):
    row_block = tendency.reshape(-1, tendency.shape[-1])
    result_rows = lax.dot_general(
        row_block, wave_table, (((1,), (1,)), ((), ())), preferred_element_type=jnp.float32
    )
    latitude = lat_start + jnp.arange(tendency.shape[0], dtype=jnp.int32)
    weight = jnp.sin((latitude.astype(jnp.float32) + 0.5) * (math.pi / NLAT)) / math.sqrt(NLAT)
    result_rows = result_rows.reshape(tendency.shape[0], -1) * weight[:, None]
    return result_rows.astype(jnp.bfloat16).reshape(
        tendency.shape[0], tendency.shape[1], 4, wave_table.shape[0] // 2
    )


def shards(spectrum, legendre, owners):
    lev_count = spectrum.shape[0]
    pair_count = spectrum.shape[2]
    slot_count = 2 * pair_count
    lat_band = NLAT // lax.axis_size("wave")
    pair_base = lax.axis_index("wave") * pair_count
    leading = lax.dynamic_slice_in_dim(owners[0::2], pair_base, pair_count)
    in_first, in_second, sign_first, sign_second = pair_masks(leading)
    mask_first = in_first.astype(jnp.bfloat16)
    mask_second = in_second.astype(jnp.bfloat16)
    signed_first = (in_first * sign_first).astype(jnp.bfloat16)
    signed_second = (in_second * sign_second).astype(jnp.bfloat16)
    spec_rows = spectrum.reshape(lev_count * 4, pair_count, NPK)
    masked = jnp.stack(
        [
            spec_rows * mask_first,
            spec_rows * mask_second,
            spec_rows * signed_first,
            spec_rows * signed_second,
        ],
        axis=2,
    )
    waves = jnp.einsum(
        "cpvk,pjk->jcpv", masked, legendre, preferred_element_type=jnp.float32
    ).astype(jnp.bfloat16)
    northern = waves[..., :2].reshape(NLATH, lev_count, 4, slot_count)
    southern = waves[..., 2:].reshape(NLATH, lev_count, 4, slot_count)[::-1]
    fourier = jnp.concatenate([northern, southern], axis=0)
    banded = lax.all_to_all(fourier, "wave", split_axis=0, concat_axis=3, tiled=True)
    wave_table = make_table(owners, LON)
    lat_start = lax.axis_index("wave") * lat_band
    grid_vals = synthesize(banded, wave_table)
    padded = with_halo(grid_vals, (("lev", 1),), 1)
    coeffs = analyze(advect(padded), wave_table, lat_start)
    owned_rows = lax.all_to_all(coeffs, "wave", split_axis=3, concat_axis=0, tiled=True)
    northern = owned_rows[:NLATH].reshape(NLATH, lev_count * 4, pair_count, 2)
    southern = owned_rows[NLATH:][::-1].reshape(NLATH, lev_count * 4, pair_count, 2)
    halves = jnp.concatenate([northern, southern], axis=3)
    partial_value = jnp.einsum(
        "jcpv,pjk->cpvk", halves, legendre, preferred_element_type=jnp.float32
    )
    tendency_sum = in_first * (
        partial_value[:, :, 0] + sign_first * partial_value[:, :, 2]
    ) + in_second * (partial_value[:, :, 1] + sign_second * partial_value[:, :, 3])
    return tendency_sum.reshape(lev_count, 4, pair_count, NPK)


def solution(mesh):
    in_specs = (P("lev", None, "wave", None), P("wave", None, None), P())
    out_specs = P("lev", None, "wave", None)
    return jax.shard_map(shards, mesh=mesh, in_specs=in_specs, out_specs=out_specs, check_vma=False)
```

profile of v0, /device:TPU:129, one launch (start us, length us, event | category | flops | bytes accessed | tf_op | source)
XLA Modules:
  0.0 165.7 jit_solution(4944135558487219909)
XLA Ops:
  0.0 0.9 slice.45
  1.0 0.7 fusion.49
  1.9 1.0 broadcast_multiply_fusion.3
  2.8 3.9 %fusion.21 = bf16[640,4,5,4]{0,3,1,2:T(4,128)(2,1)S(1)} fusion(bf16[5,640,768]{2,1,0:T(8,128)(2,1)} %param.4, bf16[4,5,1,768]{3,2,0,1:T(2,128)(2,1)S(1)} %get-tuple-element.18, bf16[4,5,1,768]{3,2,0,1:T(2,128)(2,1)S(1)} %get-tuple-element.17, bf16[4,5,1,768]{3,2,0,1:T(2,128)(2,1)S(1)} %get-tuple-element.16, bf16[4,5,1,768]{3,2,0,1:T(2,128)(2,1)S(1)} %get-tuple-element.15), kind=kOutput, calls=%fused_computation.20 | convolution fusion | flops 79185920 | bytes 5140480 | tf_op jit(solution)/shard_map/cpvk,pjk->jcpv/dot_general | solution.py:94
  6.8 0.6 rev.6
  7.5 0.9 copy.85
  8.4 1.9 %reshape.424 = bf16[64,2,400]{2,1,0:T(2,128)(2,1)} reshape(bf16[1280,1,4,10]{3,2,1,0:T(4,128)(2,1)S(1)} %copy.85) | data formatting | bytes 204800
  10.3 11.4 %all-to-all-start = ((bf16[64,2,400]{2,1,0:T(2,128)(2,1)}), bf16[64,2,400]{2,1,0:T(2,128)(2,1)S(1)}, u32[]{:S(2)}, u32[]{:S(2)}) async-start(bf16[64,2,400]{2,1,0:T(2,128)(2,1)} %reshape.424), calls=%async_computation | async-start | bytes 262144 | tf_op jit(solution)/shard_map/all_to_all | solution.py:100
  21.7 31.3 %cosine_convert_fusion = (bf16[640,2688]{1,0:T(8,128)(2,1)}, bf16[640,2688]{1,0:T(8,128)(2,1)}) fusion(s32[640]{0:T(1024)S(1)} %copy-done.3), kind=kLoop, calls=%fused_computation.7 | loop fusion | flops 20643840 | bytes 6883840 | tf_op jit(solution)/shard_map/convert.2
  53.0 1.0 reshape.425
  54.0 3.4 %copy.99 = bf16[64,20,1,4,10]{1,0,3,4,2:T(8,128)(2,1)S(1)} copy(bf16[64,20,1,4,10]{4,3,1,0,2:T(4,128)(2,1)S(1)} %bitcast.76) | data formatting | bytes 204800 | tf_op jit(solution)/shard_map/all_to_all | solution.py:100
  57.4 3.0 %copy.87 = bf16[20,1,4,64,10]{4,3,2,0,1:T(8,128)(2,1)S(1)} copy(bf16[20,1,4,64,10]{0,3,2,4,1:T(8,128)(2,1)S(1)} %bitcast.79) | data formatting | bytes 204800 | tf_op jit(solution)/shard_map/all_to_all | solution.py:100
  60.4 2.4 %reshape.418 = bf16[20,2,1280]{2,1,0:T(2,128)(2,1)S(1)} reshape(bf16[20,1,4,64,10]{4,3,2,0,1:T(8,128)(2,1)S(1)} %copy.87) | data formatting | bytes 204800 | tf_op jit(solution)/shard_map/reshape.150
  62.8 5.2 %fusion.12 = f32[20,1,2,2688]{3,0,2,1:T(8,128)} fusion(bf16[640,2688]{1,0:T(8,128)(2,1)} %get-tuple-element.20, bf16[640,2688]{1,0:T(8,128)(2,1)} %get-tuple-element.19, bf16[20,2,1280]{2,1,0:T(2,128)(2,1)S(1)} %reshape.418), kind=kOutput, calls=%fused_computation.17 | convolution fusion | flops 289013760 | bytes 7413760 | tf_op jit(solution)/shard_map/dot_general | solution.py:47
  68.0 3.4 %collective-permute-start = (f32[20,1,2,2688]{3,0,2,1:T(8,128)}, f32[20,1,2,2688]{3,0,2,1:T(8,128)}, u32[]{:S(2)}, u32[]{:S(2)}) collective-permute-start(f32[20,1,2,2688]{3,0,2,1:T(8,128)} %fusion.12), channel_id=1, source_target_pairs={{1,0},{2,1},{3,2},{4,3},{5,4},{6,5},{7,6},{8,7},{9,8},{10,9},{11,1... | collective-permute-start | bytes 1290248 | tf_op jit(solution)/shard_map/ppermute | solution.py:23
  71.4 5.8 %collective-permute-start.1 = (f32[20,1,2,2688]{3,0,2,1:T(8,128)}, f32[20,1,2,2688]{3,0,2,1:T(8,128)}, u32[]{:S(2)}, u32[]{:S(2)}) collective-permute-start(f32[20,1,2,2688]{3,0,2,1:T(8,128)} %fusion.12), channel_id=1, source_target_pairs={{0,1},{1,2},{2,3},{3,4},{4,5},{5,6},{6,7},{7,8},{8,9},{9,10},{10,1... | collective-permute-start | bytes 1290248 | tf_op jit(solution)/shard_map/ppermute | solution.py:20
  77.3 9.7 %collective-permute-done = f32[20,1,2,2688]{3,0,2,1:T(8,128)} collective-permute-done((f32[20,1,2,2688]{3,0,2,1:T(8,128)}, f32[20,1,2,2688]{3,0,2,1:T(8,128)}, u32[]{:S(2)}, u32[]{:S(2)}) %collective-permute-start) | collective-permute-done | bytes 430112 | tf_op jit(solution)/shard_map/ppermute | solution.py:23
  87.0 26.0 %collective-permute-done.1 = f32[20,1,2,2688]{3,0,2,1:T(8,128)} collective-permute-done((f32[20,1,2,2688]{3,0,2,1:T(8,128)}, f32[20,1,2,2688]{3,0,2,1:T(8,128)}, u32[]{:S(2)}, u32[]{:S(2)}) %collective-permute-start.1) | collective-permute-done | bytes 430112 | tf_op jit(solution)/shard_map/ppermute | solution.py:20
  113.0 1.2 subtract_multiply_fusion
  114.2 1.1 fusion.25
  115.4 0.9 copy.89
  116.3 1.7 %convert_element_type.117 = bf16[40,2688]{1,0:T(8,128)(2,1)} reshape(bf16[20,1,2,2688]{3,2,0,1:T(2,128)(2,1)} %copy.89) | data formatting | bytes 430080 | tf_op jit(solution)/shard_map/convert_element_type | solution.py:56
  118.0 5.0 %fusion.11 = f32[40,1280]{1,0:T(8,128)} fusion(bf16[40,2688]{1,0:T(8,128)(2,1)} %convert_element_type.117, bf16[640,2688]{1,0:T(8,128)(2,1)} %get-tuple-element.20, bf16[640,2688]{1,0:T(8,128)(2,1)S(1)} %copy-done), kind=kOutput, calls=%fused_computation.16 | convolution fusion | flops 289013760 | bytes 7301120 | tf_op jit(solution)/shard_map/dot_general | solution.py:61
  123.0 1.0 reshape.419
  124.6 1.2 reshape.426
  125.8 22.0 %all-to-all-start.1 = ((bf16[64,2,400]{2,1,0:T(2,128)(2,1)}), bf16[64,2,400]{2,1,0:T(2,128)(2,1)S(1)}, u32[]{:S(2)}, u32[]{:S(2)}) async-start(bf16[64,2,400]{2,1,0:T(2,128)(2,1)} %reshape.426), calls=%async_computation.1 | async-start | bytes 262144 | tf_op jit(solution)/shard_map/all_to_all | solution.py:106
  147.9 10.8 %all-to-all-done.1 = bf16[64,2,400]{2,1,0:T(2,128)(2,1)S(1)} async-done(((bf16[64,2,400]{2,1,0:T(2,128)(2,1)}), bf16[64,2,400]{2,1,0:T(2,128)(2,1)S(1)}, u32[]{:S(2)}, u32[]{:S(2)}) %all-to-all-start.1) | async-done | bytes 102432 | tf_op jit(solution)/shard_map/all_to_all | solution.py:106
  158.7 0.8 reshape.427
  160.3 0.6 rev.7
  161.0 0.5 reshape.420
  161.5 3.3 %fusion.15 = f32[4,5,4,768]{3,2,0,1:T(4,128)S(1)} fusion(bf16[5,640,768]{2,1,0:T(8,128)(2,1)} %param.4, bf16[640,4,5,2]{0,3,1,2:T(2,128)(2,1)S(1)} %copy.94, bf16[640,4,5,2]{0,3,2,1:T(2,128)(2,1)S(1)} %reshape.420), kind=kOutput, calls=%fused_computation.18 | convolution fusion | flops 78848000 | bytes 5263360 | tf_op jit(solution)/shard_map/jcpv,pjk->cpvk/dot_general | solution.py:110
  165.0 0.7 fusion.39
  (29 shorter events, 2.2 us)
Async XLA Ops:
  2.8 18.9 %copy-start.3 = (s32[640]{0:T(1024)S(1)}, s32[640]{0:T(1024)}, u32[]{:S(2)}) copy-start(s32[640]{0:T(1024)} %param.5) | copy-start | bytes 7684
  10.3 42.7 %all-to-all-start = ((bf16[64,2,400]{2,1,0:T(2,128)(2,1)}), bf16[64,2,400]{2,1,0:T(2,128)(2,1)S(1)}, u32[]{:S(2)}, u32[]{:S(2)}) async-start(bf16[64,2,400]{2,1,0:T(2,128)(2,1)} %reshape.424), calls=%async_computation | async-start | bytes 262144 | tf_op jit(solution)/shard_map/all_to_all | solution.py:100
  62.8 55.2 %copy-start = (bf16[640,2688]{1,0:T(8,128)(2,1)S(1)}, bf16[640,2688]{1,0:T(8,128)(2,1)}, u32[]{:S(2)}) copy-start(bf16[640,2688]{1,0:T(8,128)(2,1)} %get-tuple-element.19) | copy-start | bytes 10321924
  68.0 18.9 %collective-permute-start = (f32[20,1,2,2688]{3,0,2,1:T(8,128)}, f32[20,1,2,2688]{3,0,2,1:T(8,128)}, u32[]{:S(2)}, u32[]{:S(2)}) collective-permute-start(f32[20,1,2,2688]{3,0,2,1:T(8,128)} %fusion.12), channel_id=1, source_target_pairs={{1,0},{2,1},{3,2},{4,3},{5,4},{6,5},{7,6},{8,7},{9,8},{10,9},{11,1... | collective-permute-start | bytes 1290248 | tf_op jit(solution)/shard_map/ppermute | solution.py:23
  71.4 41.6 %collective-permute-start.1 = (f32[20,1,2,2688]{3,0,2,1:T(8,128)}, f32[20,1,2,2688]{3,0,2,1:T(8,128)}, u32[]{:S(2)}, u32[]{:S(2)}) collective-permute-start(f32[20,1,2,2688]{3,0,2,1:T(8,128)} %fusion.12), channel_id=1, source_target_pairs={{0,1},{1,2},{2,3},{3,4},{4,5},{5,6},{6,7},{7,8},{8,9},{9,10},{10,1... | collective-permute-start | bytes 1290248 | tf_op jit(solution)/shard_map/ppermute | solution.py:20
  125.8 32.9 %all-to-all-start.1 = ((bf16[64,2,400]{2,1,0:T(2,128)(2,1)}), bf16[64,2,400]{2,1,0:T(2,128)(2,1)S(1)}, u32[]{:S(2)}, u32[]{:S(2)}) async-start(bf16[64,2,400]{2,1,0:T(2,128)(2,1)} %reshape.426), calls=%async_computation.1 | async-start | bytes 262144 | tf_op jit(solution)/shard_map/all_to_all | solution.py:106
  147.9 17.1 %copy-start.1 = (f32[5,768]{1,0:T(8,128)S(1)}, f32[5,768]{1,0:T(8,128)}, u32[]{:S(2)}) copy-start(f32[5,768]{1,0:T(8,128)} %get-tuple-element.23) | copy-start | bytes 46084
  147.9 17.1 %copy-start.2 = (f32[5,768]{1,0:T(8,128)S(1)}, f32[5,768]{1,0:T(8,128)}, u32[]{:S(2)}) copy-start(f32[5,768]{1,0:T(8,128)} %get-tuple-element.26) | copy-start | bytes 46084
where the time goes:
time: 166 us
  waiting for transfers between devices  46.5 us (28%)
  starting transfers between devices  42.6 us (26%)
  other arithmetic  36.6 us (22%)
  local copies, waits for them, and re-layouts  22.4 us (13%)
  matrix products  17.4 us (10%)
    another operation x2, other arithmetic  32.4 us
    ppermute x1, waiting for transfers between devices, with_halo(): lax.ppermute(lax.slice_in_dim(block, block.shape[dim] - width, None, axis...  26 us
    all_to_all x1, starting transfers between devices, shards(): lax.all_to_all(coeffs, 'wave', split_axis=3, concat_axis=0, tiled=True)  22 us
    all_to_all x1, starting transfers between devices, shards(): lax.all_to_all(fourier, 'wave', split_axis=0, concat_axis=3, tiled=True)  11.4 us
    all_to_all x1, waiting for transfers between devices, shards(): lax.all_to_all(coeffs, 'wave', split_axis=3, concat_axis=0, tiled=True)  10.8 us
    ppermute x1, waiting for transfers between devices, with_halo(): lax.ppermute(lax.slice_in_dim(block, 0, width, axis=dim), axis, backward)  9.68 us
    all_to_all x2, local copies, waits for them, and re-layouts, shards(): lax.all_to_all(fourier, 'wave', split_axis=0, concat_axis=3, tiled=True)  6.35 us
    ppermute x1, starting transfers between devices, with_halo(): lax.ppermute(lax.slice_in_dim(block, block.shape[dim] - width, None, axis...  5.8 us
  transfers between devices with their start and end apart: 4, of which 3 were waited for; matrix products, arithmetic and copies ran while one was open for 19% of the time, Pallas kernels for 0%

commit v1 on v0

--- a/solution.py
+++ b/solution.py
@@ -36,10 +36,18 @@
 
 
 def make_table(owners, lon_count):
-    columns = jnp.arange(lon_count, dtype=jnp.int32)
-    phases = owners[:, None] * columns[None, :] % lon_count
-    angles = phases.astype(jnp.float32) * (2.0 * math.pi / lon_count)
-    return jnp.concatenate([jnp.cos(angles), -jnp.sin(angles)], axis=0).astype(jnp.bfloat16)
+    inner = 128 if lon_count % 128 == 0 else lon_count
+    outer = lon_count // inner
+    scale = 2.0 * math.pi / lon_count
+    fine = jnp.arange(inner, dtype=jnp.int32)
+    coarse = jnp.arange(outer, dtype=jnp.int32) * inner
+    fine_angle = (owners[:, None] * fine[None, :] % lon_count).astype(jnp.float32) * scale
+    coarse_angle = (owners[:, None] * coarse[None, :] % lon_count).astype(jnp.float32) * scale
+    cos_f, sin_f = jnp.cos(fine_angle)[:, None, :], jnp.sin(fine_angle)[:, None, :]
+    cos_c, sin_c = jnp.cos(coarse_angle)[:, :, None], jnp.sin(coarse_angle)[:, :, None]
+    cos_t = (cos_c * cos_f - sin_c * sin_f).reshape(owners.shape[0], lon_count)
+    sin_t = (sin_c * cos_f + cos_c * sin_f).reshape(owners.shape[0], lon_count)
+    return jnp.concatenate([cos_t, -sin_t], axis=0).astype(jnp.bfloat16)
 
 
 def synthesize(coeffs, wave_table):
@@ -100,8 +108,7 @@
     banded = lax.all_to_all(fourier, "wave", split_axis=0, concat_axis=3, tiled=True)
     wave_table = make_table(owners, LON)
     lat_start = lax.axis_index("wave") * lat_band
-    grid_vals = synthesize(banded, wave_table)
-    padded = with_halo(grid_vals, (("lev", 1),), 1)
+    padded = synthesize(with_halo(banded, (("lev", 1),), 1), wave_table)
     coeffs = analyze(advect(padded), wave_table, lat_start)
     owned_rows = lax.all_to_all(coeffs, "wave", split_axis=3, concat_axis=0, tiled=True)
     northern = owned_rows[:NLATH].reshape(NLATH, lev_count * 4, pair_count, 2)

time: 166 us -> 112 us (0.67)
  the two profiles are of different devices: /device:TPU:129 before, /device:TPU:1 now
where the time goes in v1:
time: 112 us
  starting transfers between devices  39.6 us (35%)
  local copies, waits for them, and re-layouts  36.5 us (33%)
  matrix products  16.2 us (14%)
  waiting for transfers between devices  10.8 us (10%)
  other arithmetic  8.23 us (7%)
    all_to_all x1, starting transfers between devices, shards(): lax.all_to_all(fourier, 'wave', split_axis=0, concat_axis=3, tiled=True)  18.9 us
    all_to_all x1, starting transfers between devices, shards(): lax.all_to_all(coeffs, 'wave', split_axis=3, concat_axis=0, tiled=True)  11.3 us
    all_to_all x1, waiting for transfers between devices, shards(): lax.all_to_all(coeffs, 'wave', split_axis=3, concat_axis=0, tiled=True)  10.8 us
    ppermute x1, starting transfers between devices, with_halo(): lax.ppermute(lax.slice_in_dim(block, block.shape[dim] - width, None, axis...  8.12 us
    all_to_all x4, local copies, waits for them, and re-layouts, shards(): lax.all_to_all(fourier, 'wave', split_axis=0, concat_axis=3, tiled=True)  7.26 us
    unnamed x8, local copies, waits for them, and re-layouts  7.03 us
    neg x1, local copies, waits for them, and re-layouts, make_table(): return jnp.concatenate([cos_t, -sin_t], axis=0).astype(jnp.bfloat16)  5.91 us
    dot_general x1, matrix products, analyze(): lax.dot_general(row_block, wave_table, (((1,), (1,)), ((), ())), preferre...  5.01 us
  transfers between devices with their start and end apart: 4, of which 1 were waited for; matrix products, arithmetic and copies ran while one was open for 20% of the time, Pallas kernels for 0%

profile of v1, /device:TPU:1, one launch (start us, length us, event | category | flops | bytes accessed | tf_op | source)
XLA Modules:
  0.0 111.8 jit_solution(3720329934000347045)
XLA Ops:
  0.0 0.9 slice.54
  1.2 1.0 broadcast_multiply_fusion.3
  2.2 3.9 %fusion.13 = bf16[640,4,5,4]{0,3,1,2:T(4,128)(2,1)S(1)} fusion(bf16[5,640,768]{2,1,0:T(8,128)(2,1)} %param.4, bf16[4,5,1,768]{3,2,0,1:T(2,128)(2,1)S(1)} %get-tuple-element.20, bf16[4,5,1,768]{3,2,0,1:T(2,128)(2,1)S(1)} %get-tuple-element.19, bf16[4,5,1,768]{3,2,0,1:T(2,128)(2,1)S(1)} %get-tuple-element.18, bf16[4,5,1,768]{3,2,0,1:T(2,128)(2,1)S(1)} %get-tuple-element.17), kind=kOutput, calls=%fused_computation.12 | convolution fusion | flops 79185920 | bytes 5140480 | tf_op jit(solution)/shard_map/cpvk,pjk->jcpv/dot_general | solution.py:102
  6.2 0.6 rev.6
  6.9 0.9 copy.113
  7.8 1.9 %reshape.544 = bf16[64,2,400]{2,1,0:T(2,128)(2,1)} reshape(bf16[1280,1,4,10]{3,2,1,0:T(4,128)(2,1)S(1)} %copy.113) | data formatting | bytes 204800
  9.7 18.9 %all-to-all-start = ((bf16[64,2,400]{2,1,0:T(2,128)(2,1)}), bf16[64,2,400]{2,1,0:T(2,128)(2,1)}, u32[]{:S(2)}, u32[]{:S(2)}) async-start(bf16[64,2,400]{2,1,0:T(2,128)(2,1)} %reshape.544), calls=%async_computation | async-start | bytes 262144 | tf_op jit(solution)/shard_map/all_to_all | solution.py:108
  28.6 1.4 %fusion.27 = (f32[640,128]{0,1:T(8,128)S(1)}, f32[640,128]{0,1:T(8,128)S(1)}) fusion(s32[640]{0:T(1024)S(1)} %copy-done.1), kind=kLoop, calls=%fused_computation.27 | loop fusion | flops 737280 | bytes 657920 | tf_op jit(solution)/shard_map/cos | solution.py:46
  30.4 4.1 %subtract_convert_fusion = (bf16[640,21,128]{0,2,1:T(8,128)(2,1)S(1)}, bf16[640,21,128]{0,2,1:T(8,128)(2,1)}) fusion(f32[640,128]{0,1:T(8,128)S(1)} %get-tuple-element.24, f32[640,21]{0,1:T(8,128)S(1)} %get-tuple-element.22, f32[640,128]{0,1:T(8,128)S(1)} %get-tuple-element.23, f32[640,21]{0,1:T(8,128)S(1)} %get-tuple-element.21), kind=kLoop, calls=%fused_computation.4 | loop fusion | flops 15482880 | bytes 7644160 | tf_op jit(solution)/shard_map/convert.5
  34.4 5.9 %copy.123 = bf16[640,2688]{1,0:T(8,128)(2,1)} copy(bf16[640,2688]{0,1:T(8,128)(2,1)} %bitcast.78) | data formatting | bytes 6881280 | tf_op jit(solution)/shard_map/neg | solution.py:50
  40.4 3.7 %copy.122 = bf16[640,2688]{1,0:T(8,128)(2,1)} copy(bf16[640,2688]{0,1:T(8,128)(2,1)S(1)} %bitcast.77) | data formatting | bytes 6881280 | tf_op jit(solution)/shard_map/sub | solution.py:48
  44.1 3.1 %reshape.545 = bf16[1280,1,4,10]{3,2,1,0:T(4,128)(2,1)S(1)} reshape(bf16[64,2,400]{2,1,0:T(2,128)(2,1)} %all-to-all-done) | data formatting | bytes 204800
  47.2 3.4 %copy.135 = bf16[64,20,1,4,10]{1,0,3,4,2:T(8,128)(2,1)S(1)} copy(bf16[64,20,1,4,10]{4,3,1,0,2:T(4,128)(2,1)S(1)} %bitcast.81) | data formatting | bytes 204800 | tf_op jit(solution)/shard_map/all_to_all | solution.py:108
  51.5 1.3 %collective-permute-start.1 = (bf16[20,1,4,640]{3,2,1,0:T(4,128)(2,1)S(1)}, bf16[20,1,4,640]{3,2,1,0:T(4,128)(2,1)S(1)}, u32[]{:S(2)}, u32[]{:S(2)}) collective-permute-start(bf16[20,1,4,640]{3,2,1,0:T(4,128)(2,1)S(1)} %copy.116), channel_id=1, source_target_pairs={{1,0},{2,1},{3,2},{4,3},{5,4},{6,5},{7,6},{8,7},{9,8},{10,9},{11,1... | collective-permute-start | bytes 307208 | tf_op jit(solution)/shard_map/ppermute | solution.py:23
  52.8 8.1 %collective-permute-start = (bf16[20,1,4,640]{3,2,1,0:T(4,128)(2,1)S(1)}, bf16[20,1,4,640]{3,2,1,0:T(4,128)(2,1)S(1)}, u32[]{:S(2)}, u32[]{:S(2)}) collective-permute-start(bf16[20,1,4,640]{3,2,1,0:T(4,128)(2,1)S(1)} %copy.116), channel_id=1, source_target_pairs={{0,1},{1,2},{2,3},{3,4},{4,5},{5,6},{6,7},{7,8},{8,9},{9,10},{10,1... | collective-permute-start | bytes 307208 | tf_op jit(solution)/shard_map/ppermute | solution.py:20
  61.0 3.0 %copy.117 = bf16[20,1,4,64,10]{4,3,2,0,1:T(8,128)(2,1)S(1)} copy(bf16[20,1,4,64,10]{0,3,2,4,1:T(8,128)(2,1)S(1)} %bitcast.80) | data formatting | bytes 204800 | tf_op jit(solution)/shard_map/all_to_all | solution.py:108
  64.0 2.4 %concatenate.25 = bf16[20,1,2,1280]{3,2,0,1:T(2,128)(2,1)S(1)} reshape(bf16[20,1,4,64,10]{4,3,2,0,1:T(8,128)(2,1)S(1)} %copy.117) | data formatting | bytes 204800 | tf_op jit(solution)/shard_map/concatenate | solution.py:24
  66.4 0.7 copy.120
  67.2 0.7 copy.121
  68.0 4.1 %fusion = f32[20,3,2,2688]{3,0,2,1:T(8,128)S(1)} fusion(bf16[640,2688]{1,0:T(8,128)(2,1)} %copy.123, bf16[640,2688]{1,0:T(8,128)(2,1)} %copy.122, bf16[20,1,2,1280]{3,0,2,1:T(8,128)(2,1)} %copy.121, bf16[20,1,2,1280]{3,0,2,1:T(8,128)(2,1)} %copy.120, bf16[20,1,2,1280]{3,0,2,1:T(8,128)(2,1)S(1)} %copy.119), kind=kOutput, calls=%fused_computation.1 | convolution fusion | flops 839823360 | bytes 8478720 | tf_op jit(solution)/shard_map/dot_general | solution.py:55
  72.3 0.9 copy.124
  73.1 1.7 %convert_element_type.135 = bf16[40,2688]{1,0:T(8,128)(2,1)} reshape(bf16[20,1,2,2688]{3,2,0,1:T(2,128)(2,1)} %copy.124) | data formatting | bytes 430080 | tf_op jit(solution)/shard_map/convert_element_type | solution.py:64
  74.8 5.0 %fusion.6 = f32[40,1280]{1,0:T(8,128)} fusion(bf16[40,2688]{1,0:T(8,128)(2,1)} %convert_element_type.135, bf16[640,2688]{1,0:T(8,128)(2,1)S(1)} %copy-done, bf16[640,2688]{1,0:T(8,128)(2,1)} %copy.122), kind=kOutput, calls=%fused_computation.9 | convolution fusion | flops 289013760 | bytes 7301120 | tf_op jit(solution)/shard_map/dot_general | solution.py:69
  79.8 1.0 reshape.539
  81.4 1.2 %reshape.546 = bf16[64,2,400]{2,1,0:T(2,128)(2,1)} reshape(bf16[640,1,4,20]{3,2,1,0:T(4,128)(2,1)S(1)} %bitcast.83) | data formatting | bytes 204800
  82.6 11.3 %all-to-all-start.1 = ((bf16[64,2,400]{2,1,0:T(2,128)(2,1)}), bf16[64,2,400]{2,1,0:T(2,128)(2,1)S(1)}, u32[]{:S(2)}, u32[]{:S(2)}) async-start(bf16[64,2,400]{2,1,0:T(2,128)(2,1)} %reshape.546), calls=%async_computation.1 | async-start | bytes 262144 | tf_op jit(solution)/shard_map/all_to_all | solution.py:113
  93.9 10.8 %all-to-all-done.1 = bf16[64,2,400]{2,1,0:T(2,128)(2,1)S(1)} async-done(((bf16[64,2,400]{2,1,0:T(2,128)(2,1)}), bf16[64,2,400]{2,1,0:T(2,128)(2,1)S(1)}, u32[]{:S(2)}, u32[]{:S(2)}) %all-to-all-start.1) | async-done | bytes 102432 | tf_op jit(solution)/shard_map/all_to_all | solution.py:113
  104.8 0.8 reshape.547
  106.4 0.6 rev.7
  107.1 0.5 reshape.540
  107.6 3.3 %fusion.7 = f32[4,5,4,768]{3,2,0,1:T(4,128)S(1)} fusion(bf16[5,640,768]{2,1,0:T(8,128)(2,1)} %param.4, bf16[640,4,5,2]{0,3,1,2:T(2,128)(2,1)S(1)} %copy.129, bf16[640,4,5,2]{0,3,2,1:T(2,128)(2,1)S(1)} %reshape.540), kind=kOutput, calls=%fused_computation.10 | convolution fusion | flops 78848000 | bytes 5263360 | tf_op jit(solution)/shard_map/jcpv,pjk->cpvk/dot_general | solution.py:117
  111.1 0.7 fusion.45
  (37 shorter events, 3.8 us)
Async XLA Ops:
  2.2 26.4 %copy-start.1 = (s32[640]{0:T(1024)S(1)}, s32[640]{0:T(1024)}, u32[]{:S(2)}) copy-start(s32[640]{0:T(1024)} %param.5) | copy-start | bytes 7684
  9.7 34.4 %all-to-all-start = ((bf16[64,2,400]{2,1,0:T(2,128)(2,1)}), bf16[64,2,400]{2,1,0:T(2,128)(2,1)}, u32[]{:S(2)}, u32[]{:S(2)}) async-start(bf16[64,2,400]{2,1,0:T(2,128)(2,1)} %reshape.544), calls=%async_computation | async-start | bytes 262144 | tf_op jit(solution)/shard_map/all_to_all | solution.py:108
  51.5 15.6 %collective-permute-start.1 = (bf16[20,1,4,640]{3,2,1,0:T(4,128)(2,1)S(1)}, bf16[20,1,4,640]{3,2,1,0:T(4,128)(2,1)S(1)}, u32[]{:S(2)}, u32[]{:S(2)}) collective-permute-start(bf16[20,1,4,640]{3,2,1,0:T(4,128)(2,1)S(1)} %copy.116), channel_id=1, source_target_pairs={{1,0},{2,1},{3,2},{4,3},{5,4},{6,5},{7,6},{8,7},{9,8},{10,9},{11,1... | collective-permute-start | bytes 307208 | tf_op jit(solution)/shard_map/ppermute | solution.py:23
  52.8 15.0 %collective-permute-start = (bf16[20,1,4,640]{3,2,1,0:T(4,128)(2,1)S(1)}, bf16[20,1,4,640]{3,2,1,0:T(4,128)(2,1)S(1)}, u32[]{:S(2)}, u32[]{:S(2)}) collective-permute-start(bf16[20,1,4,640]{3,2,1,0:T(4,128)(2,1)S(1)} %copy.116), channel_id=1, source_target_pairs={{0,1},{1,2},{2,3},{3,4},{4,5},{5,6},{6,7},{7,8},{8,9},{9,10},{10,1... | collective-permute-start | bytes 307208 | tf_op jit(solution)/shard_map/ppermute | solution.py:20
  68.0 6.9 %copy-start = (bf16[640,2688]{1,0:T(8,128)(2,1)S(1)}, bf16[640,2688]{1,0:T(8,128)(2,1)}, u32[]{:S(2)}) copy-start(bf16[640,2688]{1,0:T(8,128)(2,1)} %copy.123) | copy-start | bytes 10321924
  82.6 22.2 %all-to-all-start.1 = ((bf16[64,2,400]{2,1,0:T(2,128)(2,1)}), bf16[64,2,400]{2,1,0:T(2,128)(2,1)S(1)}, u32[]{:S(2)}, u32[]{:S(2)}) async-start(bf16[64,2,400]{2,1,0:T(2,128)(2,1)} %reshape.546), calls=%async_computation.1 | async-start | bytes 262144 | tf_op jit(solution)/shard_map/all_to_all | solution.py:113

commit v2 on v1

--- a/solution.py
+++ b/solution.py
@@ -3,6 +3,7 @@
 import jax
 import jax.numpy as jnp
 from jax import lax
+from jax.experimental import pallas as pl
 from jax.sharding import PartitionSpec as P
 
 M = 640
@@ -35,6 +36,18 @@
     return (in_first, in_second, sign_first, sign_second)
 
 
+def table_kernel(cos_c_ref, sin_c_ref, cos_f_ref, sin_f_ref, out_ref):
+    inner = cos_f_ref.shape[1]
+    cos_f = cos_f_ref[...]
+    sin_f = sin_f_ref[...]
+    for k in range(cos_c_ref.shape[1]):
+        cos_c = cos_c_ref[:, k : k + 1]
+        sin_c = sin_c_ref[:, k : k + 1]
+        columns = slice(k * inner, (k + 1) * inner)
+        out_ref[0, :, columns] = (cos_c * cos_f - sin_c * sin_f).astype(out_ref.dtype)
+        out_ref[1, :, columns] = (-(sin_c * cos_f + cos_c * sin_f)).astype(out_ref.dtype)
+
+
 def make_table(owners, lon_count):
     inner = 128 if lon_count % 128 == 0 else lon_count
     outer = lon_count // inner
@@ -43,11 +56,21 @@
     coarse = jnp.arange(outer, dtype=jnp.int32) * inner
     fine_angle = (owners[:, None] * fine[None, :] % lon_count).astype(jnp.float32) * scale
     coarse_angle = (owners[:, None] * coarse[None, :] % lon_count).astype(jnp.float32) * scale
-    cos_f, sin_f = jnp.cos(fine_angle)[:, None, :], jnp.sin(fine_angle)[:, None, :]
-    cos_c, sin_c = jnp.cos(coarse_angle)[:, :, None], jnp.sin(coarse_angle)[:, :, None]
-    cos_t = (cos_c * cos_f - sin_c * sin_f).reshape(owners.shape[0], lon_count)
-    sin_t = (sin_c * cos_f + cos_c * sin_f).reshape(owners.shape[0], lon_count)
-    return jnp.concatenate([cos_t, -sin_t], axis=0).astype(jnp.bfloat16)
+    rows = owners.shape[0]
+    block = 128 if rows % 128 == 0 else rows
+    table = pl.pallas_call(
+        table_kernel,
+        grid=(rows // block,),
+        in_specs=[
+            pl.BlockSpec((block, outer), lambda i: (i, 0)),
+            pl.BlockSpec((block, outer), lambda i: (i, 0)),
+            pl.BlockSpec((block, inner), lambda i: (i, 0)),
+            pl.BlockSpec((block, inner), lambda i: (i, 0)),
+        ],
+        out_specs=pl.BlockSpec((2, block, lon_count), lambda i: (0, i, 0)),
+        out_shape=jax.ShapeDtypeStruct((2, rows, lon_count), jnp.bfloat16),
+    )(jnp.cos(coarse_angle), jnp.sin(coarse_angle), jnp.cos(fine_angle), jnp.sin(fine_angle))
+    return table.reshape(2 * rows, lon_count)
 
 
 def synthesize(coeffs, wave_table):

time: 112 us -> 99.6 us (0.89)
  local copies, waits for them, and re-layouts: 36.5 us -> 20.4 us
  starting transfers between devices: 39.6 us -> 31.4 us
  Pallas kernels: 0 us -> 7.01 us
  waiting for transfers between devices: 10.8 us -> 16.3 us
  other arithmetic: 8.23 us -> 6.82 us
    pallas_call x0 -> x1, Pallas kernels: none -> 7.01 us  [make_table(): pl.pallas_call(table_kernel, grid=(rows // block,), in_specs=[pl.BlockSpe...]
    ppermute x1, starting transfers between devices: 8.12 us -> 1.3 us  [with_halo(): lax.ppermute(lax.slice_in_dim(block, block.shape[dim] - width, None, axis...]
    neg x1 -> x0, local copies, waits for them, and re-layouts: 5.91 us -> none  [make_table(): return jnp.concatenate([cos_t, -sin_t], axis=0).astype(jnp.bfloat16)]
    ppermute x1, waiting for transfers between devices: 0.01 us -> 5.51 us  [with_halo(): lax.ppermute(lax.slice_in_dim(block, 0, width, axis=dim), axis, backward)]
    sin x0 -> x2, other arithmetic: none -> 4.24 us  [the longest x1 2.32 us: make_table(): jnp.sin(fine_angle)]
    another operation x2 -> x1, other arithmetic: 4.15 us -> 0.08 us
    sub x1 -> x0, local copies, waits for them, and re-layouts: 3.74 us -> none  [make_table(): cos_t = (cos_c * cos_f - sin_c * sin_f).reshape(owners.shape[0], lon_count)]
    unnamed x8 -> x6, local copies, waits for them, and re-layouts: 7.03 us -> 4.94 us
  transfers between devices with their start and end apart: 4 -> 4, of which waited for: 1 -> 2; matrix products, arithmetic and copies ran while one was open for 20% -> 10% of each run, Pallas kernels for 0% -> 7%
where the time goes in v2:
time: 99.6 us; the launch traced here: 98.9 us
  starting transfers between devices  31.4 us (32%)
  local copies, waits for them, and re-layouts  20.4 us (20%)
  matrix products  16.6 us (17%)
  waiting for transfers between devices  16.3 us (16%)
  Pallas kernels  7.01 us (7%)
  other arithmetic  6.82 us (7%)
    all_to_all x1, starting transfers between devices, shards(): lax.all_to_all(fourier, 'wave', split_axis=0, concat_axis=3, tiled=True)  18.1 us
    all_to_all x1, waiting for transfers between devices, shards(): lax.all_to_all(coeffs, 'wave', split_axis=3, concat_axis=0, tiled=True)  10.8 us
    all_to_all x1, starting transfers between devices, shards(): lax.all_to_all(coeffs, 'wave', split_axis=3, concat_axis=0, tiled=True)  10.5 us
    all_to_all x4, local copies, waits for them, and re-layouts, shards(): lax.all_to_all(fourier, 'wave', split_axis=0, concat_axis=3, tiled=True)  7.26 us
    pallas_call x1, Pallas kernels, make_table(): pl.pallas_call(table_kernel, grid=(rows // block,), in_specs=[pl.BlockSpe...  7.01 us
    ppermute x1, waiting for transfers between devices, with_halo(): lax.ppermute(lax.slice_in_dim(block, 0, width, axis=dim), axis, backward)  5.51 us
    dot_general x1, matrix products, analyze(): lax.dot_general(row_block, wave_table, (((1,), (1,)), ((), ())), preferre...  5.16 us
    unnamed x6, local copies, waits for them, and re-layouts  4.94 us
  transfers between devices with their start and end apart: 4, of which 2 were waited for; matrix products, arithmetic and copies ran while one was open for 10% of the time, Pallas kernels for 7%

profile of v2, /device:TPU:1, one launch (start us, length us, event | category | flops | bytes accessed | tf_op | source)
XLA Modules:
  0.0 98.9 jit_solution(15695408707343427576)
XLA Ops:
  0.0 0.9 slice.54
  1.2 1.0 broadcast_multiply_fusion.3
  2.2 3.9 %fusion.10 = bf16[640,4,5,4]{0,3,1,2:T(4,128)(2,1)S(1)} fusion(bf16[5,640,768]{2,1,0:T(8,128)(2,1)} %param.4, bf16[4,5,1,768]{3,2,0,1:T(2,128)(2,1)S(1)} %get-tuple-element.20, bf16[4,5,1,768]{3,2,0,1:T(2,128)(2,1)S(1)} %get-tuple-element.19, bf16[4,5,1,768]{3,2,0,1:T(2,128)(2,1)S(1)} %get-tuple-element.18, bf16[4,5,1,768]{3,2,0,1:T(2,128)(2,1)S(1)} %get-tuple-element.17), kind=kOutput, calls=%fused_computation.6 | convolution fusion | flops 79185920 | bytes 5140480 | tf_op jit(solution)/shard_map/cpvk,pjk->jcpv/dot_general | solution.py:125
  6.2 0.6 rev.6
  6.9 0.9 copy.105
  7.8 1.9 %reshape.456 = bf16[64,2,400]{2,1,0:T(2,128)(2,1)} reshape(bf16[1280,1,4,10]{3,2,1,0:T(4,128)(2,1)S(1)} %copy.105) | data formatting | bytes 204800
  9.7 18.1 %all-to-all-start = ((bf16[64,2,400]{2,1,0:T(2,128)(2,1)}), bf16[64,2,400]{2,1,0:T(2,128)(2,1)S(1)}, u32[]{:S(2)}, u32[]{:S(2)}) async-start(bf16[64,2,400]{2,1,0:T(2,128)(2,1)} %reshape.456), calls=%async_computation | async-start | bytes 262144 | tf_op jit(solution)/shard_map/all_to_all | solution.py:131
  28.2 1.9 %multiply_sine_fusion = (f32[640,21]{1,0:T(8,128)}, f32[640,21]{1,0:T(8,128)}) fusion(f32[640,21]{1,0:T(8,128)S(1)} %copy.114), kind=kLoop, calls=%fused_computation.24 | loop fusion | flops 13440 | bytes 161280 | tf_op jit(solution)/shard_map/sin | solution.py:72
  30.1 2.3 %fusion.24 = (f32[640,128]{1,0:T(8,128)}, f32[640,128]{1,0:T(8,128)}) fusion(s32[640]{0:T(1024)S(1)} %copy-done), kind=kLoop, calls=%fused_computation.21 | loop fusion | flops 737280 | bytes 657920 | tf_op jit(solution)/shard_map/sin | solution.py:72
  32.4 7.0 %shard_map.37 = bf16[2,640,2688]{2,1,0:T(8,128)(2,1)} custom-call(f32[640,21]{1,0:T(8,128)} %get-tuple-element.10.cos_c_ref, f32[640,21]{1,0:T(8,128)} %get-tuple-element.9.sin_c_ref, f32[640,128]{1,0:T(8,128)} %get-tuple-element.22.cos_f_ref, f32[640,128]{1,0:T(8,128)} %get-tuple-element.21.sin_f_ref), custom_call_target="tpu_custom_call" | custom-call | tf_op jit(solution)/shard_map/pallas_call | solution.py:61
  39.4 1.0 %reshape.457 = bf16[1280,1,4,10]{3,2,1,0:T(4,128)(2,1)S(1)} reshape(bf16[64,2,400]{2,1,0:T(2,128)(2,1)S(1)} %all-to-all-done) | data formatting | bytes 204800
  40.5 3.4 %copy.126 = bf16[64,20,1,4,10]{1,0,3,4,2:T(8,128)(2,1)S(1)} copy(bf16[64,20,1,4,10]{4,3,1,0,2:T(4,128)(2,1)S(1)} %bitcast.81) | data formatting | bytes 204800 | tf_op jit(solution)/shard_map/all_to_all | solution.py:131
  43.8 0.5 copy.107
  44.4 0.4 copy.108
  44.8 1.3 %collective-permute-start = (bf16[20,1,4,640]{3,2,1,0:T(4,128)(2,1)S(1)}, bf16[20,1,4,640]{3,2,1,0:T(4,128)(2,1)S(1)}, u32[]{:S(2)}, u32[]{:S(2)}) collective-permute-start(bf16[20,1,4,640]{3,2,1,0:T(4,128)(2,1)S(1)} %copy.108), channel_id=1, source_target_pairs={{0,1},{1,2},{2,3},{3,4},{4,5},{5,6},{6,7},{7,8},{8,9},{9,10},{10,1... | collective-permute-start | bytes 307208 | tf_op jit(solution)/shard_map/ppermute | solution.py:21
  46.1 1.5 %collective-permute-start.1 = (bf16[20,1,4,640]{3,2,1,0:T(4,128)(2,1)S(1)}, bf16[20,1,4,640]{3,2,1,0:T(4,128)(2,1)S(1)}, u32[]{:S(2)}, u32[]{:S(2)}) collective-permute-start(bf16[20,1,4,640]{3,2,1,0:T(4,128)(2,1)S(1)} %copy.108), channel_id=1, source_target_pairs={{1,0},{2,1},{3,2},{4,3},{5,4},{6,5},{7,6},{8,7},{9,8},{10,9},{11,1... | collective-permute-start | bytes 307208 | tf_op jit(solution)/shard_map/ppermute | solution.py:24
  47.6 3.0 %copy.109 = bf16[20,1,4,64,10]{4,3,2,0,1:T(8,128)(2,1)S(1)} copy(bf16[20,1,4,64,10]{0,3,2,4,1:T(8,128)(2,1)S(1)} %bitcast.80) | data formatting | bytes 204800 | tf_op jit(solution)/shard_map/all_to_all | solution.py:131
  50.6 2.4 %concatenate.27 = bf16[20,1,2,1280]{3,2,0,1:T(2,128)(2,1)S(1)} reshape(bf16[20,1,4,64,10]{4,3,2,0,1:T(8,128)(2,1)S(1)} %copy.109) | data formatting | bytes 204800 | tf_op jit(solution)/shard_map/concatenate | solution.py:25
  53.2 5.5 %collective-permute-done.1 = bf16[20,1,4,640]{3,2,1,0:T(4,128)(2,1)S(1)} collective-permute-done((bf16[20,1,4,640]{3,2,1,0:T(4,128)(2,1)S(1)}, bf16[20,1,4,640]{3,2,1,0:T(4,128)(2,1)S(1)}, u32[]{:S(2)}, u32[]{:S(2)}) %collective-permute-start.1) | collective-permute-done | bytes 102432 | tf_op jit(solution)/shard_map/ppermute | solution.py:24
  58.8 4.2 %fusion.14 = f32[20,3,2,2688]{3,0,2,1:T(8,128)S(1)} fusion(bf16[1280,2688,1,1]{1,0,3,2:T(8,128)(2,1)} %bitcast.77, bf16[20,1,2,1280]{3,0,2,1:T(8,128)(2,1)S(1)} %copy.113, bf16[20,1,2,1280]{3,0,2,1:T(8,128)(2,1)S(1)} %copy.112, bf16[20,1,2,1280]{3,0,2,1:T(8,128)(2,1)S(1)} %copy.111), kind=kOutput, calls=%fused_computation.10 | convolution fusion | flops 826060800 | bytes 8478720 | tf_op jit(solution)/shard_map/dot_general | solution.py:78
  63.5 5.2 %fusion.73 = f32[40,1280]{1,0:T(8,128)S(1)} fusion(bf16[40,2688]{1,0:T(8,128)(2,1)S(1)} %convert_element_type.132, bf16[1280,2688]{1,0:T(8,128)(2,1)} %bitcast.78), kind=kOutput, calls=%fused_computation.101 | convolution fusion | flops 275251200 | bytes 7301120 | tf_op jit(solution)/shard_map/dot_general | solution.py:92
  68.9 0.4 copy.116
  69.3 1.2 %reshape.458 = bf16[64,2,400]{2,1,0:T(2,128)(2,1)} reshape(bf16[640,1,4,20]{3,2,1,0:T(4,128)(2,1)S(1)} %bitcast.83) | data formatting | bytes 204800
  70.5 10.5 %all-to-all-start.1 = ((bf16[64,2,400]{2,1,0:T(2,128)(2,1)}), bf16[64,2,400]{2,1,0:T(2,128)(2,1)S(1)}, u32[]{:S(2)}, u32[]{:S(2)}) async-start(bf16[64,2,400]{2,1,0:T(2,128)(2,1)} %reshape.458), calls=%async_computation.1 | async-start | bytes 262144 | tf_op jit(solution)/shard_map/all_to_all | solution.py:136
  81.1 10.8 %all-to-all-done.1 = bf16[64,2,400]{2,1,0:T(2,128)(2,1)S(1)} async-done(((bf16[64,2,400]{2,1,0:T(2,128)(2,1)}), bf16[64,2,400]{2,1,0:T(2,128)(2,1)S(1)}, u32[]{:S(2)}, u32[]{:S(2)}) %all-to-all-start.1) | async-done | bytes 102432 | tf_op jit(solution)/shard_map/all_to_all | solution.py:136
  91.9 0.8 reshape.459
  92.7 0.2 fusion.70
  93.0 0.5 slice.65
  93.5 0.6 rev.7
  94.2 0.5 reshape.452
  94.7 3.3 %fusion.4 = f32[4,5,4,768]{3,2,0,1:T(4,128)S(1)} fusion(bf16[5,640,768]{2,1,0:T(8,128)(2,1)} %param.4, bf16[640,4,5,2]{0,3,1,2:T(2,128)(2,1)S(1)} %copy.120, bf16[640,4,5,2]{0,3,2,1:T(2,128)(2,1)S(1)} %reshape.452), kind=kOutput, calls=%fused_computation.4 | convolution fusion | flops 78848000 | bytes 5263360 | tf_op jit(solution)/shard_map/jcpv,pjk->cpvk/dot_general | solution.py:140
  98.2 0.7 fusion.42
  (35 shorter events, 2.1 us)
Async XLA Ops:
  2.2 25.6 %copy-start = (s32[640]{0:T(1024)S(1)}, s32[640]{0:T(1024)}, u32[]{:S(2)}) copy-start(s32[640]{0:T(1024)} %param.5) | copy-start | bytes 7684
  9.7 29.7 %all-to-all-start = ((bf16[64,2,400]{2,1,0:T(2,128)(2,1)}), bf16[64,2,400]{2,1,0:T(2,128)(2,1)S(1)}, u32[]{:S(2)}, u32[]{:S(2)}) async-start(bf16[64,2,400]{2,1,0:T(2,128)(2,1)} %reshape.456), calls=%async_computation | async-start | bytes 262144 | tf_op jit(solution)/shard_map/all_to_all | solution.py:131
  44.8 8.3 %collective-permute-start = (bf16[20,1,4,640]{3,2,1,0:T(4,128)(2,1)S(1)}, bf16[20,1,4,640]{3,2,1,0:T(4,128)(2,1)S(1)}, u32[]{:S(2)}, u32[]{:S(2)}) collective-permute-start(bf16[20,1,4,640]{3,2,1,0:T(4,128)(2,1)S(1)} %copy.108), channel_id=1, source_target_pairs={{0,1},{1,2},{2,3},{3,4},{4,5},{5,6},{6,7},{7,8},{8,9},{9,10},{10,1... | collective-permute-start | bytes 307208 | tf_op jit(solution)/shard_map/ppermute | solution.py:21
  46.1 12.6 %collective-permute-start.1 = (bf16[20,1,4,640]{3,2,1,0:T(4,128)(2,1)S(1)}, bf16[20,1,4,640]{3,2,1,0:T(4,128)(2,1)S(1)}, u32[]{:S(2)}, u32[]{:S(2)}) collective-permute-start(bf16[20,1,4,640]{3,2,1,0:T(4,128)(2,1)S(1)} %copy.108), channel_id=1, source_target_pairs={{1,0},{2,1},{3,2},{4,3},{5,4},{6,5},{7,6},{8,7},{9,8},{10,9},{11,1... | collective-permute-start | bytes 307208 | tf_op jit(solution)/shard_map/ppermute | solution.py:24
  70.5 21.4 %all-to-all-start.1 = ((bf16[64,2,400]{2,1,0:T(2,128)(2,1)}), bf16[64,2,400]{2,1,0:T(2,128)(2,1)S(1)}, u32[]{:S(2)}, u32[]{:S(2)}) async-start(bf16[64,2,400]{2,1,0:T(2,128)(2,1)} %reshape.458), calls=%async_computation.1 | async-start | bytes 262144 | tf_op jit(solution)/shard_map/all_to_all | solution.py:136

commit v3 on v2

v3 whole, which is shorter than its diff:
```python
import math

import jax
import jax.numpy as jnp
from jax import lax
from jax.experimental import pallas as pl
from jax.sharding import PartitionSpec as P

M = 640
NLAT = 1280
LON = 2688
NLATH = 640
NPK = 768


def with_halo(block, sides, width):
    for axis, dim in sides:
        count = lax.axis_size(axis)
        forward = [(i, i + 1) for i in range(count - 1)]
        backward = [(target, source) for source, target in forward]
        low = lax.ppermute(
            lax.slice_in_dim(block, block.shape[dim] - width, None, axis=dim), axis, forward
        )
        high = lax.ppermute(lax.slice_in_dim(block, 0, width, axis=dim), axis, backward)
        block = jnp.concatenate([low, block, high], axis=dim)
    return block


def pair_masks(leading):
    packed = jnp.arange(NPK, dtype=jnp.int32)[None, :]
    split_at = (M - leading)[:, None]
    in_first = (packed < split_at).astype(jnp.float32)
    in_second = ((packed >= split_at) & (packed < M + 1)).astype(jnp.float32)
    sign_first = (1 - 2 * (packed % 2)).astype(jnp.float32)
    sign_second = (1 - 2 * ((packed - split_at) % 2)).astype(jnp.float32)
    return (in_first, in_second, sign_first, sign_second)


def table_kernel(cos_c_ref, sin_c_ref, cos_f_ref, sin_f_ref, out_ref):
    inner = cos_f_ref.shape[1]
    cos_f = cos_f_ref[...]
    sin_f = sin_f_ref[...]
    for k in range(cos_c_ref.shape[1]):
        cos_c = cos_c_ref[:, k : k + 1]
        sin_c = sin_c_ref[:, k : k + 1]
        out_ref[:, k * inner : (k + 1) * inner] = (cos_c * cos_f - sin_c * sin_f).astype(out_ref.dtype)


def make_table(row_wave, row_part, lon_count):
    inner = 128 if lon_count % 128 == 0 else lon_count
    outer = lon_count // inner
    scale = 2.0 * math.pi / lon_count
    fine = jnp.arange(inner, dtype=jnp.int32)
    coarse = jnp.arange(outer, dtype=jnp.int32) * inner
    fine_angle = (row_wave[:, None] * fine[None, :] % lon_count).astype(jnp.float32) * scale
    coarse_angle = (row_wave[:, None] * coarse[None, :] % lon_count).astype(jnp.float32) * scale
    is_cos = (row_part == 0)[:, None]
    cos_c, sin_c = jnp.cos(coarse_angle), jnp.sin(coarse_angle)
    lead_c = jnp.where(is_cos, cos_c, -sin_c)
    lead_s = jnp.where(is_cos, sin_c, cos_c)
    rows = row_wave.shape[0]
    block = 128 if rows % 128 == 0 else rows
    return pl.pallas_call(
        table_kernel,
        grid=(rows // block,),
        in_specs=[
            pl.BlockSpec((block, outer), lambda i: (i, 0)),
            pl.BlockSpec((block, outer), lambda i: (i, 0)),
            pl.BlockSpec((block, inner), lambda i: (i, 0)),
            pl.BlockSpec((block, inner), lambda i: (i, 0)),
        ],
        out_specs=pl.BlockSpec((block, lon_count), lambda i: (i, 0)),
        out_shape=jax.ShapeDtypeStruct((rows, lon_count), jnp.bfloat16),
    )(lead_c, lead_s, jnp.cos(fine_angle), jnp.sin(fine_angle))


def shards(spectrum, legendre, owners):
    lev_count = spectrum.shape[0]
    pair_count = spectrum.shape[2]
    slot_count = 2 * pair_count
    wave_count = lax.axis_size("wave")
    lat_count = NLATH // wave_count
    wave_index = lax.axis_index("wave")
    pair_base = wave_index * pair_count
    leading = lax.dynamic_slice_in_dim(owners[0::2], pair_base, pair_count)
    in_first, in_second, sign_first, sign_second = pair_masks(leading)
    mask_first = in_first.astype(jnp.bfloat16)
    mask_second = in_second.astype(jnp.bfloat16)
    signed_first = (in_first * sign_first).astype(jnp.bfloat16)
    signed_second = (in_second * sign_second).astype(jnp.bfloat16)
    spec_rows = spectrum.reshape(lev_count * 4, pair_count, NPK)
    masked = jnp.stack(
        [
            spec_rows * mask_first,
            spec_rows * mask_second,
            spec_rows * signed_first,
            spec_rows * signed_second,
        ],
        axis=2,
    ).reshape(lev_count, 2, 2, pair_count, 2, 2, NPK)
    leg_blocks = legendre.reshape(pair_count, wave_count, lat_count, NPK)
    payload = jnp.einsum(
        "lfrphqk,pwjk->wrpqlhjf", masked, leg_blocks, preferred_element_type=jnp.float32
    ).astype(jnp.bfloat16)
    local_k = 2 * slot_count
    row_count = lev_count * 2 * lat_count * 2
    payload = payload.reshape(wave_count, local_k, row_count)
    received = lax.all_to_all(payload, "wave", 0, 0, tiled=True)
    row_wave = jnp.broadcast_to(
        owners.reshape(wave_count, 1, slot_count), (wave_count, 2, slot_count)
    ).reshape(-1)
    row_part = jnp.broadcast_to(
        jnp.arange(2, dtype=jnp.int32)[None, :, None], (wave_count, 2, slot_count)
    ).reshape(-1)
    wave_table = make_table(row_wave, row_part, LON)
    k_all = wave_count * local_k
    fourier = received.reshape(k_all, lev_count, 2 * lat_count * 2)
    fourier = with_halo(fourier, (("lev", 1),), 1).reshape(k_all, -1)
    grid_vals = lax.dot_general(
        fourier, wave_table, (((0,), (0,)), ((), ())), preferred_element_type=jnp.float32
    ).reshape(lev_count + 2, 2, lat_count, 2, LON)
    centre = grid_vals[1:-1]
    slopes = 0.5 * (grid_vals[2:] - grid_vals[:-2])
    lead_t = centre[:, :, :, 0] * slopes[:, :, :, 1]
    second_t = centre[:, :, :, 1] * slopes[:, :, :, 0] + 0.5 * centre[:, :, :, 0] * centre[:, :, :, 1]
    tendency = jnp.stack([lead_t, second_t], axis=3).astype(jnp.bfloat16).reshape(row_count, LON)
    north = wave_index * lat_count + jnp.arange(lat_count, dtype=jnp.int32)
    latitude = jnp.stack([north, NLAT - 1 - north], axis=0)
    weight = jnp.sin((latitude.astype(jnp.float32) + 0.5) * (math.pi / NLAT)) / math.sqrt(NLAT)
    weight = jnp.broadcast_to(weight[None, :, :, None], (lev_count, 2, lat_count, 2)).reshape(-1)
    coeffs = lax.dot_general(
        wave_table, tendency, (((1,), (1,)), ((), ())), preferred_element_type=jnp.float32
    )
    coeffs = (coeffs * weight[None, :]).astype(jnp.bfloat16)
    owned = lax.all_to_all(coeffs.reshape(wave_count, local_k, row_count), "wave", 0, 0, tiled=True)
    owned = owned.reshape(wave_count, 2, pair_count, 2, lev_count, 2, lat_count, 2)
    partial = jnp.einsum(
        "wrpqlhjf,pwjk->lfrpqhk", owned, leg_blocks, preferred_element_type=jnp.float32
    )
    tendency_sum = in_first * (
        partial[:, :, :, :, 0, 0] + sign_first * partial[:, :, :, :, 0, 1]
    ) + in_second * (partial[:, :, :, :, 1, 0] + sign_second * partial[:, :, :, :, 1, 1])
    return tendency_sum.reshape(lev_count, 4, pair_count, NPK)


def solution(mesh):
    in_specs = (P("lev", None, "wave", None), P("wave", None, None), P())
    out_specs = P("lev", None, "wave", None)
    return jax.shard_map(shards, mesh=mesh, in_specs=in_specs, out_specs=out_specs, check_vma=False)
```

time: 99.6 us -> 122 us (1.22)
  the two profiles are of different devices: /device:TPU:1 before, /device:TPU:129 now
where the time goes in v3:
time: 122 us; the launch traced here: 121 us
  starting transfers between devices  36.1 us (30%)
  waiting for transfers between devices  24.5 us (20%)
  matrix products  20 us (16%)
  local copies, waits for them, and re-layouts  17.4 us (14%)
  Pallas kernels  11.6 us (10%)
  other arithmetic  11.1 us (9%)
    all_to_all x1, starting transfers between devices, shards(): lax.all_to_all(coeffs.reshape(wave_count, local_k, row_count), 'wave', 0,...  15.4 us
    pallas_call x1, Pallas kernels, make_table(): pl.pallas_call(table_kernel, grid=(rows // block,), in_specs=[pl.BlockSpe...  11.6 us
    ppermute x1, waiting for transfers between devices, with_halo(): lax.ppermute(lax.slice_in_dim(block, block.shape[dim] - width, None, axis...  11.5 us
    all_to_all x1, starting transfers between devices, shards(): received = lax.all_to_all(payload, 'wave', 0, 0, tiled=True)  11.4 us
    all_to_all x1, waiting for transfers between devices, shards(): lax.all_to_all(coeffs.reshape(wave_count, local_k, row_count), 'wave', 0,...  10.8 us
    reshape x1, local copies, waits for them, and re-layouts, shards(): leg_blocks = legendre.reshape(pair_count, wave_count, lat_count, NPK)  9.59 us
    ppermute x1, starting transfers between devices, with_halo(): lax.ppermute(lax.slice_in_dim(block, block.shape[dim] - width, None, axis...  5.98 us
    dot_general x1, matrix products, shards(): jnp.einsum('lfrphqk,pwjk->wrpqlhjf', masked, leg_blocks, preferred_elemen...  5.48 us
  transfers between devices with their start and end apart: 4, of which 3 were waited for; matrix products, arithmetic and copies ran while one was open for 8% of the time, Pallas kernels for 10%

profile of v3, /device:TPU:129, one launch (start us, length us, event | category | flops | bytes accessed | tf_op | source)
XLA Modules:
  0.0 120.9 jit_solution(2159766204535685195)
XLA Ops:
  0.0 0.9 slice.43
  1.2 0.8 bitcast_multiply_fusion.5
  2.2 9.6 %reshape.512 = bf16[5,64,10,768]{3,2,1,0:T(8,128)(2,1)} reshape(bf16[5,640,768]{2,1,0:T(8,128)(2,1)} %param.4) | data formatting | bytes 9830400 | tf_op jit(solution)/shard_map/reshape | solution.py:101
  11.8 5.5 %fusion.11 = bf16[64,2,5,2,1,2,10,2]{0,3,6,5,1,7,2,4:T(2,128)(2,1)S(1)} fusion(bf16[5,64,10,768,1,1,1]{3,2,1,0,6,5,4:T(8,128)(2,1)} %bitcast.52, bf16[2,2,5,2,2,768,1]{5,1,0,2,4,3,6:T(2,128)(2,1)S(1)} %bitcast.57), kind=kOutput, calls=%fused_computation.8 | convolution fusion | flops 78694400 | bytes 5140480 | tf_op jit(solution)/shard_map/lfrphqk,pwjk->wrpqlhjf/dot_general | solution.py:102
  17.3 0.2 copy.23
  17.5 0.3 copy.24
  17.7 1.1 reshape.523
  18.8 11.4 %all-to-all-start = ((bf16[64,2,400]{2,1,0:T(2,128)(2,1)}), bf16[64,2,400]{2,1,0:T(2,128)(2,1)S(1)}, u32[]{:S(2)}, u32[]{:S(2)}) async-start(bf16[64,2,400]{2,1,0:T(2,128)(2,1)} %reshape.523), calls=%async_computation | async-start | bytes 262144 | tf_op jit(solution)/shard_map/all_to_all | solution.py:108
  30.7 4.3 %fusion.26 = (f32[1280,21]{1,0:T(8,128)}, f32[1280,21]{1,0:T(8,128)}) fusion(s32[21]{0:T(128)S(1)} %iota_multiply_fusion, s32[1280]{0:T(1024)S(1)} %mul.280, pred[1280]{0:T(1024)(128)(4,1)S(1)} %eq.27), kind=kLoop, calls=%fused_computation.26 | loop fusion | flops 322560 | bytes 221524 | tf_op jit(solution)/shard_map/jit(_where)/select_n | solution.py:60
  35.0 4.0 %fusion.20 = (f32[1280,128]{1,0:T(8,128)}, f32[1280,128]{1,0:T(8,128)}) fusion(s32[1280]{0:T(1024)S(1)} %mul.280), kind=kLoop, calls=%fused_computation.18 | loop fusion | flops 1474560 | bytes 1315840 | tf_op jit(solution)/shard_map/sin | solution.py:74
  39.0 2.1 %all-to-all-done = bf16[64,2,400]{2,1,0:T(2,128)(2,1)S(1)} async-done(((bf16[64,2,400]{2,1,0:T(2,128)(2,1)}), bf16[64,2,400]{2,1,0:T(2,128)(2,1)S(1)}, u32[]{:S(2)}, u32[]{:S(2)}) %all-to-all-start) | async-done | bytes 102432 | tf_op jit(solution)/shard_map/all_to_all | solution.py:108
  41.1 0.5 reshape.524
  41.7 3.4 %collective-permute-start.1 = (bf16[1280,1,40]{2,0,1:T(8,128)(2,1)S(1)}, bf16[1280,1,40]{2,0,1:T(8,128)(2,1)S(1)}, u32[]{:S(2)}, u32[]{:S(2)}) collective-permute-start(bf16[1280,1,40]{2,0,1:T(8,128)(2,1)S(1)} %reshape.514), channel_id=1, source_target_pairs={{1,0},{2,1},{3,2},{4,3},{5,4},{6,5},{7,6},{8,7},{9,8},{10,9},{11,1... | collective-permute-start | bytes 307208 | tf_op jit(solution)/shard_map/ppermute | solution.py:24
  45.1 6.0 %collective-permute-start = (bf16[1280,1,40]{2,0,1:T(8,128)(2,1)S(1)}, bf16[1280,1,40]{2,0,1:T(8,128)(2,1)S(1)}, u32[]{:S(2)}, u32[]{:S(2)}) collective-permute-start(bf16[1280,1,40]{2,0,1:T(8,128)(2,1)S(1)} %reshape.514), channel_id=1, source_target_pairs={{0,1},{1,2},{2,3},{3,4},{4,5},{5,6},{6,7},{7,8},{8,9},{9,10},{10,1... | collective-permute-start | bytes 307208 | tf_op jit(solution)/shard_map/ppermute | solution.py:21
  51.4 11.6 %shard_map.37 = bf16[1280,2688]{1,0:T(8,128)(2,1)} custom-call(f32[1280,21]{1,0:T(8,128)} %get-tuple-element.18.cos_c_ref, f32[1280,21]{1,0:T(8,128)} %get-tuple-element.17.sin_c_ref, f32[1280,128]{1,0:T(8,128)} %get-tuple-element.20.cos_f_ref, f32[1280,128]{1,0:T(8,128)} %get-tuple-element.19.sin_f_ref), custom_call_target="tpu_custom_call" | custom-call | tf_op jit(solution)/shard_map/pallas_call | solution.py:63
  63.1 0.2 copy.27
  63.3 11.5 %collective-permute-done = bf16[1280,1,40]{2,0,1:T(8,128)(2,1)S(1)} collective-permute-done((bf16[1280,1,40]{2,0,1:T(8,128)(2,1)S(1)}, bf16[1280,1,40]{2,0,1:T(8,128)(2,1)S(1)}, u32[]{:S(2)}, u32[]{:S(2)}) %collective-permute-start) | collective-permute-done | bytes 102432 | tf_op jit(solution)/shard_map/ppermute | solution.py:21
  75.0 4.1 %fusion.62 = f32[120,2688]{1,0:T(8,128)S(1)} fusion(bf16[1280,120]{0,1:T(8,128)(2,1)S(1)} %bitcast.54, bf16[1280,2688]{1,0:T(8,128)(2,1)} %shard_map.37), kind=kOutput, calls=%fused_computation.91 | convolution fusion | flops 825753600 | bytes 8478720 | tf_op jit(solution)/shard_map/dot_general | solution.py:119
  79.2 0.2 mul.307
  79.4 0.2 slice.45
  79.7 0.6 fusion.31
  80.3 0.5 pad_maximum_fusion.1
  80.9 5.2 %fusion.4 = bf16[1280,40]{0,1:T(8,128)(2,1)S(1)} fusion(bf16[1280,2688]{1,0:T(8,128)(2,1)} %shard_map.37, bf16[40,2688]{1,0:T(8,128)(2,1)S(1)} %convert_element_type.124, f32[40]{0:T(128)S(1)} %broadcast_in_dim.54), kind=kOutput, calls=%fused_computation.5 | convolution fusion | flops 275353600 | bytes 7198880 | tf_op jit(solution)/shard_map/dot_general | solution.py:131
  86.0 0.2 copy.28
  86.4 1.1 reshape.525
  87.4 15.4 %all-to-all-start.1 = ((bf16[64,2,400]{2,1,0:T(2,128)(2,1)}), bf16[64,2,400]{2,1,0:T(2,128)(2,1)S(1)}, u32[]{:S(2)}, u32[]{:S(2)}) async-start(bf16[64,2,400]{2,1,0:T(2,128)(2,1)} %reshape.525), calls=%async_computation.1 | async-start | bytes 262144 | tf_op jit(solution)/shard_map/all_to_all | solution.py:135
  102.9 10.8 %all-to-all-done.1 = bf16[64,2,400]{2,1,0:T(2,128)(2,1)S(1)} async-done(((bf16[64,2,400]{2,1,0:T(2,128)(2,1)}), bf16[64,2,400]{2,1,0:T(2,128)(2,1)S(1)}, u32[]{:S(2)}, u32[]{:S(2)}) %all-to-all-start.1) | async-done | bytes 102432 | tf_op jit(solution)/shard_map/all_to_all | solution.py:135
  113.7 0.5 reshape.526
  114.2 0.3 copy.29
  114.5 5.3 %fusion.8 = f32[1,2,2,5,2,2,768]{6,1,5,4,2,3,0:T(2,128)S(1)} fusion(bf16[5,64,10,768,1,1,1]{3,2,1,0,6,5,4:T(8,128)(2,1)} %bitcast.53, bf16[64,2,5,2,2,10,2]{0,6,5,4,3,2,1:T(2,128)(2,1)S(1)} %bitcast.56), kind=kOutput, calls=%fused_computation.7 | convolution fusion | flops 78643200 | bytes 5263360 | tf_op jit(solution)/shard_map/wrpqlhjf,pwjk->lfrpqhk/dot_general | solution.py:137
  120.1 0.2 fusion.36
  120.3 0.6 copy.36
  (34 shorter events, 2.3 us)
Async XLA Ops:
  11.8 18.4 %copy-start = (s32[640]{0:T(1024)S(1)}, s32[640]{0:T(1024)}, u32[]{:S(2)}) copy-start(s32[640]{0:T(1024)} %param.5) | copy-start | bytes 7684
  18.8 22.3 %all-to-all-start = ((bf16[64,2,400]{2,1,0:T(2,128)(2,1)}), bf16[64,2,400]{2,1,0:T(2,128)(2,1)S(1)}, u32[]{:S(2)}, u32[]{:S(2)}) async-start(bf16[64,2,400]{2,1,0:T(2,128)(2,1)} %reshape.523), calls=%async_computation | async-start | bytes 262144 | tf_op jit(solution)/shard_map/all_to_all | solution.py:108
  41.7 21.4 %collective-permute-start.1 = (bf16[1280,1,40]{2,0,1:T(8,128)(2,1)S(1)}, bf16[1280,1,40]{2,0,1:T(8,128)(2,1)S(1)}, u32[]{:S(2)}, u32[]{:S(2)}) collective-permute-start(bf16[1280,1,40]{2,0,1:T(8,128)(2,1)S(1)} %reshape.514), channel_id=1, source_target_pairs={{1,0},{2,1},{3,2},{4,3},{5,4},{6,5},{7,6},{8,7},{9,8},{10,9},{11,1... | collective-permute-start | bytes 307208 | tf_op jit(solution)/shard_map/ppermute | solution.py:24
  45.1 29.7 %collective-permute-start = (bf16[1280,1,40]{2,0,1:T(8,128)(2,1)S(1)}, bf16[1280,1,40]{2,0,1:T(8,128)(2,1)S(1)}, u32[]{:S(2)}, u32[]{:S(2)}) collective-permute-start(bf16[1280,1,40]{2,0,1:T(8,128)(2,1)S(1)} %reshape.514), channel_id=1, source_target_pairs={{0,1},{1,2},{2,3},{3,4},{4,5},{5,6},{6,7},{7,8},{8,9},{9,10},{10,1... | collective-permute-start | bytes 307208 | tf_op jit(solution)/shard_map/ppermute | solution.py:21
  87.4 26.3 %all-to-all-start.1 = ((bf16[64,2,400]{2,1,0:T(2,128)(2,1)}), bf16[64,2,400]{2,1,0:T(2,128)(2,1)S(1)}, u32[]{:S(2)}, u32[]{:S(2)}) async-start(bf16[64,2,400]{2,1,0:T(2,128)(2,1)} %reshape.525), calls=%async_computation.1 | async-start | bytes 262144 | tf_op jit(solution)/shard_map/all_to_all | solution.py:135

commit v4 on v3

--- a/solution.py
+++ b/solution.py
@@ -43,24 +43,22 @@
     for k in range(cos_c_ref.shape[1]):
         cos_c = cos_c_ref[:, k : k + 1]
         sin_c = sin_c_ref[:, k : k + 1]
-        out_ref[:, k * inner : (k + 1) * inner] = (cos_c * cos_f - sin_c * sin_f).astype(out_ref.dtype)
+        columns = slice(k * inner, (k + 1) * inner)
+        out_ref[0, :, columns] = (cos_c * cos_f - sin_c * sin_f).astype(out_ref.dtype)
+        out_ref[1, :, columns] = (-(sin_c * cos_f + cos_c * sin_f)).astype(out_ref.dtype)
 
 
-def make_table(row_wave, row_part, lon_count):
+def make_table(owners, lon_count):
     inner = 128 if lon_count % 128 == 0 else lon_count
     outer = lon_count // inner
     scale = 2.0 * math.pi / lon_count
     fine = jnp.arange(inner, dtype=jnp.int32)
     coarse = jnp.arange(outer, dtype=jnp.int32) * inner
-    fine_angle = (row_wave[:, None] * fine[None, :] % lon_count).astype(jnp.float32) * scale
-    coarse_angle = (row_wave[:, None] * coarse[None, :] % lon_count).astype(jnp.float32) * scale
-    is_cos = (row_part == 0)[:, None]
-    cos_c, sin_c = jnp.cos(coarse_angle), jnp.sin(coarse_angle)
-    lead_c = jnp.where(is_cos, cos_c, -sin_c)
-    lead_s = jnp.where(is_cos, sin_c, cos_c)
-    rows = row_wave.shape[0]
+    fine_angle = (owners[:, None] * fine[None, :] % lon_count).astype(jnp.float32) * scale
+    coarse_angle = (owners[:, None] * coarse[None, :] % lon_count).astype(jnp.float32) * scale
+    rows = owners.shape[0]
     block = 128 if rows % 128 == 0 else rows
-    return pl.pallas_call(
+    table = pl.pallas_call(
         table_kernel,
         grid=(rows // block,),
         in_specs=[
@@ -69,9 +67,10 @@
             pl.BlockSpec((block, inner), lambda i: (i, 0)),
             pl.BlockSpec((block, inner), lambda i: (i, 0)),
         ],
-        out_specs=pl.BlockSpec((block, lon_count), lambda i: (i, 0)),
-        out_shape=jax.ShapeDtypeStruct((rows, lon_count), jnp.bfloat16),
-    )(lead_c, lead_s, jnp.cos(fine_angle), jnp.sin(fine_angle))
+        out_specs=pl.BlockSpec((2, block, lon_count), lambda i: (0, i, 0)),
+        out_shape=jax.ShapeDtypeStruct((2, rows, lon_count), jnp.bfloat16),
+    )(jnp.cos(coarse_angle), jnp.sin(coarse_angle), jnp.cos(fine_angle), jnp.sin(fine_angle))
+    return table.reshape(2 * rows, lon_count)
 
 
 def shards(spectrum, legendre, owners):
@@ -98,23 +97,20 @@
         ],
         axis=2,
     ).reshape(lev_count, 2, 2, pair_count, 2, 2, NPK)
-    leg_blocks = legendre.reshape(pair_count, wave_count, lat_count, NPK)
-    payload = jnp.einsum(
-        "lfrphqk,pwjk->wrpqlhjf", masked, leg_blocks, preferred_element_type=jnp.float32
+    waves = jnp.einsum(
+        "lfrphqk,pjk->jrpqlhf", masked, legendre, preferred_element_type=jnp.float32
     ).astype(jnp.bfloat16)
+    waves = waves.reshape(wave_count, lat_count, 2, pair_count, 2, lev_count, 2, 2)
+    payload = jnp.transpose(waves, (0, 2, 3, 4, 5, 6, 1, 7))
     local_k = 2 * slot_count
     row_count = lev_count * 2 * lat_count * 2
     payload = payload.reshape(wave_count, local_k, row_count)
     received = lax.all_to_all(payload, "wave", 0, 0, tiled=True)
-    row_wave = jnp.broadcast_to(
-        owners.reshape(wave_count, 1, slot_count), (wave_count, 2, slot_count)
-    ).reshape(-1)
-    row_part = jnp.broadcast_to(
-        jnp.arange(2, dtype=jnp.int32)[None, :, None], (wave_count, 2, slot_count)
-    ).reshape(-1)
-    wave_table = make_table(row_wave, row_part, LON)
+    wave_table = make_table(owners, LON)
+    received, wave_table = lax.optimization_barrier((received, wave_table))
     k_all = wave_count * local_k
-    fourier = received.reshape(k_all, lev_count, 2 * lat_count * 2)
+    fourier = jnp.transpose(received.reshape(wave_count, 2, slot_count, row_count), (1, 0, 2, 3))
+    fourier = fourier.reshape(k_all, lev_count, 2 * lat_count * 2)
     fourier = with_halo(fourier, (("lev", 1),), 1).reshape(k_all, -1)
     grid_vals = lax.dot_general(
         fourier, wave_table, (((0,), (0,)), ((), ())), preferred_element_type=jnp.float32
@@ -132,10 +128,14 @@
         wave_table, tendency, (((1,), (1,)), ((), ())), preferred_element_type=jnp.float32
     )
     coeffs = (coeffs * weight[None, :]).astype(jnp.bfloat16)
+    coeffs = jnp.transpose(coeffs.reshape(2, wave_count, slot_count, row_count), (1, 0, 2, 3))
     owned = lax.all_to_all(coeffs.reshape(wave_count, local_k, row_count), "wave", 0, 0, tiled=True)
     owned = owned.reshape(wave_count, 2, pair_count, 2, lev_count, 2, lat_count, 2)
+    owned = jnp.transpose(owned, (2, 4, 7, 1, 3, 5, 0, 6)).reshape(
+        pair_count, lev_count, 2, 2, 2, 2, NLATH
+    )
     partial = jnp.einsum(
-        "wrpqlhjf,pwjk->lfrpqhk", owned, leg_blocks, preferred_element_type=jnp.float32
+        "plfrqhj,pjk->lfrpqhk", owned, legendre, preferred_element_type=jnp.float32
     )
     tendency_sum = in_first * (
         partial[:, :, :, :, 0, 0] + sign_first * partial[:, :, :, :, 0, 1]

time: 122 us -> 120 us (0.984)
  the two profiles are of different devices: /device:TPU:129 before, /device:TPU:1 now
where the time goes in v4:
time: 120 us; the launch traced here: 119 us
  starting transfers between devices  38.5 us (32%)
  waiting for transfers between devices  32.9 us (27%)
  matrix products  16.4 us (14%)
  local copies, waits for them, and re-layouts  16 us (13%)
  other arithmetic  7.61 us (6%)
  Pallas kernels  7 us (6%)
    all_to_all x1, starting transfers between devices, shards(): received = lax.all_to_all(payload, 'wave', 0, 0, tiled=True)  18.1 us
    all_to_all x1, starting transfers between devices, shards(): lax.all_to_all(coeffs.reshape(wave_count, local_k, row_count), 'wave', 0,...  17.6 us
    ppermute x1, waiting for transfers between devices, with_halo(): lax.ppermute(lax.slice_in_dim(block, 0, width, axis=dim), axis, backward)  17.2 us
    all_to_all x1, waiting for transfers between devices, shards(): lax.all_to_all(coeffs.reshape(wave_count, local_k, row_count), 'wave', 0,...  10.8 us
    pallas_call x1, Pallas kernels, make_table(): pl.pallas_call(table_kernel, grid=(rows // block,), in_specs=[pl.BlockSpe...  7 us
    dot_general x1, matrix products, shards(): lax.dot_general(wave_table, tendency, (((1,), (1,)), ((), ())), preferred...  5.17 us
    ppermute x1, waiting for transfers between devices, with_halo(): lax.ppermute(lax.slice_in_dim(block, block.shape[dim] - width, None, axis...  4.87 us
    dot_general x1, matrix products, shards(): lax.dot_general(fourier, wave_table, (((0,), (0,)), ((), ())), preferred_...  4.07 us
  transfers between devices with their start and end apart: 4, of which 3 were waited for; matrix products, arithmetic and copies ran while one was open for 4% of the time, Pallas kernels for 6%

profile of v4, /device:TPU:1, one launch (start us, length us, event | category | flops | bytes accessed | tf_op | source)
XLA Modules:
  0.0 118.7 jit_solution(17725619962069518303)
XLA Ops:
  0.0 0.9 slice.43
  1.2 0.8 bitcast_multiply_fusion.3
  2.3 3.9 %fusion.11 = bf16[640,2,5,2,1,2,2]{0,3,5,1,6,2,4:T(2,128)(2,1)S(1)} fusion(bf16[5,640,768]{2,1,0:T(8,128)(2,1)} %param.4, bf16[2,2,5,2,2,768]{5,1,0,2,4,3:T(2,128)(2,1)S(1)} %reshape.525), kind=kOutput, calls=%fused_computation.8 | convolution fusion | flops 78694400 | bytes 5140480 | tf_op jit(solution)/shard_map/lfrphqk,pjk->jrpqlhf/dot_general | solution.py:100
  6.2 3.1 %reshape.514 = bf16[64,10,2,5,2,1,2,2]{1,0,7,6,4,3,2,5:T(8,128)(2,1)S(1)} reshape(bf16[640,2,5,2,1,2,2]{0,6,5,3,2,1,4:T(2,128)(2,1)S(1)} %copy.28) | data formatting | bytes 204800 | tf_op jit(solution)/shard_map/reshape | solution.py:103
  9.3 0.7 copy.29
  10.3 1.1 reshape.530
  11.4 18.1 %all-to-all-start = ((bf16[64,2,400]{2,1,0:T(2,128)(2,1)}), bf16[64,2,400]{2,1,0:T(2,128)(2,1)S(1)}, u32[]{:S(2)}, u32[]{:S(2)}) async-start(bf16[64,2,400]{2,1,0:T(2,128)(2,1)} %reshape.530), calls=%async_computation | async-start | bytes 262144 | tf_op jit(solution)/shard_map/all_to_all | solution.py:108
  29.9 1.9 %multiply_sine_fusion = (f32[640,21]{1,0:T(8,128)}, f32[640,21]{1,0:T(8,128)}) fusion(f32[640,21]{1,0:T(8,128)S(1)} %copy.31), kind=kLoop, calls=%fused_computation.20 | loop fusion | flops 13440 | bytes 161280 | tf_op jit(solution)/shard_map/sin | solution.py:72
  31.8 2.3 %fusion.19 = (f32[640,128]{1,0:T(8,128)}, f32[640,128]{1,0:T(8,128)}) fusion(s32[640]{0:T(1024)S(1)} %copy-done), kind=kLoop, calls=%fused_computation.17 | loop fusion | flops 737280 | bytes 657920 | tf_op jit(solution)/shard_map/sin | solution.py:72
  34.1 7.0 %shard_map.37 = bf16[2,640,2688]{2,1,0:T(8,128)(2,1)} custom-call(f32[640,21]{1,0:T(8,128)} %get-tuple-element.18.cos_c_ref, f32[640,21]{1,0:T(8,128)} %get-tuple-element.17.sin_c_ref, f32[640,128]{1,0:T(8,128)} %get-tuple-element.24.cos_f_ref, f32[640,128]{1,0:T(8,128)} %get-tuple-element.23.sin_f_ref), custom_call_target="tpu_custom_call" | custom-call | tf_op jit(solution)/shard_map/pallas_call | solution.py:61
  41.1 0.5 reshape.531
  41.6 0.3 copy.32
  41.9 0.4 copy.33
  42.5 1.3 %collective-permute-start = (bf16[1280,1,40]{2,0,1:T(8,128)(2,1)S(1)}, bf16[1280,1,40]{2,0,1:T(8,128)(2,1)S(1)}, u32[]{:S(2)}, u32[]{:S(2)}) collective-permute-start(bf16[1280,1,40]{2,0,1:T(8,128)(2,1)S(1)} %reshape.518), channel_id=1, source_target_pairs={{0,1},{1,2},{2,3},{3,4},{4,5},{5,6},{6,7},{7,8},{8,9},{9,10},{10,1... | collective-permute-start | bytes 307208 | tf_op jit(solution)/shard_map/ppermute | solution.py:21
  43.8 1.5 %collective-permute-start.1 = (bf16[1280,1,40]{2,0,1:T(8,128)(2,1)S(1)}, bf16[1280,1,40]{2,0,1:T(8,128)(2,1)S(1)}, u32[]{:S(2)}, u32[]{:S(2)}) collective-permute-start(bf16[1280,1,40]{2,0,1:T(8,128)(2,1)S(1)} %reshape.518), channel_id=1, source_target_pairs={{1,0},{2,1},{3,2},{4,3},{5,4},{6,5},{7,6},{8,7},{9,8},{10,9},{11,1... | collective-permute-start | bytes 307208 | tf_op jit(solution)/shard_map/ppermute | solution.py:24
  45.7 4.9 %collective-permute-done = bf16[1280,1,40]{2,0,1:T(8,128)(2,1)S(1)} collective-permute-done((bf16[1280,1,40]{2,0,1:T(8,128)(2,1)S(1)}, bf16[1280,1,40]{2,0,1:T(8,128)(2,1)S(1)}, u32[]{:S(2)}, u32[]{:S(2)}) %collective-permute-start) | collective-permute-done | bytes 102432 | tf_op jit(solution)/shard_map/ppermute | solution.py:21
  50.7 17.2 %collective-permute-done.1 = bf16[1280,1,40]{2,0,1:T(8,128)(2,1)S(1)} collective-permute-done((bf16[1280,1,40]{2,0,1:T(8,128)(2,1)S(1)}, bf16[1280,1,40]{2,0,1:T(8,128)(2,1)S(1)}, u32[]{:S(2)}, u32[]{:S(2)}) %collective-permute-start.1) | collective-permute-done | bytes 102432 | tf_op jit(solution)/shard_map/ppermute | solution.py:24
  68.2 4.1 %fusion.51 = f32[120,2688]{1,0:T(8,128)S(1)} fusion(bf16[1280,120]{0,1:T(8,128)(2,1)S(1)} %bitcast.66, bf16[1280,2688]{1,0:T(8,128)(2,1)} %bitcast.63), kind=kOutput, calls=%fused_computation.83 | convolution fusion | flops 825753600 | bytes 8478720 | tf_op jit(solution)/shard_map/dot_general | solution.py:115
  72.8 0.6 fusion.23
  73.4 0.5 pad_maximum_fusion.1
  74.0 5.2 %fusion.4 = bf16[1280,40]{0,1:T(8,128)(2,1)S(1)} fusion(bf16[1280,2688]{1,0:T(8,128)(2,1)} %bitcast.64, bf16[40,2688]{1,0:T(8,128)(2,1)S(1)} %convert_element_type.124, f32[40]{0:T(128)S(1)} %broadcast_in_dim.5), kind=kOutput, calls=%fused_computation.5 | convolution fusion | flops 275353600 | bytes 7198880 | tf_op jit(solution)/shard_map/dot_general | solution.py:127
  79.6 0.4 copy.38
  80.2 1.1 reshape.532
  81.2 17.6 %all-to-all-start.1 = ((bf16[64,2,400]{2,1,0:T(2,128)(2,1)}), bf16[64,2,400]{2,1,0:T(2,128)(2,1)S(1)}, u32[]{:S(2)}, u32[]{:S(2)}) async-start(bf16[64,2,400]{2,1,0:T(2,128)(2,1)} %reshape.532), calls=%async_computation.1 | async-start | bytes 262144 | tf_op jit(solution)/shard_map/all_to_all | solution.py:132
  98.9 10.8 %all-to-all-done.1 = bf16[64,2,400]{2,1,0:T(2,128)(2,1)S(1)} async-done(((bf16[64,2,400]{2,1,0:T(2,128)(2,1)}), bf16[64,2,400]{2,1,0:T(2,128)(2,1)S(1)}, u32[]{:S(2)}, u32[]{:S(2)}) %all-to-all-start.1) | async-done | bytes 102432 | tf_op jit(solution)/shard_map/all_to_all | solution.py:132
  109.7 0.5 reshape.533
  110.3 0.3 copy.40
  110.5 0.8 copy.41
  111.3 2.4 %reshape.523 = bf16[5,2,2,2,2,640]{5,4,3,2,1,0:T(2,128)(2,1)S(1)} reshape(bf16[5,1,2,2,2,2,64,10]{7,6,5,4,3,2,0,1:T(8,128)(2,1)S(1)} %copy.41) | data formatting | bytes 204800 | tf_op jit(solution)/shard_map/reshape.7
  113.7 3.3 %fusion.5 = f32[1,2,2,5,2,2,768]{6,5,4,2,1,3,0:T(2,128)S(1)} fusion(bf16[5,2,2,2,2,640]{5,4,3,2,1,0:T(2,128)(2,1)S(1)} %reshape.523, bf16[5,640,768]{2,1,0:T(8,128)(2,1)} %param.4), kind=kOutput, calls=%fused_computation.6 | convolution fusion | flops 78643200 | bytes 5263360 | tf_op jit(solution)/shard_map/plfrqhj,pjk->lfrpqhk/dot_general | solution.py:137
  117.1 0.7 slice_reduce_fusion.2
  118.0 0.7 multiply_add_fusion
  (37 shorter events, 3.6 us)
Async XLA Ops:
  2.2 27.4 %copy-start = (s32[640]{0:T(1024)S(1)}, s32[640]{0:T(1024)}, u32[]{:S(2)}) copy-start(s32[640]{0:T(1024)} %param.5) | copy-start | bytes 7684
  11.4 29.7 %all-to-all-start = ((bf16[64,2,400]{2,1,0:T(2,128)(2,1)}), bf16[64,2,400]{2,1,0:T(2,128)(2,1)S(1)}, u32[]{:S(2)}, u32[]{:S(2)}) async-start(bf16[64,2,400]{2,1,0:T(2,128)(2,1)} %reshape.530), calls=%async_computation | async-start | bytes 262144 | tf_op jit(solution)/shard_map/all_to_all | solution.py:108
  42.5 8.1 %collective-permute-start = (bf16[1280,1,40]{2,0,1:T(8,128)(2,1)S(1)}, bf16[1280,1,40]{2,0,1:T(8,128)(2,1)S(1)}, u32[]{:S(2)}, u32[]{:S(2)}) collective-permute-start(bf16[1280,1,40]{2,0,1:T(8,128)(2,1)S(1)} %reshape.518), channel_id=1, source_target_pairs={{0,1},{1,2},{2,3},{3,4},{4,5},{5,6},{6,7},{7,8},{8,9},{9,10},{10,1... | collective-permute-start | bytes 307208 | tf_op jit(solution)/shard_map/ppermute | solution.py:21
  43.8 24.1 %collective-permute-start.1 = (bf16[1280,1,40]{2,0,1:T(8,128)(2,1)S(1)}, bf16[1280,1,40]{2,0,1:T(8,128)(2,1)S(1)}, u32[]{:S(2)}, u32[]{:S(2)}) collective-permute-start(bf16[1280,1,40]{2,0,1:T(8,128)(2,1)S(1)} %reshape.518), channel_id=1, source_target_pairs={{1,0},{2,1},{3,2},{4,3},{5,4},{6,5},{7,6},{8,7},{9,8},{10,9},{11,1... | collective-permute-start | bytes 307208 | tf_op jit(solution)/shard_map/ppermute | solution.py:24
  81.2 28.5 %all-to-all-start.1 = ((bf16[64,2,400]{2,1,0:T(2,128)(2,1)}), bf16[64,2,400]{2,1,0:T(2,128)(2,1)S(1)}, u32[]{:S(2)}, u32[]{:S(2)}) async-start(bf16[64,2,400]{2,1,0:T(2,128)(2,1)} %reshape.532), calls=%async_computation.1 | async-start | bytes 262144 | tf_op jit(solution)/shard_map/all_to_all | solution.py:132

commit v5 on v4

--- a/solution.py
+++ b/solution.py
@@ -24,6 +24,22 @@
         high = lax.ppermute(lax.slice_in_dim(block, 0, width, axis=dim), axis, backward)
         block = jnp.concatenate([low, block, high], axis=dim)
     return block
+
+
+def dense_halo(block, axis, dim):
+    count = lax.axis_size(axis)
+    forward = [(i, i + 1) for i in range(count - 1)]
+    backward = [(target, source) for source, target in forward]
+    lead = block.shape[0]
+
+    def send(part, pairs):
+        shape = part.shape
+        flat = part.reshape(-1, 128) if part.size % 128 == 0 else part.reshape(lead, -1)
+        return lax.ppermute(flat, axis, pairs).reshape(shape)
+
+    low = send(lax.slice_in_dim(block, block.shape[dim] - 1, None, axis=dim), forward)
+    high = send(lax.slice_in_dim(block, 0, 1, axis=dim), backward)
+    return jnp.concatenate([low, block, high], axis=dim)
 
 
 def pair_masks(leading):
@@ -109,9 +125,11 @@
     wave_table = make_table(owners, LON)
     received, wave_table = lax.optimization_barrier((received, wave_table))
     k_all = wave_count * local_k
-    fourier = jnp.transpose(received.reshape(wave_count, 2, slot_count, row_count), (1, 0, 2, 3))
-    fourier = fourier.reshape(k_all, lev_count, 2 * lat_count * 2)
-    fourier = with_halo(fourier, (("lev", 1),), 1).reshape(k_all, -1)
+    level_rows = 2 * lat_count * 2
+    fourier = dense_halo(received.reshape(wave_count, local_k, lev_count, level_rows), "lev", 2)
+    fourier = jnp.transpose(
+        fourier.reshape(wave_count, 2, slot_count, (lev_count + 2) * level_rows), (1, 0, 2, 3)
+    ).reshape(k_all, -1)
     grid_vals = lax.dot_general(
         fourier, wave_table, (((0,), (0,)), ((), ())), preferred_element_type=jnp.float32
     ).reshape(lev_count + 2, 2, lat_count, 2, LON)

time: 120 us -> 104 us (0.87)
  waiting for transfers between devices: 32.9 us -> 11.7 us
  starting transfers between devices: 38.5 us -> 42 us
  local copies, waits for them, and re-layouts: 16 us -> 17.7 us
    ppermute x2, waiting for transfers between devices: 22.1 us -> 0.85 us  [send(): return lax.ppermute(flat, axis, pairs).reshape(shape)]
    ppermute x2, starting transfers between devices: 2.78 us -> 9.37 us  [send(): return lax.ppermute(flat, axis, pairs).reshape(shape)]
    all_to_all x1, starting transfers between devices: 17.6 us -> 14.5 us  [shards(): lax.all_to_all(coeffs.reshape(wave_count, local_k, row_count), 'wave', 0,...]
    another operation x2 -> x3, local copies, waits for them, and re-layouts: 2.48 us -> 2.94 us
  transfers between devices with their start and end apart: 4 -> 4, of which waited for: 3 -> 3; matrix products, arithmetic and copies ran while one was open for 4% -> 5% of each run, Pallas kernels for 6% -> 7%
where the time goes in v5:
time: 104 us; the launch traced here: 103 us
  starting transfers between devices  42 us (40%)
  local copies, waits for them, and re-layouts  17.7 us (17%)
  matrix products  16.4 us (16%)
  waiting for transfers between devices  11.7 us (11%)
  other arithmetic  7.86 us (8%)
  Pallas kernels  7 us (7%)
    all_to_all x1, starting transfers between devices, shards(): received = lax.all_to_all(payload, 'wave', 0, 0, tiled=True)  18.2 us
    all_to_all x1, starting transfers between devices, shards(): lax.all_to_all(coeffs.reshape(wave_count, local_k, row_count), 'wave', 0,...  14.5 us
    all_to_all x1, waiting for transfers between devices, shards(): lax.all_to_all(coeffs.reshape(wave_count, local_k, row_count), 'wave', 0,...  10.8 us
    ppermute x2, starting transfers between devices, send(): return lax.ppermute(flat, axis, pairs).reshape(shape)  9.37 us
    pallas_call x1, Pallas kernels, make_table(): pl.pallas_call(table_kernel, grid=(rows // block,), in_specs=[pl.BlockSpe...  7 us
    dot_general x1, matrix products, shards(): lax.dot_general(wave_table, tendency, (((1,), (1,)), ((), ())), preferred...  5.17 us
    dot_general x1, matrix products, shards(): lax.dot_general(fourier, wave_table, (((0,), (0,)), ((), ())), preferred_...  4.08 us
    dot_general x1, matrix products, shards(): jnp.einsum('lfrphqk,pjk->jrpqlhf', masked, legendre, preferred_element_ty...  3.86 us
  transfers between devices with their start and end apart: 4, of which 3 were waited for; matrix products, arithmetic and copies ran while one was open for 5% of the time, Pallas kernels for 7%

profile of v5, /device:TPU:1, one launch (start us, length us, event | category | flops | bytes accessed | tf_op | source)
XLA Modules:
  0.0 103.0 jit_solution(4471496223022249759)
XLA Ops:
  0.0 0.9 slice.43
  1.2 0.8 bitcast_multiply_fusion.3
  2.3 3.9 %fusion.11 = bf16[640,2,5,2,1,2,2]{0,3,5,1,6,2,4:T(2,128)(2,1)S(1)} fusion(bf16[5,640,768]{2,1,0:T(8,128)(2,1)} %param.4, bf16[2,2,5,2,2,768]{5,1,0,2,4,3:T(2,128)(2,1)S(1)} %reshape.533), kind=kOutput, calls=%fused_computation.9 | convolution fusion | flops 78694400 | bytes 5140480 | tf_op jit(solution)/shard_map/lfrphqk,pjk->jrpqlhf/dot_general | solution.py:116
  6.2 3.1 %reshape.520 = bf16[64,10,2,5,2,1,2,2]{1,0,7,6,4,3,2,5:T(8,128)(2,1)S(1)} reshape(bf16[640,2,5,2,1,2,2]{0,6,5,3,2,1,4:T(2,128)(2,1)S(1)} %copy.28) | data formatting | bytes 204800 | tf_op jit(solution)/shard_map/reshape | solution.py:119
  9.3 0.7 copy.29
  10.3 1.1 %reshape.538 = bf16[64,2,400]{2,1,0:T(2,128)(2,1)} reshape(bf16[64,20,40]{2,1,0:T(8,128)(2,1)S(1)} %copy.30) | data formatting | bytes 204800
  11.4 18.2 %all-to-all-start = ((bf16[64,2,400]{2,1,0:T(2,128)(2,1)}), bf16[64,2,400]{2,1,0:T(2,128)(2,1)S(1)}, u32[]{:S(2)}, u32[]{:S(2)}) async-start(bf16[64,2,400]{2,1,0:T(2,128)(2,1)} %reshape.538), calls=%async_computation | async-start | bytes 262144 | tf_op jit(solution)/shard_map/all_to_all | solution.py:124
  29.9 1.9 %multiply_sine_fusion = (f32[640,21]{1,0:T(8,128)}, f32[640,21]{1,0:T(8,128)}) fusion(f32[640,21]{1,0:T(8,128)S(1)} %copy.31), kind=kLoop, calls=%fused_computation.21 | loop fusion | flops 13440 | bytes 161280 | tf_op jit(solution)/shard_map/sin | solution.py:88
  31.8 2.3 %fusion.19 = (f32[640,128]{1,0:T(8,128)}, f32[640,128]{1,0:T(8,128)}) fusion(s32[640]{0:T(1024)S(1)} %copy-done), kind=kLoop, calls=%fused_computation.18 | loop fusion | flops 737280 | bytes 657920 | tf_op jit(solution)/shard_map/sin | solution.py:88
  34.1 7.0 %shard_map.37 = bf16[2,640,2688]{2,1,0:T(8,128)(2,1)} custom-call(f32[640,21]{1,0:T(8,128)} %get-tuple-element.18.cos_c_ref, f32[640,21]{1,0:T(8,128)} %get-tuple-element.17.sin_c_ref, f32[640,128]{1,0:T(8,128)} %get-tuple-element.24.cos_f_ref, f32[640,128]{1,0:T(8,128)} %get-tuple-element.23.sin_f_ref), custom_call_target="tpu_custom_call" | custom-call | tf_op jit(solution)/shard_map/pallas_call | solution.py:77
  41.1 0.5 reshape.539
  41.6 0.5 reshape_reshape.4
  42.1 1.3 %collective-permute-start.1 = (bf16[400,128]{1,0:T(8,128)(2,1)S(1)}, bf16[400,128]{1,0:T(8,128)(2,1)S(1)}, u32[]{:S(2)}, u32[]{:S(2)}) collective-permute-start(bf16[400,128]{1,0:T(8,128)(2,1)S(1)} %reshape_reshape.4), channel_id=1, source_target_pairs={{1,0},{2,1},{3,2},{4,3},{5,4},{6,5},{7,6},{8,7},{9,8},{10,9},{11,1... | collective-permute-start | bytes 307208 | tf_op jit(solution)/shard_map/ppermute | solution.py:38
  43.4 8.1 %collective-permute-start = (bf16[400,128]{1,0:T(8,128)(2,1)S(1)}, bf16[400,128]{1,0:T(8,128)(2,1)S(1)}, u32[]{:S(2)}, u32[]{:S(2)}) collective-permute-start(bf16[400,128]{1,0:T(8,128)(2,1)S(1)} %reshape_reshape.4), channel_id=1, source_target_pairs={{0,1},{1,2},{2,3},{3,4},{4,5},{5,6},{6,7},{7,8},{8,9},{9,10},{10,1... | collective-permute-start | bytes 307208 | tf_op jit(solution)/shard_map/ppermute | solution.py:38
  51.8 0.4 reshape.525
  52.2 0.8 collective-permute-done
  53.0 0.4 reshape.523
  53.7 1.2 %copy.32 = bf16[64,20,3,40]{0,3,2,1:T(8,128)(2,1)S(1)} copy(bf16[64,20,3,40]{3,1,0,2:T(8,128)(2,1)S(1)} %pad_maximum_fusion) | data formatting | bytes 614400 | tf_op jit(solution)/shard_map/concatenate | solution.py:42
  54.8 0.5 copy.33
  55.5 4.1 %fusion.51 = f32[120,2688]{1,0:T(8,128)S(1)} fusion(bf16[1280,120]{1,0:T(8,128)(2,1)S(1)} %reshape.527, bf16[1280,2688]{1,0:T(8,128)(2,1)} %bitcast.63), kind=kOutput, calls=%fused_computation.83 | convolution fusion | flops 825753600 | bytes 8478720 | tf_op jit(solution)/shard_map/dot_general | solution.py:133
  60.2 0.6 fusion.23
  60.8 0.5 pad_maximum_fusion.1
  61.4 5.2 %fusion.4 = bf16[1280,40]{0,1:T(8,128)(2,1)S(1)} fusion(bf16[1280,2688]{1,0:T(8,128)(2,1)} %bitcast.64, bf16[40,2688]{1,0:T(8,128)(2,1)S(1)} %convert_element_type.124, f32[40]{0:T(128)S(1)} %broadcast_in_dim.5), kind=kOutput, calls=%fused_computation.5 | convolution fusion | flops 275353600 | bytes 7198880 | tf_op jit(solution)/shard_map/dot_general | solution.py:145
  67.5 1.1 %reshape.540 = bf16[64,2,400]{2,1,0:T(2,128)(2,1)} reshape(bf16[64,20,40]{2,1,0:T(8,128)(2,1)S(1)} %copy.36) | data formatting | bytes 204800
  68.6 14.5 %all-to-all-start.1 = ((bf16[64,2,400]{2,1,0:T(2,128)(2,1)}), bf16[64,2,400]{2,1,0:T(2,128)(2,1)S(1)}, u32[]{:S(2)}, u32[]{:S(2)}) async-start(bf16[64,2,400]{2,1,0:T(2,128)(2,1)} %reshape.540), calls=%async_computation.1 | async-start | bytes 262144 | tf_op jit(solution)/shard_map/all_to_all | solution.py:150
  83.2 10.8 %all-to-all-done.1 = bf16[64,2,400]{2,1,0:T(2,128)(2,1)S(1)} async-done(((bf16[64,2,400]{2,1,0:T(2,128)(2,1)}), bf16[64,2,400]{2,1,0:T(2,128)(2,1)S(1)}, u32[]{:S(2)}, u32[]{:S(2)}) %all-to-all-start.1) | async-done | bytes 102432 | tf_op jit(solution)/shard_map/all_to_all | solution.py:150
  94.0 0.5 reshape.541
  94.8 0.8 copy.38
  95.6 2.4 %reshape.531 = bf16[5,2,2,2,2,640]{5,4,3,2,1,0:T(2,128)(2,1)S(1)} reshape(bf16[5,1,2,2,2,2,64,10]{7,6,5,4,3,2,0,1:T(8,128)(2,1)S(1)} %copy.38) | data formatting | bytes 204800 | tf_op jit(solution)/shard_map/reshape.7
  98.0 3.3 %fusion.5 = f32[1,2,2,5,2,2,768]{6,5,4,2,1,3,0:T(2,128)S(1)} fusion(bf16[5,2,2,2,2,640]{5,4,3,2,1,0:T(2,128)(2,1)S(1)} %reshape.531, bf16[5,640,768]{2,1,0:T(8,128)(2,1)} %param.4), kind=kOutput, calls=%fused_computation.7 | convolution fusion | flops 78643200 | bytes 5263360 | tf_op jit(solution)/shard_map/plfrqhj,pjk->lfrpqhk/dot_general | solution.py:155
  101.3 0.7 slice_reduce_fusion.2
  102.3 0.7 multiply_add_fusion
  (37 shorter events, 4.1 us)
Async XLA Ops:
  2.2 27.4 %copy-start = (s32[640]{0:T(1024)S(1)}, s32[640]{0:T(1024)}, u32[]{:S(2)}) copy-start(s32[640]{0:T(1024)} %param.5) | copy-start | bytes 7684
  11.4 29.7 %all-to-all-start = ((bf16[64,2,400]{2,1,0:T(2,128)(2,1)}), bf16[64,2,400]{2,1,0:T(2,128)(2,1)S(1)}, u32[]{:S(2)}, u32[]{:S(2)}) async-start(bf16[64,2,400]{2,1,0:T(2,128)(2,1)} %reshape.538), calls=%async_computation | async-start | bytes 262144 | tf_op jit(solution)/shard_map/all_to_all | solution.py:124
  42.1 9.7 %collective-permute-start.1 = (bf16[400,128]{1,0:T(8,128)(2,1)S(1)}, bf16[400,128]{1,0:T(8,128)(2,1)S(1)}, u32[]{:S(2)}, u32[]{:S(2)}) collective-permute-start(bf16[400,128]{1,0:T(8,128)(2,1)S(1)} %reshape_reshape.4), channel_id=1, source_target_pairs={{1,0},{2,1},{3,2},{4,3},{5,4},{6,5},{7,6},{8,7},{9,8},{10,9},{11,1... | collective-permute-start | bytes 307208 | tf_op jit(solution)/shard_map/ppermute | solution.py:38
  43.4 9.6 %collective-permute-start = (bf16[400,128]{1,0:T(8,128)(2,1)S(1)}, bf16[400,128]{1,0:T(8,128)(2,1)S(1)}, u32[]{:S(2)}, u32[]{:S(2)}) collective-permute-start(bf16[400,128]{1,0:T(8,128)(2,1)S(1)} %reshape_reshape.4), channel_id=1, source_target_pairs={{0,1},{1,2},{2,3},{3,4},{4,5},{5,6},{6,7},{7,8},{8,9},{9,10},{10,1... | collective-permute-start | bytes 307208 | tf_op jit(solution)/shard_map/ppermute | solution.py:38
  68.6 25.4 %all-to-all-start.1 = ((bf16[64,2,400]{2,1,0:T(2,128)(2,1)}), bf16[64,2,400]{2,1,0:T(2,128)(2,1)S(1)}, u32[]{:S(2)}, u32[]{:S(2)}) async-start(bf16[64,2,400]{2,1,0:T(2,128)(2,1)} %reshape.540), calls=%async_computation.1 | async-start | bytes 262144 | tf_op jit(solution)/shard_map/all_to_all | solution.py:150

commit v6 on v5

--- a/solution.py
+++ b/solution.py
@@ -103,7 +103,7 @@
     mask_second = in_second.astype(jnp.bfloat16)
     signed_first = (in_first * sign_first).astype(jnp.bfloat16)
     signed_second = (in_second * sign_second).astype(jnp.bfloat16)
-    spec_rows = spectrum.reshape(lev_count * 4, pair_count, NPK)
+    spec_rows = dense_halo(spectrum, "lev", 0).reshape((lev_count + 2) * 4, pair_count, NPK)
     masked = jnp.stack(
         [
             spec_rows * mask_first,
@@ -112,23 +112,21 @@
             spec_rows * signed_second,
         ],
         axis=2,
-    ).reshape(lev_count, 2, 2, pair_count, 2, 2, NPK)
+    ).reshape(lev_count + 2, 2, 2, pair_count, 2, 2, NPK)
     waves = jnp.einsum(
         "lfrphqk,pjk->jrpqlhf", masked, legendre, preferred_element_type=jnp.float32
     ).astype(jnp.bfloat16)
-    waves = waves.reshape(wave_count, lat_count, 2, pair_count, 2, lev_count, 2, 2)
+    waves = waves.reshape(wave_count, lat_count, 2, pair_count, 2, lev_count + 2, 2, 2)
     payload = jnp.transpose(waves, (0, 2, 3, 4, 5, 6, 1, 7))
     local_k = 2 * slot_count
     row_count = lev_count * 2 * lat_count * 2
-    payload = payload.reshape(wave_count, local_k, row_count)
+    payload = payload.reshape(wave_count, local_k, -1)
     received = lax.all_to_all(payload, "wave", 0, 0, tiled=True)
     wave_table = make_table(owners, LON)
     received, wave_table = lax.optimization_barrier((received, wave_table))
     k_all = wave_count * local_k
-    level_rows = 2 * lat_count * 2
-    fourier = dense_halo(received.reshape(wave_count, local_k, lev_count, level_rows), "lev", 2)
     fourier = jnp.transpose(
-        fourier.reshape(wave_count, 2, slot_count, (lev_count + 2) * level_rows), (1, 0, 2, 3)
+        received.reshape(wave_count, 2, slot_count, -1), (1, 0, 2, 3)
     ).reshape(k_all, -1)
     grid_vals = lax.dot_general(
         fourier, wave_table, (((0,), (0,)), ((), ())), preferred_element_type=jnp.float32

time: 104 us -> 107 us (1.029)
  starting transfers between devices: 42 us -> 29.1 us
  local copies, waits for them, and re-layouts: 17.7 us -> 26.4 us
  waiting for transfers between devices: 11.7 us -> 19.5 us
    reshape x3 -> x5, local copies, waits for them, and re-layouts: 3.53 us -> 11.7 us  [the longest x1 10.1 us: shards(): waves.reshape(wave_count, lat_count, 2, pair_count, 2, lev_count + 2, 2, 2)]
    all_to_all x1, starting transfers between devices: 14.5 us -> 7.22 us  [shards(): lax.all_to_all(coeffs.reshape(wave_count, local_k, row_count), 'wave', 0,...]
    all_to_all x1, starting transfers between devices: 18.2 us -> 11.9 us  [shards(): received = lax.all_to_all(payload, 'wave', 0, 0, tiled=True)]
    ppermute x2, waiting for transfers between devices: 0.85 us -> 5.13 us  [send(): return lax.ppermute(flat, axis, pairs).reshape(shape)]
    transpose x1, local copies, waits for them, and re-layouts: 0.74 us -> 4.5 us  [shards(): payload = jnp.transpose(waves, (0, 2, 3, 4, 5, 6, 1, 7))]
    all_to_all x1, waiting for transfers between devices: 0.01 us -> 3.51 us  [shards(): received = lax.all_to_all(payload, 'wave', 0, 0, tiled=True)]
    concatenate x1 -> x0, local copies, waits for them, and re-layouts: 1.18 us -> none  [dense_halo(): return jnp.concatenate([low, block, high], axis=dim)]
    another operation x3 -> x1, local copies, waits for them, and re-layouts: 2.94 us -> 2.43 us
  transfers between devices with their start and end apart: 4 -> 4, of which waited for: 3 -> 3; matrix products, arithmetic and copies ran while one was open for 5% -> 6% of each run, Pallas kernels for 7% -> 7%
where the time goes in v6:
time: 107 us; the launch traced here: 106 us
  starting transfers between devices  29.1 us (27%)
  local copies, waits for them, and re-layouts  26.4 us (25%)
  waiting for transfers between devices  19.5 us (18%)
  matrix products  16.6 us (16%)
  other arithmetic  7.51 us (7%)
  Pallas kernels  7 us (7%)
    all_to_all x1, starting transfers between devices, shards(): received = lax.all_to_all(payload, 'wave', 0, 0, tiled=True)  11.9 us
    all_to_all x1, waiting for transfers between devices, shards(): lax.all_to_all(coeffs.reshape(wave_count, local_k, row_count), 'wave', 0,...  10.8 us
    reshape x1, local copies, waits for them, and re-layouts, shards(): waves.reshape(wave_count, lat_count, 2, pair_count, 2, lev_count + 2, 2, 2)  10.1 us
    ppermute x2, starting transfers between devices, send(): return lax.ppermute(flat, axis, pairs).reshape(shape)  10 us
    all_to_all x1, starting transfers between devices, shards(): lax.all_to_all(coeffs.reshape(wave_count, local_k, row_count), 'wave', 0,...  7.22 us
    pallas_call x1, Pallas kernels, make_table(): pl.pallas_call(table_kernel, grid=(rows // block,), in_specs=[pl.BlockSpe...  7 us
    dot_general x1, matrix products, shards(): lax.dot_general(wave_table, tendency, (((1,), (1,)), ((), ())), preferred...  5.17 us
    ppermute x2, waiting for transfers between devices, send(): return lax.ppermute(flat, axis, pairs).reshape(shape)  5.13 us
  transfers between devices with their start and end apart: 4, of which 3 were waited for; matrix products, arithmetic and copies ran while one was open for 6% of the time, Pallas kernels for 7%

profile of v6, /device:TPU:1, one launch (start us, length us, event | category | flops | bytes accessed | tf_op | source)
XLA Modules:
  0.0 106.4 jit_solution(9392569454104543136)
XLA Ops:
  0.0 0.8 copy.31
  0.8 8.7 %collective-permute-start = (bf16[120,128]{1,0:T(8,128)(2,1)S(1)}, bf16[120,128]{1,0:T(8,128)(2,1)S(1)}, u32[]{:S(2)}, u32[]{:S(2)}) collective-permute-start(bf16[120,128]{1,0:T(8,128)(2,1)S(1)} %reshape.515), channel_id=1, source_target_pairs={{0,1},{1,2},{2,3},{3,4},{4,5},{5,6},{6,7},{7,8},{8,9},{9,10},{10,1... | collective-permute-start | bytes 92168 | tf_op jit(solution)/shard_map/ppermute | solution.py:38
  9.5 1.3 %collective-permute-start.1 = (bf16[120,128]{1,0:T(8,128)(2,1)S(1)}, bf16[120,128]{1,0:T(8,128)(2,1)S(1)}, u32[]{:S(2)}, u32[]{:S(2)}) collective-permute-start(bf16[120,128]{1,0:T(8,128)(2,1)S(1)} %reshape.515), channel_id=1, source_target_pairs={{1,0},{2,1},{3,2},{4,3},{5,4},{6,5},{7,6},{8,7},{9,8},{10,9},{11,1... | collective-permute-start | bytes 92168 | tf_op jit(solution)/shard_map/ppermute | solution.py:38
  10.9 0.9 slice.43
  12.0 0.8 fusion.25
  13.0 5.1 %collective-permute-done.1 = bf16[120,128]{1,0:T(8,128)(2,1)S(1)} collective-permute-done((bf16[120,128]{1,0:T(8,128)(2,1)S(1)}, bf16[120,128]{1,0:T(8,128)(2,1)S(1)}, u32[]{:S(2)}, u32[]{:S(2)}) %collective-permute-start.1) | collective-permute-done | bytes 30752 | tf_op jit(solution)/shard_map/ppermute | solution.py:38
  18.4 0.3 reshape.531
  18.6 4.1 %fusion.8 = bf16[640,2,5,2,3,2,2]{0,4,3,5,1,6,2:T(4,128)(2,1)S(1)} fusion(bf16[5,640,768]{2,1,0:T(8,128)(2,1)} %param.4, bf16[3,2,2,5,2,2,768]{6,2,1,0,3,5,4:T(2,128)(2,1)S(1)} %reshape.531), kind=kOutput, calls=%fused_computation.7 | convolution fusion | flops 236083200 | bytes 5591040 | tf_op jit(solution)/shard_map/lfrphqk,pjk->jrpqlhf/dot_general | solution.py:116
  22.7 0.3 copy.36
  23.0 10.1 %reshape.520 = bf16[64,10,2,5,2,3,2,2]{1,0,7,6,5,4,3,2:T(8,128)(2,1)} reshape(bf16[640,2,5,2,3,2,2]{0,6,5,4,3,2,1:T(2,128)(2,1)S(1)} %copy.36) | data formatting | bytes 614400 | tf_op jit(solution)/shard_map/reshape | solution.py:119
  33.1 4.5 %copy.37 = bf16[64,2,5,2,3,2,10,2]{0,7,6,5,4,3,2,1:T(2,128)(2,1)S(1)} copy(bf16[64,2,5,2,3,2,10,2]{6,0,7,5,4,3,2,1:T(8,128)(2,1)} %bitcast.59) | data formatting | bytes 614400 | tf_op jit(solution)/shard_map/transpose | solution.py:120
  37.6 1.0 copy.38
  38.7 11.9 %all-to-all-start = ((bf16[64,20,120]{2,1,0:T(8,128)(2,1)}), bf16[64,20,120]{2,1,0:T(8,128)(2,1)S(1)}, u32[]{:S(2)}, u32[]{:S(2)}) async-start(bf16[64,20,120]{2,1,0:T(8,128)(2,1)} %copy.38), calls=%async_computation | async-start | bytes 786432 | tf_op jit(solution)/shard_map/all_to_all | solution.py:124
  51.0 2.3 %fusion.20 = (f32[640,128]{1,0:T(8,128)}, f32[640,128]{1,0:T(8,128)}) fusion(s32[640]{0:T(1024)S(1)} %copy-done), kind=kLoop, calls=%fused_computation.19 | loop fusion | flops 737280 | bytes 657920 | tf_op jit(solution)/shard_map/sin | solution.py:88
  53.3 1.9 %multiply_sine_fusion = (f32[640,21]{1,0:T(8,128)}, f32[640,21]{1,0:T(8,128)}) fusion(f32[640,21]{1,0:T(8,128)S(1)} %copy.39), kind=kLoop, calls=%fused_computation.22 | loop fusion | flops 13440 | bytes 161280 | tf_op jit(solution)/shard_map/sin | solution.py:88
  55.2 7.0 %shard_map.37 = bf16[2,640,2688]{2,1,0:T(8,128)(2,1)} custom-call(f32[640,21]{1,0:T(8,128)} %get-tuple-element.18.cos_c_ref, f32[640,21]{1,0:T(8,128)} %get-tuple-element.17.sin_c_ref, f32[640,128]{1,0:T(8,128)} %get-tuple-element.24.cos_f_ref, f32[640,128]{1,0:T(8,128)} %get-tuple-element.23.sin_f_ref), custom_call_target="tpu_custom_call" | custom-call | tf_op jit(solution)/shard_map/pallas_call | solution.py:77
  62.2 3.5 %all-to-all-done = bf16[64,20,120]{2,1,0:T(8,128)(2,1)S(1)} async-done(((bf16[64,20,120]{2,1,0:T(8,128)(2,1)}), bf16[64,20,120]{2,1,0:T(8,128)(2,1)S(1)}, u32[]{:S(2)}, u32[]{:S(2)}) %all-to-all-start) | async-done | bytes 307232 | tf_op jit(solution)/shard_map/all_to_all | solution.py:124
  66.2 4.1 %fusion.51 = f32[120,2688]{1,0:T(8,128)S(1)} fusion(bf16[1280,120]{1,0:T(8,128)(2,1)S(1)} %reshape.524, bf16[1280,2688]{1,0:T(8,128)(2,1)} %bitcast.57), kind=kOutput, calls=%fused_computation.83 | convolution fusion | flops 825753600 | bytes 8478720 | tf_op jit(solution)/shard_map/dot_general | solution.py:131
  70.9 0.6 fusion.24
  71.5 0.5 pad_maximum_fusion.1
  72.1 5.2 %fusion.4 = bf16[1280,40]{0,1:T(8,128)(2,1)S(1)} fusion(bf16[1280,2688]{1,0:T(8,128)(2,1)} %bitcast.58, bf16[40,2688]{1,0:T(8,128)(2,1)S(1)} %convert_element_type.116, f32[40]{0:T(128)S(1)} %broadcast_in_dim.5), kind=kOutput, calls=%fused_computation.5 | convolution fusion | flops 275353600 | bytes 7198880 | tf_op jit(solution)/shard_map/dot_general | solution.py:143
  77.6 0.4 copy.43
  78.2 1.1 %reshape.536 = bf16[64,2,400]{2,1,0:T(2,128)(2,1)} reshape(bf16[64,20,40]{2,1,0:T(8,128)(2,1)S(1)} %copy.44) | data formatting | bytes 204800
  79.3 7.2 %all-to-all-start.1 = ((bf16[64,2,400]{2,1,0:T(2,128)(2,1)}), bf16[64,2,400]{2,1,0:T(2,128)(2,1)S(1)}, u32[]{:S(2)}, u32[]{:S(2)}) async-start(bf16[64,2,400]{2,1,0:T(2,128)(2,1)} %reshape.536), calls=%async_computation.1 | async-start | bytes 262144 | tf_op jit(solution)/shard_map/all_to_all | solution.py:148
  86.6 10.8 %all-to-all-done.1 = bf16[64,2,400]{2,1,0:T(2,128)(2,1)S(1)} async-done(((bf16[64,2,400]{2,1,0:T(2,128)(2,1)}), bf16[64,2,400]{2,1,0:T(2,128)(2,1)S(1)}, u32[]{:S(2)}, u32[]{:S(2)}) %all-to-all-start.1) | async-done | bytes 102432 | tf_op jit(solution)/shard_map/all_to_all | solution.py:148
  97.4 0.5 reshape.537
  97.9 0.3 copy.45
  98.2 0.8 copy.46
  99.0 2.4 %reshape.528 = bf16[5,2,2,2,2,640]{5,4,3,2,1,0:T(2,128)(2,1)S(1)} reshape(bf16[5,1,2,2,2,2,64,10]{7,6,5,4,3,2,0,1:T(8,128)(2,1)S(1)} %copy.46) | data formatting | bytes 204800 | tf_op jit(solution)/shard_map/reshape.5
  101.4 3.3 %fusion.11 = f32[1,2,2,5,2,2,768]{6,5,4,2,1,3,0:T(2,128)S(1)} fusion(bf16[5,2,2,2,2,640]{5,4,3,2,1,0:T(2,128)(2,1)S(1)} %reshape.528, bf16[5,640,768]{2,1,0:T(8,128)(2,1)} %param.4), kind=kOutput, calls=%fused_computation.8 | convolution fusion | flops 78643200 | bytes 5263360 | tf_op jit(solution)/shard_map/plfrqhj,pjk->lfrpqhk/dot_general | solution.py:153
  104.7 0.7 slice_reduce_fusion.2
  105.7 0.7 multiply_add_fusion
  (36 shorter events, 3.1 us)
Async XLA Ops:
  0.8 12.1 %collective-permute-start = (bf16[120,128]{1,0:T(8,128)(2,1)S(1)}, bf16[120,128]{1,0:T(8,128)(2,1)S(1)}, u32[]{:S(2)}, u32[]{:S(2)}) collective-permute-start(bf16[120,128]{1,0:T(8,128)(2,1)S(1)} %reshape.515), channel_id=1, source_target_pairs={{0,1},{1,2},{2,3},{3,4},{4,5},{5,6},{6,7},{7,8},{8,9},{9,10},{10,1... | collective-permute-start | bytes 92168 | tf_op jit(solution)/shard_map/ppermute | solution.py:38
  9.5 8.6 %collective-permute-start.1 = (bf16[120,128]{1,0:T(8,128)(2,1)S(1)}, bf16[120,128]{1,0:T(8,128)(2,1)S(1)}, u32[]{:S(2)}, u32[]{:S(2)}) collective-permute-start(bf16[120,128]{1,0:T(8,128)(2,1)S(1)} %reshape.515), channel_id=1, source_target_pairs={{1,0},{2,1},{3,2},{4,3},{5,4},{6,5},{7,6},{8,7},{9,8},{10,9},{11,1... | collective-permute-start | bytes 92168 | tf_op jit(solution)/shard_map/ppermute | solution.py:38
  23.0 28.0 %copy-start = (s32[640]{0:T(1024)S(1)}, s32[640]{0:T(1024)}, u32[]{:S(2)}) copy-start(s32[640]{0:T(1024)} %param.5) | copy-start | bytes 7684
  38.7 27.0 %all-to-all-start = ((bf16[64,20,120]{2,1,0:T(8,128)(2,1)}), bf16[64,20,120]{2,1,0:T(8,128)(2,1)S(1)}, u32[]{:S(2)}, u32[]{:S(2)}) async-start(bf16[64,20,120]{2,1,0:T(8,128)(2,1)} %copy.38), calls=%async_computation | async-start | bytes 786432 | tf_op jit(solution)/shard_map/all_to_all | solution.py:124
  79.3 18.1 %all-to-all-start.1 = ((bf16[64,2,400]{2,1,0:T(2,128)(2,1)}), bf16[64,2,400]{2,1,0:T(2,128)(2,1)S(1)}, u32[]{:S(2)}, u32[]{:S(2)}) async-start(bf16[64,2,400]{2,1,0:T(2,128)(2,1)} %reshape.536), calls=%async_computation.1 | async-start | bytes 262144 | tf_op jit(solution)/shard_map/all_to_all | solution.py:148

commit v7 on v6

--- a/solution.py
+++ b/solution.py
@@ -103,7 +103,10 @@
     mask_second = in_second.astype(jnp.bfloat16)
     signed_first = (in_first * sign_first).astype(jnp.bfloat16)
     signed_second = (in_second * sign_second).astype(jnp.bfloat16)
-    spec_rows = dense_halo(spectrum, "lev", 0).reshape((lev_count + 2) * 4, pair_count, NPK)
+    spec_rows = dense_halo(spectrum, "lev", 0)
+    wave_table = make_table(owners, LON)
+    spec_rows, wave_table = lax.optimization_barrier((spec_rows, wave_table))
+    spec_rows = spec_rows.reshape((lev_count + 2) * 4, pair_count, NPK)
     masked = jnp.stack(
         [
             spec_rows * mask_first,
@@ -114,42 +117,38 @@
         axis=2,
     ).reshape(lev_count + 2, 2, 2, pair_count, 2, 2, NPK)
     waves = jnp.einsum(
-        "lfrphqk,pjk->jrpqlhf", masked, legendre, preferred_element_type=jnp.float32
+        "lfrphqk,pjk->rpqlhfj", masked, legendre, preferred_element_type=jnp.float32
     ).astype(jnp.bfloat16)
-    waves = waves.reshape(wave_count, lat_count, 2, pair_count, 2, lev_count + 2, 2, 2)
-    payload = jnp.transpose(waves, (0, 2, 3, 4, 5, 6, 1, 7))
     local_k = 2 * slot_count
-    row_count = lev_count * 2 * lat_count * 2
-    payload = payload.reshape(wave_count, local_k, -1)
+    row_count = lev_count * 2 * 2 * lat_count
+    payload = jnp.transpose(waves.reshape(-1, wave_count), (1, 0)).reshape(wave_count, local_k, -1)
     received = lax.all_to_all(payload, "wave", 0, 0, tiled=True)
-    wave_table = make_table(owners, LON)
-    received, wave_table = lax.optimization_barrier((received, wave_table))
     k_all = wave_count * local_k
     fourier = jnp.transpose(
         received.reshape(wave_count, 2, slot_count, -1), (1, 0, 2, 3)
     ).reshape(k_all, -1)
     grid_vals = lax.dot_general(
         fourier, wave_table, (((0,), (0,)), ((), ())), preferred_element_type=jnp.float32
-    ).reshape(lev_count + 2, 2, lat_count, 2, LON)
+    ).reshape(lev_count + 2, 2, 2, lat_count, LON)
     centre = grid_vals[1:-1]
     slopes = 0.5 * (grid_vals[2:] - grid_vals[:-2])
-    lead_t = centre[:, :, :, 0] * slopes[:, :, :, 1]
-    second_t = centre[:, :, :, 1] * slopes[:, :, :, 0] + 0.5 * centre[:, :, :, 0] * centre[:, :, :, 1]
-    tendency = jnp.stack([lead_t, second_t], axis=3).astype(jnp.bfloat16).reshape(row_count, LON)
-    north = wave_index * lat_count + jnp.arange(lat_count, dtype=jnp.int32)
+    lead_t = centre[:, :, 0] * slopes[:, :, 1]
+    second_t = centre[:, :, 1] * slopes[:, :, 0] + 0.5 * centre[:, :, 0] * centre[:, :, 1]
+    tendency = jnp.stack([lead_t, second_t], axis=2).astype(jnp.bfloat16).reshape(row_count, LON)
+    north = jnp.arange(lat_count, dtype=jnp.int32) * wave_count + wave_index
     latitude = jnp.stack([north, NLAT - 1 - north], axis=0)
     weight = jnp.sin((latitude.astype(jnp.float32) + 0.5) * (math.pi / NLAT)) / math.sqrt(NLAT)
-    weight = jnp.broadcast_to(weight[None, :, :, None], (lev_count, 2, lat_count, 2)).reshape(-1)
+    weight = jnp.broadcast_to(weight[None, :, None, :], (lev_count, 2, 2, lat_count)).reshape(-1)
     coeffs = lax.dot_general(
         wave_table, tendency, (((1,), (1,)), ((), ())), preferred_element_type=jnp.float32
     )
     coeffs = (coeffs * weight[None, :]).astype(jnp.bfloat16)
     coeffs = jnp.transpose(coeffs.reshape(2, wave_count, slot_count, row_count), (1, 0, 2, 3))
     owned = lax.all_to_all(coeffs.reshape(wave_count, local_k, row_count), "wave", 0, 0, tiled=True)
-    owned = owned.reshape(wave_count, 2, pair_count, 2, lev_count, 2, lat_count, 2)
-    owned = jnp.transpose(owned, (2, 4, 7, 1, 3, 5, 0, 6)).reshape(
-        pair_count, lev_count, 2, 2, 2, 2, NLATH
+    owned = jnp.transpose(owned.reshape(wave_count, -1), (1, 0)).reshape(
+        2, pair_count, 2, lev_count, 2, 2, NLATH
     )
+    owned = jnp.transpose(owned, (1, 3, 5, 0, 2, 4, 6))
     partial = jnp.einsum(
         "plfrqhj,pjk->lfrpqhk", owned, legendre, preferred_element_type=jnp.float32
     )

time: 107 us -> 95 us (0.89)
  the two profiles are of different devices: /device:TPU:1 before, /device:TPU:513 now
where the time goes in v7:
time: 95 us; the launch traced here: 94.1 us
  starting transfers between devices  28.7 us (30%)
  waiting for transfers between devices  25.7 us (27%)
  matrix products  16.6 us (17%)
  local copies, waits for them, and re-layouts  8.63 us (9%)
  other arithmetic  7.26 us (8%)
  Pallas kernels  7.01 us (7%)
    all_to_all x1, waiting for transfers between devices, shards(): received = lax.all_to_all(payload, 'wave', 0, 0, tiled=True)  14.9 us
    all_to_all x1, starting transfers between devices, shards(): received = lax.all_to_all(payload, 'wave', 0, 0, tiled=True)  11.9 us
    ppermute x2, starting transfers between devices, send(): return lax.ppermute(flat, axis, pairs).reshape(shape)  11.3 us
    all_to_all x1, waiting for transfers between devices, shards(): lax.all_to_all(coeffs.reshape(wave_count, local_k, row_count), 'wave', 0,...  10.8 us
    pallas_call x1, Pallas kernels, make_table(): pl.pallas_call(table_kernel, grid=(rows // block,), in_specs=[pl.BlockSpe...  7.01 us
    all_to_all x1, starting transfers between devices, shards(): lax.all_to_all(coeffs.reshape(wave_count, local_k, row_count), 'wave', 0,...  5.43 us
    dot_general x1, matrix products, shards(): lax.dot_general(wave_table, tendency, (((1,), (1,)), ((), ())), preferred...  5.16 us
    dot_general x1, matrix products, shards(): lax.dot_general(fourier, wave_table, (((0,), (0,)), ((), ())), preferred_...  4.08 us
  transfers between devices with their start and end apart: 4, of which 2 were waited for; matrix products, arithmetic and copies ran while one was open for 8% of the time, Pallas kernels for 7%

profile of v7, /device:TPU:513, one launch (start us, length us, event | category | flops | bytes accessed | tf_op | source)
XLA Modules:
  0.0 94.1 jit_solution(1993276619366396558)
XLA Ops:
  0.0 0.8 copy.38
  0.8 7.9 %collective-permute-start = (bf16[120,128]{1,0:T(8,128)(2,1)S(1)}, bf16[120,128]{1,0:T(8,128)(2,1)S(1)}, u32[]{:S(2)}, u32[]{:S(2)}) collective-permute-start(bf16[120,128]{1,0:T(8,128)(2,1)S(1)} %reshape.519), channel_id=1, source_target_pairs={{0,1},{1,2},{2,3},{3,4},{4,5},{5,6},{6,7},{7,8},{8,9},{9,10},{10,1... | collective-permute-start | bytes 92168 | tf_op jit(solution)/shard_map/ppermute | solution.py:38
  8.7 3.4 %collective-permute-start.1 = (bf16[120,128]{1,0:T(8,128)(2,1)S(1)}, bf16[120,128]{1,0:T(8,128)(2,1)S(1)}, u32[]{:S(2)}, u32[]{:S(2)}) collective-permute-start(bf16[120,128]{1,0:T(8,128)(2,1)S(1)} %reshape.519), channel_id=1, source_target_pairs={{1,0},{2,1},{3,2},{4,3},{5,4},{6,5},{7,6},{8,7},{9,8},{10,9},{11,1... | collective-permute-start | bytes 92168 | tf_op jit(solution)/shard_map/ppermute | solution.py:38
  12.2 0.9 slice.43
  13.1 3.0 %fusion.22 = (f32[640,128]{1,0:T(8,128)}, f32[640,128]{1,0:T(8,128)}) fusion(s32[640]{0:T(1024)} %param.5), kind=kLoop, calls=%fused_computation.25 | loop fusion | flops 737280 | bytes 657920 | tf_op jit(solution)/shard_map/sin | solution.py:88
  16.3 0.8 fusion.27
  17.1 0.2 copy.40
  17.2 1.9 %multiply_sine_fusion = (f32[640,21]{1,0:T(8,128)}, f32[640,21]{1,0:T(8,128)}) fusion(f32[640,21]{1,0:T(8,128)S(1)} %copy.40), kind=kLoop, calls=%fused_computation.28 | loop fusion | flops 13440 | bytes 161280 | tf_op jit(solution)/shard_map/sin | solution.py:88
  19.3 7.0 %shard_map.37 = bf16[2,640,2688]{2,1,0:T(8,128)(2,1)} custom-call(f32[640,21]{1,0:T(8,128)} %get-tuple-element.18.cos_c_ref, f32[640,21]{1,0:T(8,128)} %get-tuple-element.17.sin_c_ref, f32[640,128]{1,0:T(8,128)} %get-tuple-element.24.cos_f_ref, f32[640,128]{1,0:T(8,128)} %get-tuple-element.23.sin_f_ref), custom_call_target="tpu_custom_call" | custom-call | tf_op jit(solution)/shard_map/pallas_call | solution.py:77
  26.6 0.3 reshape.536
  26.9 4.1 %fusion.8 = bf16[2,5,2,3,2,2,640]{6,3,2,4,0,5,1:T(4,128)(2,1)S(1)} fusion(bf16[5,640,768]{2,1,0:T(8,128)(2,1)} %param.4, bf16[3,2,2,5,2,2,768]{6,2,1,0,3,5,4:T(2,128)(2,1)S(1)} %reshape.536), kind=kOutput, calls=%fused_computation.7 | convolution fusion | flops 236083200 | bytes 5591040 | tf_op jit(solution)/shard_map/lfrphqk,pjk->rpqlhfj/dot_general | solution.py:119
  30.9 0.3 copy.44
  31.2 0.4 reshape.525
  31.6 1.1 %copy.45 = bf16[64,20,120]{2,1,0:T(8,128)(2,1)} copy(bf16[64,20,120]{0,2,1:T(8,128)(2,1)S(1)} %bitcast.58) | data formatting | bytes 614400 | tf_op jit(solution)/shard_map/reshape | solution.py:124
  32.7 11.9 %all-to-all-start = ((bf16[64,20,120]{2,1,0:T(8,128)(2,1)}), bf16[64,20,120]{2,1,0:T(8,128)(2,1)S(1)}, u32[]{:S(2)}, u32[]{:S(2)}) async-start(bf16[64,20,120]{2,1,0:T(8,128)(2,1)} %copy.45), calls=%async_computation | async-start | bytes 786432 | tf_op jit(solution)/shard_map/all_to_all | solution.py:125
  44.8 14.9 %all-to-all-done = bf16[64,20,120]{2,1,0:T(8,128)(2,1)S(1)} async-done(((bf16[64,20,120]{2,1,0:T(8,128)(2,1)}), bf16[64,20,120]{2,1,0:T(8,128)(2,1)S(1)}, u32[]{:S(2)}, u32[]{:S(2)}) %all-to-all-start) | async-done | bytes 307232 | tf_op jit(solution)/shard_map/all_to_all | solution.py:125
  59.7 0.2 copy.47
  59.9 0.2 reshape.528
  60.1 4.1 %fusion.53 = f32[120,2688]{1,0:T(8,128)S(1)} fusion(bf16[1280,120]{1,0:T(8,128)(2,1)S(1)} %reshape.528, bf16[1280,2688]{1,0:T(8,128)(2,1)} %bitcast.56), kind=kOutput, calls=%fused_computation.85 | convolution fusion | flops 825753600 | bytes 8478720 | tf_op jit(solution)/shard_map/dot_general | solution.py:130
  64.7 5.2 %fusion.4 = bf16[1280,40]{0,1:T(8,128)(2,1)S(1)} fusion(bf16[1280,2688]{1,0:T(8,128)(2,1)} %bitcast.57, bf16[40,2688]{1,0:T(8,128)(2,1)S(1)} %convert_element_type.116, f32[40]{0:T(128)S(1)} %broadcast_in_dim.5), kind=kOutput, calls=%fused_computation.5 | convolution fusion | flops 275353600 | bytes 7198880 | tf_op jit(solution)/shard_map/dot_general | solution.py:142
  69.8 0.2 copy.48
  70.2 0.4 copy.49
  70.6 0.3 copy.50
  70.8 1.1 %reshape.541 = bf16[64,2,400]{2,1,0:T(2,128)(2,1)} reshape(bf16[64,20,40]{2,1,0:T(8,128)(2,1)S(1)} %copy.50) | data formatting | bytes 204800
  71.9 5.4 %all-to-all-start.1 = ((bf16[64,2,400]{2,1,0:T(2,128)(2,1)}), bf16[64,2,400]{2,1,0:T(2,128)(2,1)S(1)}, u32[]{:S(2)}, u32[]{:S(2)}) async-start(bf16[64,2,400]{2,1,0:T(2,128)(2,1)} %reshape.541), calls=%async_computation.1 | async-start | bytes 262144 | tf_op jit(solution)/shard_map/all_to_all | solution.py:147
  77.4 10.8 %all-to-all-done.1 = bf16[64,2,400]{2,1,0:T(2,128)(2,1)S(1)} async-done(((bf16[64,2,400]{2,1,0:T(2,128)(2,1)}), bf16[64,2,400]{2,1,0:T(2,128)(2,1)S(1)}, u32[]{:S(2)}, u32[]{:S(2)}) %all-to-all-start.1) | async-done | bytes 102432 | tf_op jit(solution)/shard_map/all_to_all | solution.py:147
  88.2 0.5 reshape.542
  88.8 0.3 copy.51
  89.0 0.2 reshape.532
  89.2 3.3 %fusion.11 = f32[1,2,2,5,2,2,768]{6,5,4,2,1,3,0:T(2,128)S(1)} fusion(bf16[5,640,768]{2,1,0:T(8,128)(2,1)} %param.4, bf16[2,5,2,1,2,2,640]{6,5,4,2,1,0,3:T(2,128)(2,1)S(1)} %reshape.532), kind=kOutput, calls=%fused_computation.8 | convolution fusion | flops 78643200 | bytes 5263360 | tf_op jit(solution)/shard_map/plfrqhj,pjk->lfrpqhk/dot_general | solution.py:152
  92.5 0.7 slice_reduce_fusion.2
  93.5 0.7 multiply_add_fusion
  (32 shorter events, 1.7 us)
Async XLA Ops:
  0.8 25.5 %collective-permute-start = (bf16[120,128]{1,0:T(8,128)(2,1)S(1)}, bf16[120,128]{1,0:T(8,128)(2,1)S(1)}, u32[]{:S(2)}, u32[]{:S(2)}) collective-permute-start(bf16[120,128]{1,0:T(8,128)(2,1)S(1)} %reshape.519), channel_id=1, source_target_pairs={{0,1},{1,2},{2,3},{3,4},{4,5},{5,6},{6,7},{7,8},{8,9},{9,10},{10,1... | collective-permute-start | bytes 92168 | tf_op jit(solution)/shard_map/ppermute | solution.py:38
  8.7 17.6 %collective-permute-start.1 = (bf16[120,128]{1,0:T(8,128)(2,1)S(1)}, bf16[120,128]{1,0:T(8,128)(2,1)S(1)}, u32[]{:S(2)}, u32[]{:S(2)}) collective-permute-start(bf16[120,128]{1,0:T(8,128)(2,1)S(1)} %reshape.519), channel_id=1, source_target_pairs={{1,0},{2,1},{3,2},{4,3},{5,4},{6,5},{7,6},{8,7},{9,8},{10,9},{11,1... | collective-permute-start | bytes 92168 | tf_op jit(solution)/shard_map/ppermute | solution.py:38
  32.7 27.0 %all-to-all-start = ((bf16[64,20,120]{2,1,0:T(8,128)(2,1)}), bf16[64,20,120]{2,1,0:T(8,128)(2,1)S(1)}, u32[]{:S(2)}, u32[]{:S(2)}) async-start(bf16[64,20,120]{2,1,0:T(8,128)(2,1)} %copy.45), calls=%async_computation | async-start | bytes 786432 | tf_op jit(solution)/shard_map/all_to_all | solution.py:125
  71.9 16.3 %all-to-all-start.1 = ((bf16[64,2,400]{2,1,0:T(2,128)(2,1)}), bf16[64,2,400]{2,1,0:T(2,128)(2,1)S(1)}, u32[]{:S(2)}, u32[]{:S(2)}) async-start(bf16[64,2,400]{2,1,0:T(2,128)(2,1)} %reshape.541), calls=%async_computation.1 | async-start | bytes 262144 | tf_op jit(solution)/shard_map/all_to_all | solution.py:147

commit v8 on v7

--- a/solution.py
+++ b/solution.py
@@ -64,7 +64,7 @@
         out_ref[1, :, columns] = (-(sin_c * cos_f + cos_c * sin_f)).astype(out_ref.dtype)
 
 
-def make_table(owners, lon_count):
+def table_parts(owners, lon_count):
     inner = 128 if lon_count % 128 == 0 else lon_count
     outer = lon_count // inner
     scale = 2.0 * math.pi / lon_count
@@ -72,7 +72,12 @@
     coarse = jnp.arange(outer, dtype=jnp.int32) * inner
     fine_angle = (owners[:, None] * fine[None, :] % lon_count).astype(jnp.float32) * scale
     coarse_angle = (owners[:, None] * coarse[None, :] % lon_count).astype(jnp.float32) * scale
-    rows = owners.shape[0]
+    return (jnp.cos(coarse_angle), jnp.sin(coarse_angle), jnp.cos(fine_angle), jnp.sin(fine_angle))
+
+
+def make_table(parts, lon_count):
+    rows, outer = parts[0].shape
+    inner = parts[2].shape[1]
     block = 128 if rows % 128 == 0 else rows
     table = pl.pallas_call(
         table_kernel,
@@ -85,7 +90,7 @@
         ],
         out_specs=pl.BlockSpec((2, block, lon_count), lambda i: (0, i, 0)),
         out_shape=jax.ShapeDtypeStruct((2, rows, lon_count), jnp.bfloat16),
-    )(jnp.cos(coarse_angle), jnp.sin(coarse_angle), jnp.cos(fine_angle), jnp.sin(fine_angle))
+    )(*parts)
     return table.reshape(2 * rows, lon_count)
 
 
@@ -104,8 +109,8 @@
     signed_first = (in_first * sign_first).astype(jnp.bfloat16)
     signed_second = (in_second * sign_second).astype(jnp.bfloat16)
     spec_rows = dense_halo(spectrum, "lev", 0)
-    wave_table = make_table(owners, LON)
-    spec_rows, wave_table = lax.optimization_barrier((spec_rows, wave_table))
+    parts = table_parts(owners, LON)
+    spec_rows, parts = lax.optimization_barrier((spec_rows, parts))
     spec_rows = spec_rows.reshape((lev_count + 2) * 4, pair_count, NPK)
     masked = jnp.stack(
         [
@@ -123,6 +128,8 @@
     row_count = lev_count * 2 * 2 * lat_count
     payload = jnp.transpose(waves.reshape(-1, wave_count), (1, 0)).reshape(wave_count, local_k, -1)
     received = lax.all_to_all(payload, "wave", 0, 0, tiled=True)
+    wave_table = make_table(parts, LON)
+    received, wave_table = lax.optimization_barrier((received, wave_table))
     k_all = wave_count * local_k
     fourier = jnp.transpose(
         received.reshape(wave_count, 2, slot_count, -1), (1, 0, 2, 3)

time: 95 us -> 88.1 us (0.927)
  waiting for transfers between devices: 25.7 us -> 18.7 us
    all_to_all x1, waiting for transfers between devices: 14.9 us -> 7.88 us  [shards(): received = lax.all_to_all(payload, 'wave', 0, 0, tiled=True)]
    sin x2, other arithmetic: 4.89 us -> 5.95 us  [the longest x1 2.98 us: table_parts(): jnp.sin(fine_angle)]
  transfers between devices with their start and end apart: 4 -> 4, of which waited for: 2 -> 2; matrix products, arithmetic and copies ran while one was open for 8% -> 9% of each run, Pallas kernels for 7% -> 8%
where the time goes in v8:
time: 88.1 us; the launch traced here: 87.2 us
  starting transfers between devices  28.7 us (33%)
  waiting for transfers between devices  18.7 us (21%)
  matrix products  16.6 us (19%)
  local copies, waits for them, and re-layouts  8.46 us (10%)
  other arithmetic  7.51 us (9%)
  Pallas kernels  7 us (8%)
    all_to_all x1, starting transfers between devices, shards(): received = lax.all_to_all(payload, 'wave', 0, 0, tiled=True)  11.9 us
    ppermute x2, starting transfers between devices, send(): return lax.ppermute(flat, axis, pairs).reshape(shape)  11.3 us
    all_to_all x1, waiting for transfers between devices, shards(): lax.all_to_all(coeffs.reshape(wave_count, local_k, row_count), 'wave', 0,...  10.8 us
    all_to_all x1, waiting for transfers between devices, shards(): received = lax.all_to_all(payload, 'wave', 0, 0, tiled=True)  7.88 us
    pallas_call x1, Pallas kernels, make_table(): pl.pallas_call(table_kernel, grid=(rows // block,), in_specs=[pl.BlockSpe...  7 us
    all_to_all x1, starting transfers between devices, shards(): lax.all_to_all(coeffs.reshape(wave_count, local_k, row_count), 'wave', 0,...  5.43 us
    dot_general x1, matrix products, shards(): lax.dot_general(wave_table, tendency, (((1,), (1,)), ((), ())), preferred...  5.16 us
    dot_general x1, matrix products, shards(): lax.dot_general(fourier, wave_table, (((0,), (0,)), ((), ())), preferred_...  4.08 us
  transfers between devices with their start and end apart: 4, of which 2 were waited for; matrix products, arithmetic and copies ran while one was open for 9% of the time, Pallas kernels for 8%

profile of v8, /device:TPU:513, one launch (start us, length us, event | category | flops | bytes accessed | tf_op | source)
XLA Modules:
  0.0 87.2 jit_solution(15251904240059995746)
XLA Ops:
  0.0 0.8 copy.24
  0.8 7.9 %collective-permute-start = (bf16[120,128]{1,0:T(8,128)(2,1)S(1)}, bf16[120,128]{1,0:T(8,128)(2,1)S(1)}, u32[]{:S(2)}, u32[]{:S(2)}) collective-permute-start(bf16[120,128]{1,0:T(8,128)(2,1)S(1)} %reshape.519), channel_id=1, source_target_pairs={{0,1},{1,2},{2,3},{3,4},{4,5},{5,6},{6,7},{7,8},{8,9},{9,10},{10,1... | collective-permute-start | bytes 92168 | tf_op jit(solution)/shard_map/ppermute | solution.py:38
  8.7 3.4 %collective-permute-start.1 = (bf16[120,128]{1,0:T(8,128)(2,1)S(1)}, bf16[120,128]{1,0:T(8,128)(2,1)S(1)}, u32[]{:S(2)}, u32[]{:S(2)}) collective-permute-start(bf16[120,128]{1,0:T(8,128)(2,1)S(1)} %reshape.519), channel_id=1, source_target_pairs={{1,0},{2,1},{3,2},{4,3},{5,4},{6,5},{7,6},{8,7},{9,8},{10,9},{11,1... | collective-permute-start | bytes 92168 | tf_op jit(solution)/shard_map/ppermute | solution.py:38
  12.2 0.9 %slice.43 = s32[320]{0:T(512)S(1)} slice(s32[640]{0:T(1024)} %param.5), slice={[0:640:2]} | slice | bytes 2560 | tf_op jit(solution)/shard_map/slice | solution.py:105
  13.1 3.0 %fusion.24 = (f32[640,128]{1,0:T(8,128)}, f32[640,128]{1,0:T(8,128)}) fusion(s32[640]{0:T(1024)} %param.5), kind=kLoop, calls=%fused_computation.28 | loop fusion | flops 737280 | bytes 657920 | tf_op jit(solution)/shard_map/sin | solution.py:75
  16.0 3.0 %fusion.28 = (f32[640,21]{1,0:T(8,128)}, f32[640,21]{1,0:T(8,128)}) fusion(s32[21]{0:T(128)S(1)} %iota_multiply_fusion, s32[640]{0:T(1024)} %param.5), kind=kLoop, calls=%fused_computation.33 | loop fusion | flops 120960 | bytes 110164 | tf_op jit(solution)/shard_map/sin | solution.py:75
  19.2 0.1 select_convert_fusion
  19.7 0.3 reshape.536
  19.9 4.1 %fusion.8 = bf16[2,5,2,3,2,2,640]{6,3,2,4,0,5,1:T(4,128)(2,1)S(1)} fusion(bf16[5,640,768]{2,1,0:T(8,128)(2,1)} %param.4, bf16[3,2,2,5,2,2,768]{6,2,1,0,3,5,4:T(2,128)(2,1)S(1)} %reshape.536), kind=kOutput, calls=%fused_computation.7 | convolution fusion | flops 236083200 | bytes 5591040 | tf_op jit(solution)/shard_map/lfrphqk,pjk->rpqlhfj/dot_general | solution.py:124
  24.0 0.3 copy.29
  24.3 0.4 reshape.524
  24.7 1.1 %copy.30 = bf16[64,20,120]{2,1,0:T(8,128)(2,1)} copy(bf16[64,20,120]{0,2,1:T(8,128)(2,1)S(1)} %bitcast.58) | data formatting | bytes 614400 | tf_op jit(solution)/shard_map/reshape | solution.py:129
  25.7 11.9 %all-to-all-start = ((bf16[64,20,120]{2,1,0:T(8,128)(2,1)}), bf16[64,20,120]{2,1,0:T(8,128)(2,1)S(1)}, u32[]{:S(2)}, u32[]{:S(2)}) async-start(bf16[64,20,120]{2,1,0:T(8,128)(2,1)} %copy.30), calls=%async_computation | async-start | bytes 786432 | tf_op jit(solution)/shard_map/all_to_all | solution.py:130
  37.8 7.0 %shard_map.37 = bf16[2,640,2688]{2,1,0:T(8,128)(2,1)} custom-call(f32[640,21]{1,0:T(8,128)} %get-tuple-element.13.cos_c_ref, f32[640,21]{1,0:T(8,128)} %get-tuple-element.14.sin_c_ref, f32[640,128]{1,0:T(8,128)} %get-tuple-element.15.cos_f_ref, f32[640,128]{1,0:T(8,128)} %get-tuple-element.16.sin_f_ref), custom_call_target="tpu_custom_call" | custom-call | tf_op jit(solution)/shard_map/pallas_call | solution.py:82
  44.8 7.9 %all-to-all-done = bf16[64,20,120]{2,1,0:T(8,128)(2,1)S(1)} async-done(((bf16[64,20,120]{2,1,0:T(8,128)(2,1)}), bf16[64,20,120]{2,1,0:T(8,128)(2,1)S(1)}, u32[]{:S(2)}, u32[]{:S(2)}) %all-to-all-start) | async-done | bytes 307232 | tf_op jit(solution)/shard_map/all_to_all | solution.py:130
  52.8 0.2 copy.32
  53.0 0.2 reshape.528
  53.2 4.1 %fusion.56 = f32[120,2688]{1,0:T(8,128)S(1)} fusion(bf16[1280,120]{1,0:T(8,128)(2,1)S(1)} %reshape.528, bf16[1280,2688]{1,0:T(8,128)(2,1)} %bitcast.56), kind=kOutput, calls=%fused_computation.86 | convolution fusion | flops 825753600 | bytes 8478720 | tf_op jit(solution)/shard_map/dot_general | solution.py:137
  57.7 5.2 %fusion.4 = bf16[1280,40]{0,1:T(8,128)(2,1)S(1)} fusion(bf16[1280,2688]{1,0:T(8,128)(2,1)} %bitcast.57, bf16[40,2688]{1,0:T(8,128)(2,1)S(1)} %convert_element_type.116, f32[40]{0:T(128)S(1)} %broadcast_in_dim.5), kind=kOutput, calls=%fused_computation.5 | convolution fusion | flops 275353600 | bytes 7198880 | tf_op jit(solution)/shard_map/dot_general | solution.py:149
  62.9 0.2 copy.33
  63.1 0.1 reshape.529
  63.3 0.4 copy.34
  63.6 0.3 copy.35
  63.9 1.1 %reshape.541 = bf16[64,2,400]{2,1,0:T(2,128)(2,1)} reshape(bf16[64,20,40]{2,1,0:T(8,128)(2,1)S(1)} %copy.35) | data formatting | bytes 204800
  65.0 5.4 %all-to-all-start.1 = ((bf16[64,2,400]{2,1,0:T(2,128)(2,1)}), bf16[64,2,400]{2,1,0:T(2,128)(2,1)S(1)}, u32[]{:S(2)}, u32[]{:S(2)}) async-start(bf16[64,2,400]{2,1,0:T(2,128)(2,1)} %reshape.541), calls=%async_computation.1 | async-start | bytes 262144 | tf_op jit(solution)/shard_map/all_to_all | solution.py:154
  70.5 10.8 %all-to-all-done.1 = bf16[64,2,400]{2,1,0:T(2,128)(2,1)S(1)} async-done(((bf16[64,2,400]{2,1,0:T(2,128)(2,1)}), bf16[64,2,400]{2,1,0:T(2,128)(2,1)S(1)}, u32[]{:S(2)}, u32[]{:S(2)}) %all-to-all-start.1) | async-done | bytes 102432 | tf_op jit(solution)/shard_map/all_to_all | solution.py:154
  81.3 0.5 reshape.542
  81.8 0.3 copy.36
  82.1 0.2 reshape.532
  82.2 3.3 %fusion.11 = f32[1,2,2,5,2,2,768]{6,5,4,2,1,3,0:T(2,128)S(1)} fusion(bf16[5,640,768]{2,1,0:T(8,128)(2,1)} %param.4, bf16[2,5,2,1,2,2,640]{6,5,4,2,1,0,3:T(2,128)(2,1)S(1)} %reshape.532), kind=kOutput, calls=%fused_computation.8 | convolution fusion | flops 78643200 | bytes 5263360 | tf_op jit(solution)/shard_map/plfrqhj,pjk->lfrpqhk/dot_general | solution.py:159
  85.5 0.7 slice_reduce_fusion.2
  86.5 0.7 multiply_add_fusion
  (30 shorter events, 1.5 us)
Async XLA Ops:
  0.8 18.5 %collective-permute-start = (bf16[120,128]{1,0:T(8,128)(2,1)S(1)}, bf16[120,128]{1,0:T(8,128)(2,1)S(1)}, u32[]{:S(2)}, u32[]{:S(2)}) collective-permute-start(bf16[120,128]{1,0:T(8,128)(2,1)S(1)} %reshape.519), channel_id=1, source_target_pairs={{0,1},{1,2},{2,3},{3,4},{4,5},{5,6},{6,7},{7,8},{8,9},{9,10},{10,1... | collective-permute-start | bytes 92168 | tf_op jit(solution)/shard_map/ppermute | solution.py:38
  8.7 10.7 %collective-permute-start.1 = (bf16[120,128]{1,0:T(8,128)(2,1)S(1)}, bf16[120,128]{1,0:T(8,128)(2,1)S(1)}, u32[]{:S(2)}, u32[]{:S(2)}) collective-permute-start(bf16[120,128]{1,0:T(8,128)(2,1)S(1)} %reshape.519), channel_id=1, source_target_pairs={{1,0},{2,1},{3,2},{4,3},{5,4},{6,5},{7,6},{8,7},{9,8},{10,9},{11,1... | collective-permute-start | bytes 92168 | tf_op jit(solution)/shard_map/ppermute | solution.py:38
  25.7 27.0 %all-to-all-start = ((bf16[64,20,120]{2,1,0:T(8,128)(2,1)}), bf16[64,20,120]{2,1,0:T(8,128)(2,1)S(1)}, u32[]{:S(2)}, u32[]{:S(2)}) async-start(bf16[64,20,120]{2,1,0:T(8,128)(2,1)} %copy.30), calls=%async_computation | async-start | bytes 786432 | tf_op jit(solution)/shard_map/all_to_all | solution.py:130
  65.0 16.3 %all-to-all-start.1 = ((bf16[64,2,400]{2,1,0:T(2,128)(2,1)}), bf16[64,2,400]{2,1,0:T(2,128)(2,1)S(1)}, u32[]{:S(2)}, u32[]{:S(2)}) async-start(bf16[64,2,400]{2,1,0:T(2,128)(2,1)} %reshape.541), calls=%async_computation.1 | async-start | bytes 262144 | tf_op jit(solution)/shard_map/all_to_all | solution.py:154

commit v9 on v8

--- a/solution.py
+++ b/solution.py
@@ -109,8 +109,6 @@
     signed_first = (in_first * sign_first).astype(jnp.bfloat16)
     signed_second = (in_second * sign_second).astype(jnp.bfloat16)
     spec_rows = dense_halo(spectrum, "lev", 0)
-    parts = table_parts(owners, LON)
-    spec_rows, parts = lax.optimization_barrier((spec_rows, parts))
     spec_rows = spec_rows.reshape((lev_count + 2) * 4, pair_count, NPK)
     masked = jnp.stack(
         [
@@ -128,7 +126,7 @@
     row_count = lev_count * 2 * 2 * lat_count
     payload = jnp.transpose(waves.reshape(-1, wave_count), (1, 0)).reshape(wave_count, local_k, -1)
     received = lax.all_to_all(payload, "wave", 0, 0, tiled=True)
-    wave_table = make_table(parts, LON)
+    wave_table = make_table(table_parts(owners, LON), LON)
     received, wave_table = lax.optimization_barrier((received, wave_table))
     k_all = wave_count * local_k
     fourier = jnp.transpose(

time: 88.1 us -> 88.5 us (level)
  the two profiles are of different devices: /device:TPU:513 before, /device:TPU:1 now
where the time goes in v9:
time: 88.5 us; the launch traced here: 87.7 us
  starting transfers between devices  29 us (33%)
  waiting for transfers between devices  19.6 us (22%)
  matrix products  16.6 us (19%)
  local copies, waits for them, and re-layouts  8.62 us (10%)
  Pallas kernels  7 us (8%)
  other arithmetic  6.55 us (7%)
    all_to_all x1, starting transfers between devices, shards(): received = lax.all_to_all(payload, 'wave', 0, 0, tiled=True)  11.9 us
    all_to_all x1, waiting for transfers between devices, shards(): lax.all_to_all(coeffs.reshape(wave_count, local_k, row_count), 'wave', 0,...  10.8 us
    ppermute x2, starting transfers between devices, send(): return lax.ppermute(flat, axis, pairs).reshape(shape)  10 us
    all_to_all x1, starting transfers between devices, shards(): lax.all_to_all(coeffs.reshape(wave_count, local_k, row_count), 'wave', 0,...  7.1 us
    pallas_call x1, Pallas kernels, make_table(): pl.pallas_call(table_kernel, grid=(rows // block,), in_specs=[pl.BlockSpe...  7 us
    dot_general x1, matrix products, shards(): lax.dot_general(wave_table, tendency, (((1,), (1,)), ((), ())), preferred...  5.16 us
    ppermute x2, waiting for transfers between devices, send(): return lax.ppermute(flat, axis, pairs).reshape(shape)  5.13 us
    dot_general x1, matrix products, shards(): lax.dot_general(fourier, wave_table, (((0,), (0,)), ((), ())), preferred_...  4.08 us
  transfers between devices with their start and end apart: 4, of which 3 were waited for; matrix products, arithmetic and copies ran while one was open for 8% of the time, Pallas kernels for 8%

profile of v9, /device:TPU:1, one launch (start us, length us, event | category | flops | bytes accessed | tf_op | source)
XLA Modules:
  0.0 87.7 jit_solution(4349820344816053272)
XLA Ops:
  0.0 0.8 copy.38
  0.8 8.7 %collective-permute-start = (bf16[120,128]{1,0:T(8,128)(2,1)S(1)}, bf16[120,128]{1,0:T(8,128)(2,1)S(1)}, u32[]{:S(2)}, u32[]{:S(2)}) collective-permute-start(bf16[120,128]{1,0:T(8,128)(2,1)S(1)} %reshape.519), channel_id=1, source_target_pairs={{0,1},{1,2},{2,3},{3,4},{4,5},{5,6},{6,7},{7,8},{8,9},{9,10},{10,1... | collective-permute-start | bytes 92168 | tf_op jit(solution)/shard_map/ppermute | solution.py:38
  9.5 1.3 %collective-permute-start.1 = (bf16[120,128]{1,0:T(8,128)(2,1)S(1)}, bf16[120,128]{1,0:T(8,128)(2,1)S(1)}, u32[]{:S(2)}, u32[]{:S(2)}) collective-permute-start(bf16[120,128]{1,0:T(8,128)(2,1)S(1)} %reshape.519), channel_id=1, source_target_pairs={{1,0},{2,1},{3,2},{4,3},{5,4},{6,5},{7,6},{8,7},{9,8},{10,9},{11,1... | collective-permute-start | bytes 92168 | tf_op jit(solution)/shard_map/ppermute | solution.py:38
  10.9 0.9 %slice.43 = s32[320]{0:T(512)S(1)} slice(s32[640]{0:T(1024)} %param.5), slice={[0:640:2]} | slice | bytes 2560 | tf_op jit(solution)/shard_map/slice | solution.py:105
  12.0 0.8 fusion.27
  13.0 5.1 %collective-permute-done.1 = bf16[120,128]{1,0:T(8,128)(2,1)S(1)} collective-permute-done((bf16[120,128]{1,0:T(8,128)(2,1)S(1)}, bf16[120,128]{1,0:T(8,128)(2,1)S(1)}, u32[]{:S(2)}, u32[]{:S(2)}) %collective-permute-start.1) | collective-permute-done | bytes 30752 | tf_op jit(solution)/shard_map/ppermute | solution.py:38
  18.4 0.3 reshape.536
  18.7 4.1 %fusion.8 = bf16[2,5,2,3,2,2,640]{6,3,2,4,0,5,1:T(4,128)(2,1)S(1)} fusion(bf16[5,640,768]{2,1,0:T(8,128)(2,1)} %param.4, bf16[3,2,2,5,2,2,768]{6,2,1,0,3,5,4:T(2,128)(2,1)S(1)} %reshape.536), kind=kOutput, calls=%fused_computation.7 | convolution fusion | flops 236083200 | bytes 5591040 | tf_op jit(solution)/shard_map/lfrphqk,pjk->rpqlhfj/dot_general | solution.py:122
  22.7 0.3 copy.43
  23.0 0.4 reshape.524
  23.4 1.1 %copy.44 = bf16[64,20,120]{2,1,0:T(8,128)(2,1)} copy(bf16[64,20,120]{0,2,1:T(8,128)(2,1)S(1)} %bitcast.58) | data formatting | bytes 614400 | tf_op jit(solution)/shard_map/reshape | solution.py:127
  24.4 11.9 %all-to-all-start = ((bf16[64,20,120]{2,1,0:T(8,128)(2,1)}), bf16[64,20,120]{2,1,0:T(8,128)(2,1)S(1)}, u32[]{:S(2)}, u32[]{:S(2)}) async-start(bf16[64,20,120]{2,1,0:T(8,128)(2,1)} %copy.44), calls=%async_computation | async-start | bytes 786432 | tf_op jit(solution)/shard_map/all_to_all | solution.py:128
  36.3 0.2 copy.45
  36.7 2.3 %fusion.22 = (f32[640,128]{1,0:T(8,128)}, f32[640,128]{1,0:T(8,128)}) fusion(s32[640]{0:T(1024)S(1)} %copy-done), kind=kLoop, calls=%fused_computation.25 | loop fusion | flops 737280 | bytes 657920 | tf_op jit(solution)/shard_map/sin | solution.py:75
  39.0 1.9 %multiply_sine_fusion = (f32[640,21]{1,0:T(8,128)}, f32[640,21]{1,0:T(8,128)}) fusion(f32[640,21]{1,0:T(8,128)S(1)} %copy.45), kind=kLoop, calls=%fused_computation.28 | loop fusion | flops 13440 | bytes 161280 | tf_op jit(solution)/shard_map/sin | solution.py:75
  40.8 7.0 %shard_map.37 = bf16[2,640,2688]{2,1,0:T(8,128)(2,1)} custom-call(f32[640,21]{1,0:T(8,128)} %get-tuple-element.18.cos_c_ref, f32[640,21]{1,0:T(8,128)} %get-tuple-element.17.sin_c_ref, f32[640,128]{1,0:T(8,128)} %get-tuple-element.24.cos_f_ref, f32[640,128]{1,0:T(8,128)} %get-tuple-element.23.sin_f_ref), custom_call_target="tpu_custom_call" | custom-call | tf_op jit(solution)/shard_map/pallas_call | solution.py:82
  47.8 3.6 %all-to-all-done = bf16[64,20,120]{2,1,0:T(8,128)(2,1)S(1)} async-done(((bf16[64,20,120]{2,1,0:T(8,128)(2,1)}), bf16[64,20,120]{2,1,0:T(8,128)(2,1)S(1)}, u32[]{:S(2)}, u32[]{:S(2)}) %all-to-all-start) | async-done | bytes 307232 | tf_op jit(solution)/shard_map/all_to_all | solution.py:128
  51.5 0.2 copy.47
  51.8 0.2 reshape.528
  52.0 4.1 %fusion.53 = f32[120,2688]{1,0:T(8,128)S(1)} fusion(bf16[1280,120]{1,0:T(8,128)(2,1)S(1)} %reshape.528, bf16[1280,2688]{1,0:T(8,128)(2,1)} %bitcast.56), kind=kOutput, calls=%fused_computation.85 | convolution fusion | flops 825753600 | bytes 8478720 | tf_op jit(solution)/shard_map/dot_general | solution.py:135
  56.5 5.2 %fusion.4 = bf16[1280,40]{0,1:T(8,128)(2,1)S(1)} fusion(bf16[1280,2688]{1,0:T(8,128)(2,1)} %bitcast.57, bf16[40,2688]{1,0:T(8,128)(2,1)S(1)} %convert_element_type.116, f32[40]{0:T(128)S(1)} %broadcast_in_dim.5), kind=kOutput, calls=%fused_computation.5 | convolution fusion | flops 275353600 | bytes 7198880 | tf_op jit(solution)/shard_map/dot_general | solution.py:147
  61.7 0.2 copy.48
  62.1 0.4 copy.49
  62.4 0.3 copy.50
  62.7 1.1 %reshape.541 = bf16[64,2,400]{2,1,0:T(2,128)(2,1)} reshape(bf16[64,20,40]{2,1,0:T(8,128)(2,1)S(1)} %copy.50) | data formatting | bytes 204800
  63.7 7.1 %all-to-all-start.1 = ((bf16[64,2,400]{2,1,0:T(2,128)(2,1)}), bf16[64,2,400]{2,1,0:T(2,128)(2,1)S(1)}, u32[]{:S(2)}, u32[]{:S(2)}) async-start(bf16[64,2,400]{2,1,0:T(2,128)(2,1)} %reshape.541), calls=%async_computation.1 | async-start | bytes 262144 | tf_op jit(solution)/shard_map/all_to_all | solution.py:152
  70.9 10.8 %all-to-all-done.1 = bf16[64,2,400]{2,1,0:T(2,128)(2,1)S(1)} async-done(((bf16[64,2,400]{2,1,0:T(2,128)(2,1)}), bf16[64,2,400]{2,1,0:T(2,128)(2,1)S(1)}, u32[]{:S(2)}, u32[]{:S(2)}) %all-to-all-start.1) | async-done | bytes 102432 | tf_op jit(solution)/shard_map/all_to_all | solution.py:152
  81.8 0.5 reshape.542
  82.3 0.3 copy.51
  82.7 3.3 %fusion.11 = f32[1,2,2,5,2,2,768]{6,5,4,2,1,3,0:T(2,128)S(1)} fusion(bf16[5,640,768]{2,1,0:T(8,128)(2,1)} %param.4, bf16[2,5,2,1,2,2,640]{6,5,4,2,1,0,3:T(2,128)(2,1)S(1)} %reshape.532), kind=kOutput, calls=%fused_computation.8 | convolution fusion | flops 78643200 | bytes 5263360 | tf_op jit(solution)/shard_map/plfrqhj,pjk->lfrpqhk/dot_general | solution.py:157
  86.0 0.7 slice_reduce_fusion.2
  87.0 0.7 multiply_add_fusion
  (34 shorter events, 1.9 us)
Async XLA Ops:
  0.8 12.1 %collective-permute-start = (bf16[120,128]{1,0:T(8,128)(2,1)S(1)}, bf16[120,128]{1,0:T(8,128)(2,1)S(1)}, u32[]{:S(2)}, u32[]{:S(2)}) collective-permute-start(bf16[120,128]{1,0:T(8,128)(2,1)S(1)} %reshape.519), channel_id=1, source_target_pairs={{0,1},{1,2},{2,3},{3,4},{4,5},{5,6},{6,7},{7,8},{8,9},{9,10},{10,1... | collective-permute-start | bytes 92168 | tf_op jit(solution)/shard_map/ppermute | solution.py:38
  9.5 8.6 %collective-permute-start.1 = (bf16[120,128]{1,0:T(8,128)(2,1)S(1)}, bf16[120,128]{1,0:T(8,128)(2,1)S(1)}, u32[]{:S(2)}, u32[]{:S(2)}) collective-permute-start(bf16[120,128]{1,0:T(8,128)(2,1)S(1)} %reshape.519), channel_id=1, source_target_pairs={{1,0},{2,1},{3,2},{4,3},{5,4},{6,5},{7,6},{8,7},{9,8},{10,9},{11,1... | collective-permute-start | bytes 92168 | tf_op jit(solution)/shard_map/ppermute | solution.py:38
  18.6 18.0 %copy-start = (s32[640]{0:T(1024)S(1)}, s32[640]{0:T(1024)}, u32[]{:S(2)}) copy-start(s32[640]{0:T(1024)} %param.5) | copy-start | bytes 7684
  24.4 27.0 %all-to-all-start = ((bf16[64,20,120]{2,1,0:T(8,128)(2,1)}), bf16[64,20,120]{2,1,0:T(8,128)(2,1)S(1)}, u32[]{:S(2)}, u32[]{:S(2)}) async-start(bf16[64,20,120]{2,1,0:T(8,128)(2,1)} %copy.44), calls=%async_computation | async-start | bytes 786432 | tf_op jit(solution)/shard_map/all_to_all | solution.py:128
  63.7 18.0 %all-to-all-start.1 = ((bf16[64,2,400]{2,1,0:T(2,128)(2,1)}), bf16[64,2,400]{2,1,0:T(2,128)(2,1)S(1)}, u32[]{:S(2)}, u32[]{:S(2)}) async-start(bf16[64,2,400]{2,1,0:T(2,128)(2,1)} %reshape.541), calls=%async_computation.1 | async-start | bytes 262144 | tf_op jit(solution)/shard_map/all_to_all | solution.py:152

commit v10 on v9

--- a/solution.py
+++ b/solution.py
@@ -108,7 +108,11 @@
     mask_second = in_second.astype(jnp.bfloat16)
     signed_first = (in_first * sign_first).astype(jnp.bfloat16)
     signed_second = (in_second * sign_second).astype(jnp.bfloat16)
-    spec_rows = dense_halo(spectrum, "lev", 0)
+    lev_index = lax.axis_index("lev")
+    every_level = lax.all_gather(spectrum, "lev", axis=0, tiled=True)
+    zero_level = jnp.zeros((1,) + spectrum.shape[1:], spectrum.dtype)
+    every_level = jnp.concatenate([zero_level, every_level, zero_level], axis=0)
+    spec_rows = lax.dynamic_slice_in_dim(every_level, lev_index * lev_count, lev_count + 2, axis=0)
     spec_rows = spec_rows.reshape((lev_count + 2) * 4, pair_count, NPK)
     masked = jnp.stack(
         [

time: 88.5 us -> 145 us (1.64)
  blocking collectives: 0 us -> 66.4 us
  waiting for transfers between devices: 19.6 us -> 14.2 us
  starting transfers between devices: 29 us -> 26 us
    all_gather x0 -> x1, blocking collectives: none -> 66.4 us  [shards(): every_level = lax.all_gather(spectrum, 'lev', axis=0, tiled=True)]
    ppermute x2 -> x0, starting transfers between devices: 10 us -> none  [send(): return lax.ppermute(flat, axis, pairs).reshape(shape)]
    all_to_all x1, starting transfers between devices: 11.9 us -> 18.8 us  [shards(): received = lax.all_to_all(payload, 'wave', 0, 0, tiled=True)]
    ppermute x2 -> x0, waiting for transfers between devices: 5.13 us -> none  [send(): return lax.ppermute(flat, axis, pairs).reshape(shape)]
  transfers between devices with their start and end apart: 4 -> 2, of which waited for: 3 -> 2; matrix products, arithmetic and copies ran while one was open for 8% -> 3% of each run, Pallas kernels for 8% -> 5%
where the time goes in v10:
time: 145 us; the launch traced here: 144 us
  blocking collectives  66.4 us (46%)
  starting transfers between devices  26 us (18%)
  matrix products  16.6 us (11%)
  waiting for transfers between devices  14.2 us (10%)
  local copies, waits for them, and re-layouts  7.79 us (5%)
  Pallas kernels  7.01 us (5%)
  other arithmetic  5.96 us (4%)
    all_gather x1, blocking collectives, shards(): every_level = lax.all_gather(spectrum, 'lev', axis=0, tiled=True)  66.4 us
    all_to_all x1, starting transfers between devices, shards(): received = lax.all_to_all(payload, 'wave', 0, 0, tiled=True)  18.8 us
    all_to_all x1, waiting for transfers between devices, shards(): lax.all_to_all(coeffs.reshape(wave_count, local_k, row_count), 'wave', 0,...  10.8 us
    all_to_all x1, starting transfers between devices, shards(): lax.all_to_all(coeffs.reshape(wave_count, local_k, row_count), 'wave', 0,...  7.26 us
    pallas_call x1, Pallas kernels, make_table(): pl.pallas_call(table_kernel, grid=(rows // block,), in_specs=[pl.BlockSpe...  7.01 us
    dot_general x1, matrix products, shards(): lax.dot_general(wave_table, tendency, (((1,), (1,)), ((), ())), preferred...  5.16 us
    dot_general x1, matrix products, shards(): lax.dot_general(fourier, wave_table, (((0,), (0,)), ((), ())), preferred_...  4.08 us
    dot_general x1, matrix products, shards(): jnp.einsum('lfrphqk,pjk->rpqlhfj', masked, legendre, preferred_element_ty...  4.06 us
  transfers between devices with their start and end apart: 2, of which 2 were waited for; matrix products, arithmetic and copies ran while one was open for 3% of the time, Pallas kernels for 5%

profile of v10, /device:TPU:1, one launch (start us, length us, event | category | flops | bytes accessed | tf_op | source)
XLA Modules:
  0.0 144.2 jit_solution(5361645253923137452)
XLA Ops:
  0.0 0.9 slice.43
  1.2 66.4 %all_gather.3 = bf16[16,4,5,768]{3,1,2,0:T(4,128)(2,1)S(1)} all-gather(bf16[1,4,5,768]{3,1,2,0:T(4,128)(2,1)} %param.3), channel_id=1, replica_groups=mesh['wave'=64,'lev'=16] {'lev'}, dimensions={0}, use_global_device_ids=true | all-gather | bytes 522240 | tf_op jit(solution)/shard_map/all_gather | solution.py:112
  67.6 0.1 fusion.28
  68.0 0.3 reshape.523
  68.3 4.1 %fusion.8 = bf16[2,5,2,3,2,2,640]{6,3,2,4,0,5,1:T(4,128)(2,1)S(1)} fusion(bf16[5,640,768]{2,1,0:T(8,128)(2,1)} %param.4, bf16[3,2,2,5,2,2,768]{6,2,1,0,3,5,4:T(2,128)(2,1)S(1)} %reshape.523), kind=kOutput, calls=%fused_computation.7 | convolution fusion | flops 236083200 | bytes 5591040 | tf_op jit(solution)/shard_map/lfrphqk,pjk->rpqlhfj/dot_general | solution.py:126
  72.3 0.3 copy.35
  72.6 0.4 reshape.511
  73.0 1.1 copy.36
  74.1 18.8 %all-to-all-start = ((bf16[64,20,120]{2,1,0:T(8,128)(2,1)}), bf16[64,20,120]{2,1,0:T(8,128)(2,1)S(1)}, u32[]{:S(2)}, u32[]{:S(2)}) async-start(bf16[64,20,120]{2,1,0:T(8,128)(2,1)} %copy.36), calls=%async_computation | async-start | bytes 786432 | tf_op jit(solution)/shard_map/all_to_all | solution.py:132
  92.9 0.1 fusion.29
  93.0 0.2 copy.37
  93.3 2.3 %fusion.22 = (f32[640,128]{1,0:T(8,128)}, f32[640,128]{1,0:T(8,128)}) fusion(s32[640]{0:T(1024)S(1)} %copy-done), kind=kLoop, calls=%fused_computation.28 | loop fusion | flops 737280 | bytes 657920 | tf_op jit(solution)/shard_map/sin | solution.py:75
  95.6 1.9 %multiply_sine_fusion = (f32[640,21]{1,0:T(8,128)}, f32[640,21]{1,0:T(8,128)}) fusion(f32[640,21]{1,0:T(8,128)S(1)} %copy.37), kind=kLoop, calls=%fused_computation.31 | loop fusion | flops 13440 | bytes 161280 | tf_op jit(solution)/shard_map/sin | solution.py:75
  97.5 7.0 %shard_map.37 = bf16[2,640,2688]{2,1,0:T(8,128)(2,1)} custom-call(f32[640,21]{1,0:T(8,128)} %get-tuple-element.18.cos_c_ref, f32[640,21]{1,0:T(8,128)} %get-tuple-element.17.sin_c_ref, f32[640,128]{1,0:T(8,128)} %get-tuple-element.24.cos_f_ref, f32[640,128]{1,0:T(8,128)} %get-tuple-element.23.sin_f_ref), custom_call_target="tpu_custom_call" | custom-call | tf_op jit(solution)/shard_map/pallas_call | solution.py:82
  104.5 3.4 %all-to-all-done = bf16[64,20,120]{2,1,0:T(8,128)(2,1)S(1)} async-done(((bf16[64,20,120]{2,1,0:T(8,128)(2,1)}), bf16[64,20,120]{2,1,0:T(8,128)(2,1)S(1)}, u32[]{:S(2)}, u32[]{:S(2)}) %all-to-all-start) | async-done | bytes 307232 | tf_op jit(solution)/shard_map/all_to_all | solution.py:132
  108.0 0.2 copy.39
  108.2 0.2 reshape.515
  108.4 4.1 %fusion.55 = f32[120,2688]{1,0:T(8,128)S(1)} fusion(bf16[1280,120]{1,0:T(8,128)(2,1)S(1)} %reshape.515, bf16[1280,2688]{1,0:T(8,128)(2,1)} %bitcast.57), kind=kOutput, calls=%fused_computation.89 | convolution fusion | flops 825753600 | bytes 8478720 | tf_op jit(solution)/shard_map/dot_general | solution.py:139
  112.9 5.2 %fusion.4 = bf16[1280,40]{0,1:T(8,128)(2,1)S(1)} fusion(bf16[1280,2688]{1,0:T(8,128)(2,1)} %bitcast.58, bf16[40,2688]{1,0:T(8,128)(2,1)S(1)} %convert_element_type.116, f32[40]{0:T(128)S(1)} %broadcast_in_dim.8), kind=kOutput, calls=%fused_computation.5 | convolution fusion | flops 275353600 | bytes 7198880 | tf_op jit(solution)/shard_map/dot_general | solution.py:151
  118.1 0.2 copy.40
  118.3 0.1 reshape.516
  118.5 0.4 copy.41
  118.8 0.3 copy.42
  119.1 1.1 reshape.528
  120.2 7.3 %all-to-all-start.1 = ((bf16[64,2,400]{2,1,0:T(2,128)(2,1)}), bf16[64,2,400]{2,1,0:T(2,128)(2,1)S(1)}, u32[]{:S(2)}, u32[]{:S(2)}) async-start(bf16[64,2,400]{2,1,0:T(2,128)(2,1)} %reshape.528), calls=%async_computation.1 | async-start | bytes 262144 | tf_op jit(solution)/shard_map/all_to_all | solution.py:156
  127.5 10.8 %all-to-all-done.1 = bf16[64,2,400]{2,1,0:T(2,128)(2,1)S(1)} async-done(((bf16[64,2,400]{2,1,0:T(2,128)(2,1)}), bf16[64,2,400]{2,1,0:T(2,128)(2,1)S(1)}, u32[]{:S(2)}, u32[]{:S(2)}) %all-to-all-start.1) | async-done | bytes 102432 | tf_op jit(solution)/shard_map/all_to_all | solution.py:156
  138.3 0.5 reshape.529
  138.8 0.3 copy.43
  139.1 0.2 reshape.519
  139.2 3.3 %fusion.11 = f32[1,2,2,5,2,2,768]{6,5,4,2,1,3,0:T(2,128)S(1)} fusion(bf16[5,640,768]{2,1,0:T(8,128)(2,1)} %param.4, bf16[2,5,2,1,2,2,640]{6,5,4,2,1,0,3:T(2,128)(2,1)S(1)} %reshape.519), kind=kOutput, calls=%fused_computation.8 | convolution fusion | flops 78643200 | bytes 5263360 | tf_op jit(solution)/shard_map/plfrqhj,pjk->lfrpqhk/dot_general | solution.py:161
  142.5 0.7 slice_reduce_fusion.2
  143.5 0.7 multiply_add_fusion
  (30 shorter events, 1.5 us)
Async XLA Ops:
  68.0 24.9 %copy-start = (s32[640]{0:T(1024)S(1)}, s32[640]{0:T(1024)}, u32[]{:S(2)}) copy-start(s32[640]{0:T(1024)} %param.5) | copy-start | bytes 7684
  74.1 33.8 %all-to-all-start = ((bf16[64,20,120]{2,1,0:T(8,128)(2,1)}), bf16[64,20,120]{2,1,0:T(8,128)(2,1)S(1)}, u32[]{:S(2)}, u32[]{:S(2)}) async-start(bf16[64,20,120]{2,1,0:T(8,128)(2,1)} %copy.36), calls=%async_computation | async-start | bytes 786432 | tf_op jit(solution)/shard_map/all_to_all | solution.py:132
  120.2 18.2 %all-to-all-start.1 = ((bf16[64,2,400]{2,1,0:T(2,128)(2,1)}), bf16[64,2,400]{2,1,0:T(2,128)(2,1)S(1)}, u32[]{:S(2)}, u32[]{:S(2)}) async-start(bf16[64,2,400]{2,1,0:T(2,128)(2,1)} %reshape.528), calls=%async_computation.1 | async-start | bytes 262144 | tf_op jit(solution)/shard_map/all_to_all | solution.py:156

commit v11 on v9

--- a/solution.py
+++ b/solution.py
@@ -108,20 +108,20 @@
     mask_second = in_second.astype(jnp.bfloat16)
     signed_first = (in_first * sign_first).astype(jnp.bfloat16)
     signed_second = (in_second * sign_second).astype(jnp.bfloat16)
-    spec_rows = dense_halo(spectrum, "lev", 0)
-    spec_rows = spec_rows.reshape((lev_count + 2) * 4, pair_count, NPK)
-    masked = jnp.stack(
-        [
-            spec_rows * mask_first,
-            spec_rows * mask_second,
-            spec_rows * signed_first,
-            spec_rows * signed_second,
-        ],
-        axis=2,
-    ).reshape(lev_count + 2, 2, 2, pair_count, 2, 2, NPK)
-    waves = jnp.einsum(
-        "lfrphqk,pjk->rpqlhfj", masked, legendre, preferred_element_type=jnp.float32
-    ).astype(jnp.bfloat16)
+    def waves_of(levels):
+        rows = levels.reshape(levels.shape[0] * 4, pair_count, NPK)
+        masked = jnp.stack(
+            [rows * mask_first, rows * mask_second, rows * signed_first, rows * signed_second],
+            axis=2,
+        ).reshape(levels.shape[0], 2, 2, pair_count, 2, 2, NPK)
+        return jnp.einsum(
+            "lfrphqk,pjk->rpqlhfj", masked, legendre, preferred_element_type=jnp.float32
+        ).astype(jnp.bfloat16)
+
+    own = waves_of(spectrum)
+    halo = dense_halo(spectrum, "lev", 0)
+    near = waves_of(jnp.concatenate([halo[:1], halo[-1:]], axis=0))
+    waves = jnp.concatenate([near[:, :, :, :1], own, near[:, :, :, 1:]], axis=3)
     local_k = 2 * slot_count
     row_count = lev_count * 2 * 2 * lat_count
     payload = jnp.transpose(waves.reshape(-1, wave_count), (1, 0)).reshape(wave_count, local_k, -1)

time: 88.5 us -> 89.2 us (level)
  waiting for transfers between devices: 19.6 us -> 15.4 us
  matrix products: 16.6 us -> 20.4 us
    ppermute x2, waiting for transfers between devices: 5.13 us -> 0.94 us  [send(): return lax.ppermute(flat, axis, pairs).reshape(shape)]
    dot_general x1 -> x2, matrix products: 4.06 us -> 7.87 us  [waves_of(): jnp.einsum('lfrphqk,pjk->rpqlhfj', masked, legendre, preferred_element_ty...]
  transfers between devices with their start and end apart: 4 -> 4, of which waited for: 3 -> 3; matrix products, arithmetic and copies ran while one was open for 8% -> 12% of each run, Pallas kernels for 8% -> 8%
where the time goes in v11:
time: 89.2 us; the launch traced here: 88 us
  starting transfers between devices  29 us (33%)
  matrix products  20.4 us (23%)
  waiting for transfers between devices  15.4 us (17%)
  local copies, waits for them, and re-layouts  8.64 us (10%)
  other arithmetic  7.2 us (8%)
  Pallas kernels  7 us (8%)
    all_to_all x1, starting transfers between devices, shards(): received = lax.all_to_all(payload, 'wave', 0, 0, tiled=True)  11.9 us
    all_to_all x1, waiting for transfers between devices, shards(): lax.all_to_all(coeffs.reshape(wave_count, local_k, row_count), 'wave', 0,...  10.8 us
    ppermute x2, starting transfers between devices, send(): return lax.ppermute(flat, axis, pairs).reshape(shape)  10 us
    dot_general x2, matrix products, waves_of(): jnp.einsum('lfrphqk,pjk->rpqlhfj', masked, legendre, preferred_element_ty...  7.87 us
    all_to_all x1, starting transfers between devices, shards(): lax.all_to_all(coeffs.reshape(wave_count, local_k, row_count), 'wave', 0,...  7.12 us
    pallas_call x1, Pallas kernels, make_table(): pl.pallas_call(table_kernel, grid=(rows // block,), in_specs=[pl.BlockSpe...  7 us
    dot_general x1, matrix products, shards(): lax.dot_general(wave_table, tendency, (((1,), (1,)), ((), ())), preferred...  5.16 us
    dot_general x1, matrix products, shards(): lax.dot_general(fourier, wave_table, (((0,), (0,)), ((), ())), preferred_...  4.08 us
  transfers between devices with their start and end apart: 4, of which 3 were waited for; matrix products, arithmetic and copies ran while one was open for 12% of the time, Pallas kernels for 8%

profile of v11, /device:TPU:1, one launch (start us, length us, event | category | flops | bytes accessed | tf_op | source)
XLA Modules:
  0.0 88.0 jit_solution(2295107997681818084)
XLA Ops:
  0.0 0.8 copy.36
  0.8 8.7 %collective-permute-start = (bf16[120,128]{1,0:T(8,128)(2,1)S(1)}, bf16[120,128]{1,0:T(8,128)(2,1)S(1)}, u32[]{:S(2)}, u32[]{:S(2)}) collective-permute-start(bf16[120,128]{1,0:T(8,128)(2,1)S(1)} %reshape.569), channel_id=1, source_target_pairs={{0,1},{1,2},{2,3},{3,4},{4,5},{5,6},{6,7},{7,8},{8,9},{9,10},{10,1... | collective-permute-start | bytes 92168 | tf_op jit(solution)/shard_map/ppermute | solution.py:38
  9.6 1.3 %collective-permute-start.1 = (bf16[120,128]{1,0:T(8,128)(2,1)S(1)}, bf16[120,128]{1,0:T(8,128)(2,1)S(1)}, u32[]{:S(2)}, u32[]{:S(2)}) collective-permute-start(bf16[120,128]{1,0:T(8,128)(2,1)S(1)} %reshape.569), channel_id=1, source_target_pairs={{1,0},{2,1},{3,2},{4,3},{5,4},{6,5},{7,6},{8,7},{9,8},{10,9},{11,1... | collective-permute-start | bytes 92168 | tf_op jit(solution)/shard_map/ppermute | solution.py:38
  10.9 0.9 %slice.49 = s32[320]{0:T(512)S(1)} slice(s32[640]{0:T(1024)} %param.5), slice={[0:640:2]} | slice | bytes 2560 | tf_op jit(solution)/shard_map/slice | solution.py:105
  12.1 0.8 bitcast_multiply_fusion.3
  13.1 3.9 %fusion.19 = bf16[2,5,2,1,2,2,640]{6,2,4,0,5,3,1:T(2,128)(2,1)S(1)} fusion(bf16[5,640,768]{2,1,0:T(8,128)(2,1)} %param.4, bf16[2,2,5,2,2,768]{5,1,0,2,4,3:T(2,128)(2,1)S(1)} %reshape.589), kind=kOutput, calls=%fused_computation.12 | convolution fusion | flops 78694400 | bytes 5140480 | tf_op jit(solution)/shard_map/lfrphqk,pjk->rpqlhfj/dot_general | solution.py:117
  17.2 0.9 %collective-permute-done.1 = bf16[120,128]{1,0:T(8,128)(2,1)S(1)} collective-permute-done((bf16[120,128]{1,0:T(8,128)(2,1)S(1)}, bf16[120,128]{1,0:T(8,128)(2,1)S(1)}, u32[]{:S(2)}, u32[]{:S(2)}) %collective-permute-start.1) | collective-permute-done | bytes 30752 | tf_op jit(solution)/shard_map/ppermute | solution.py:38
  18.4 4.0 %fusion.13 = bf16[2,5,2,2,2,2,640]{6,2,4,0,5,3,1:T(2,128)(2,1)S(1)} fusion(bf16[5,640,768]{2,1,0:T(8,128)(2,1)} %param.4, bf16[2,2,2,5,2,2,768]{6,2,1,0,3,5,4:T(2,128)(2,1)S(1)} %reshape.588), kind=kOutput, calls=%fused_computation.10 | convolution fusion | flops 157388800 | bytes 5365760 | tf_op jit(solution)/shard_map/lfrphqk,pjk->rpqlhfj/dot_general | solution.py:117
  22.6 0.5 pad_maximum_fusion.1
  23.0 0.2 copy.40
  23.3 0.4 reshape.576
  23.7 1.1 %copy.41 = bf16[64,20,120]{2,1,0:T(8,128)(2,1)} copy(bf16[64,20,120]{0,2,1:T(8,128)(2,1)S(1)} %bitcast.79) | data formatting | bytes 614400 | tf_op jit(solution)/shard_map/reshape | solution.py:127
  24.7 11.9 %all-to-all-start = ((bf16[64,20,120]{2,1,0:T(8,128)(2,1)}), bf16[64,20,120]{2,1,0:T(8,128)(2,1)S(1)}, u32[]{:S(2)}, u32[]{:S(2)}) async-start(bf16[64,20,120]{2,1,0:T(8,128)(2,1)} %copy.41), calls=%async_computation | async-start | bytes 786432 | tf_op jit(solution)/shard_map/all_to_all | solution.py:128
  37.0 2.3 %fusion.29 = (f32[640,128]{1,0:T(8,128)}, f32[640,128]{1,0:T(8,128)}) fusion(s32[640]{0:T(1024)S(1)} %copy-done), kind=kLoop, calls=%fused_computation.27 | loop fusion | flops 737280 | bytes 657920 | tf_op jit(solution)/shard_map/sin | solution.py:75
  39.3 1.9 %multiply_sine_fusion = (f32[640,21]{1,0:T(8,128)}, f32[640,21]{1,0:T(8,128)}) fusion(f32[640,21]{1,0:T(8,128)S(1)} %copy.42), kind=kLoop, calls=%fused_computation.30 | loop fusion | flops 13440 | bytes 161280 | tf_op jit(solution)/shard_map/sin | solution.py:75
  41.2 7.0 %shard_map.37 = bf16[2,640,2688]{2,1,0:T(8,128)(2,1)} custom-call(f32[640,21]{1,0:T(8,128)} %get-tuple-element.18.cos_c_ref, f32[640,21]{1,0:T(8,128)} %get-tuple-element.17.sin_c_ref, f32[640,128]{1,0:T(8,128)} %get-tuple-element.30.cos_f_ref, f32[640,128]{1,0:T(8,128)} %get-tuple-element.29.sin_f_ref), custom_call_target="tpu_custom_call" | custom-call | tf_op jit(solution)/shard_map/pallas_call | solution.py:82
  48.2 3.6 %all-to-all-done = bf16[64,20,120]{2,1,0:T(8,128)(2,1)S(1)} async-done(((bf16[64,20,120]{2,1,0:T(8,128)(2,1)}), bf16[64,20,120]{2,1,0:T(8,128)(2,1)S(1)}, u32[]{:S(2)}, u32[]{:S(2)}) %all-to-all-start) | async-done | bytes 307232 | tf_op jit(solution)/shard_map/all_to_all | solution.py:128
  51.8 0.2 copy.44
  52.1 0.2 reshape.580
  52.3 4.1 %fusion.63 = f32[120,2688]{1,0:T(8,128)S(1)} fusion(bf16[1280,120]{1,0:T(8,128)(2,1)S(1)} %reshape.580, bf16[1280,2688]{1,0:T(8,128)(2,1)} %bitcast.77), kind=kOutput, calls=%fused_computation.97 | convolution fusion | flops 825753600 | bytes 8478720 | tf_op jit(solution)/shard_map/dot_general | solution.py:135
  56.8 5.2 %fusion.6 = bf16[1280,40]{0,1:T(8,128)(2,1)S(1)} fusion(bf16[1280,2688]{1,0:T(8,128)(2,1)} %bitcast.78, bf16[40,2688]{1,0:T(8,128)(2,1)S(1)} %convert_element_type.132, f32[40]{0:T(128)S(1)} %broadcast_in_dim.5), kind=kOutput, calls=%fused_computation.7 | convolution fusion | flops 275353600 | bytes 7198880 | tf_op jit(solution)/shard_map/dot_general | solution.py:147
  62.0 0.2 copy.45
  62.4 0.4 copy.46
  62.7 0.3 copy.47
  63.0 1.1 %reshape.594 = bf16[64,2,400]{2,1,0:T(2,128)(2,1)} reshape(bf16[64,20,40]{2,1,0:T(8,128)(2,1)S(1)} %copy.47) | data formatting | bytes 204800
  64.0 7.1 %all-to-all-start.1 = ((bf16[64,2,400]{2,1,0:T(2,128)(2,1)}), bf16[64,2,400]{2,1,0:T(2,128)(2,1)S(1)}, u32[]{:S(2)}, u32[]{:S(2)}) async-start(bf16[64,2,400]{2,1,0:T(2,128)(2,1)} %reshape.594), calls=%async_computation.1 | async-start | bytes 262144 | tf_op jit(solution)/shard_map/all_to_all | solution.py:152
  71.3 10.8 %all-to-all-done.1 = bf16[64,2,400]{2,1,0:T(2,128)(2,1)S(1)} async-done(((bf16[64,2,400]{2,1,0:T(2,128)(2,1)}), bf16[64,2,400]{2,1,0:T(2,128)(2,1)S(1)}, u32[]{:S(2)}, u32[]{:S(2)}) %all-to-all-start.1) | async-done | bytes 102432 | tf_op jit(solution)/shard_map/all_to_all | solution.py:152
  82.1 0.5 reshape.595
  82.6 0.3 copy.48
  83.0 3.3 %fusion.10 = f32[1,2,2,5,2,2,768]{6,5,4,2,1,3,0:T(2,128)S(1)} fusion(bf16[5,640,768]{2,1,0:T(8,128)(2,1)} %param.4, bf16[2,5,2,1,2,2,640]{6,5,4,2,1,0,3:T(2,128)(2,1)S(1)} %reshape.584), kind=kOutput, calls=%fused_computation.9 | convolution fusion | flops 78643200 | bytes 5263360 | tf_op jit(solution)/shard_map/plfrqhj,pjk->lfrpqhk/dot_general | solution.py:157
  86.3 0.7 slice_reduce_fusion.2
  87.3 0.7 multiply_add_fusion
  (40 shorter events, 2.5 us)
Async XLA Ops:
  0.0 17.0 %copy-start = (s32[640]{0:T(1024)S(1)}, s32[640]{0:T(1024)}, u32[]{:S(2)}) copy-start(s32[640]{0:T(1024)} %param.5) | copy-start | bytes 7684
  0.8 16.3 %collective-permute-start = (bf16[120,128]{1,0:T(8,128)(2,1)S(1)}, bf16[120,128]{1,0:T(8,128)(2,1)S(1)}, u32[]{:S(2)}, u32[]{:S(2)}) collective-permute-start(bf16[120,128]{1,0:T(8,128)(2,1)S(1)} %reshape.569), channel_id=1, source_target_pairs={{0,1},{1,2},{2,3},{3,4},{4,5},{5,6},{6,7},{7,8},{8,9},{9,10},{10,1... | collective-permute-start | bytes 92168 | tf_op jit(solution)/shard_map/ppermute | solution.py:38
  9.6 8.6 %collective-permute-start.1 = (bf16[120,128]{1,0:T(8,128)(2,1)S(1)}, bf16[120,128]{1,0:T(8,128)(2,1)S(1)}, u32[]{:S(2)}, u32[]{:S(2)}) collective-permute-start(bf16[120,128]{1,0:T(8,128)(2,1)S(1)} %reshape.569), channel_id=1, source_target_pairs={{1,0},{2,1},{3,2},{4,3},{5,4},{6,5},{7,6},{8,7},{9,8},{10,9},{11,1... | collective-permute-start | bytes 92168 | tf_op jit(solution)/shard_map/ppermute | solution.py:38
  24.7 27.0 %all-to-all-start = ((bf16[64,20,120]{2,1,0:T(8,128)(2,1)}), bf16[64,20,120]{2,1,0:T(8,128)(2,1)S(1)}, u32[]{:S(2)}, u32[]{:S(2)}) async-start(bf16[64,20,120]{2,1,0:T(8,128)(2,1)} %copy.41), calls=%async_computation | async-start | bytes 786432 | tf_op jit(solution)/shard_map/all_to_all | solution.py:128
  64.0 18.0 %all-to-all-start.1 = ((bf16[64,2,400]{2,1,0:T(2,128)(2,1)}), bf16[64,2,400]{2,1,0:T(2,128)(2,1)S(1)}, u32[]{:S(2)}, u32[]{:S(2)}) async-start(bf16[64,2,400]{2,1,0:T(2,128)(2,1)} %reshape.594), calls=%async_computation.1 | async-start | bytes 262144 | tf_op jit(solution)/shard_map/all_to_all | solution.py:152
